TPU v7x, 256 devices: a whole 4x4x8 slice. The times are simulated.
256 devices in a mesh: segment: 2 (over core), ctx: 64 (over x, z, y_hi), tp: 2 (over y_lo).
Axes of the slice: x: 4, y: 4 (y_hi: 2, y_lo: 2; y = y_hi * 2 + y_lo), z: 8, core: 2. Of those that a mesh axis runs over, the one named last changes fastest.
Arguments:
- queries: bfloat16 [8192, 32, 128], P('ctx', 'tp'), may hold values from -14 to 14
- keys: bfloat16 [8192, 8, 128], P('ctx', 'tp'), may hold values from -10 to 10
- values: bfloat16 [8192, 8, 128], P('ctx', 'tp'), may hold values from -6 to 6
- layer_in: bfloat16 [8192, 4096], P('ctx', 'tp'), may hold values from -6 to 6
- w_bc: bfloat16 [1, 4096, 1024], P(None, 'tp'), may hold values from -0.09375 to 0.09375
- w_dt: bfloat16 [1, 4096, 64], P(None, 'tp'), may hold values from -0.09375 to 0.09375
- dt_bias: float32 [1, 64], P(None, 'tp'), may hold values from -1 to 1
- decay_rate: float32 [1, 64], P(None, 'tp'), may hold values from 1.2207031e-05 to 0.06
- skip_gain: float32 [1, 64], P(None, 'tp'), may hold values from 0.5 to 2
- out_gain: float32 [1, 64, 64], P(None, 'tp'), may hold values from 0.5 to 1.5
Outputs:
- section_out: bfloat16 [2, 8192, 4096], P('segment', 'ctx', 'tp')
All inputs are finite; a program needn't handle non-finite values.
Results may differ from a plain program's by a relative error of at most 0.002.
Values may be sent and summed in bfloat16 or wider, within the bound.
No kernel may reach another device: no remote copies, remote signals or barrier semaphores. Data moves between devices by JAX's collectives and lax.ppermute only.
A program may use at most 256 MiB of HBM per device.

v0:
```python
import functools
import math

import jax
import jax.numpy as jnp
from jax import lax
from jax.experimental import pallas as pl
from jax.experimental.pallas import tpu as pltpu
from jax.sharding import PartitionSpec as P

GROUPS = 4
STATE = 128


EPSILON = 1e-05


def shifted_up(value, axis, distance):
    size = lax.axis_size(axis)
    pairs = [(source, source + distance) for source in range(size - distance)]
    return lax.ppermute(value, axis, pairs)


def swapped(value, axis):
    return lax.ppermute(value, axis, [(0, 1), (1, 0)])


def span_terms(normed, b_rows, c_rows, step_sizes, rate_row, skip_row):
    count_rows, head_count, head_width = normed.shape
    group_count = b_rows.shape[1]
    per_group = head_count // group_count
    state_root = math.sqrt(b_rows.shape[2])
    log_decay = jnp.cumsum(-step_sizes * rate_row[None, :], axis=0)
    lower_mask = jnp.arange(count_rows)[:, None] >= jnp.arange(count_rows)[None, :]
    intersection = (
        jnp.einsum("tgn,sgn->gts", c_rows, b_rows, precision=lax.Precision.HIGHEST) / state_root
    )
    log_gaps = log_decay.T[:, :, None] - log_decay.T[:, None, :]
    decays = jnp.where(lower_mask[None], jnp.exp(jnp.where(lower_mask[None], log_gaps, 0.0)), 0.0)
    mixing = (
        decays.reshape(group_count, per_group, count_rows, count_rows)
        * intersection[:, None]
        * step_sizes.T.reshape(group_count, per_group, 1, count_rows)
    )
    grouped = normed.reshape(count_rows, group_count, per_group, head_width)
    local_part = jnp.einsum(
        "gkts,sgkp->tgkp", mixing, grouped, precision=lax.Precision.HIGHEST
    ).reshape(count_rows, head_count, head_width)
    tail_weight = jnp.exp(log_decay[-1][None, :] - log_decay) * step_sizes
    weighted = (normed * tail_weight[:, :, None]).reshape(
        count_rows, group_count, per_group, head_width
    )
    ending = jnp.einsum(
        "sgkp,sgn->gkpn", weighted, b_rows, precision=lax.Precision.HIGHEST
    ).reshape(head_count, head_width, b_rows.shape[2])
    return (
        log_decay,
        local_part + skip_row[None, :, None] * normed,
        ending,
        jnp.exp(log_decay[-1]),
    )


def span_inflow(log_decay, c_rows, state_in):
    count_rows, group_count, state_n = c_rows.shape
    head_count, head_width = (state_in.shape[0], state_in.shape[1])
    per_group = head_count // group_count
    state_root = math.sqrt(state_n)
    inflow = jnp.einsum(
        "tgn,gkpn->tgkp",
        c_rows,
        state_in.reshape(group_count, per_group, head_width, state_n),
        precision=lax.Precision.HIGHEST,
    )
    return (
        jnp.exp(log_decay)[:, :, None]
        * inflow.reshape(count_rows, head_count, head_width)
        / state_root
    )


def merge_states(earlier, later):
    return (earlier[0] * later[0], later[0][:, None, None] * earlier[1] + later[1])


def exclusive_scan(decay, state, axis, radix=4):
    place = lax.axis_index(axis)
    size = lax.axis_size(axis)
    incl = (decay, state)
    excl = (jnp.ones_like(decay), jnp.zeros_like(state))
    stride = 1
    while stride < size:
        joined = None
        for step in range(radix - 1, 0, -1):
            distance = step * stride
            if distance >= size:
                continue
            got = jax.tree.map(lambda a: shifted_up(a, axis, distance), incl)
            present = place >= distance
            got = (jnp.where(present, got[0], 1.0), jnp.where(present, got[1], 0.0))
            joined = got if joined is None else merge_states(joined, got)
        excl = merge_states(joined, excl)
        if stride * radix < size:
            incl = merge_states(joined, incl)
        stride *= radix
    return excl


def flash_kernel(first_ref, q_ref, k_ref, v_ref, o_ref, top_ref, total_ref, acc_ref, *, row_count, key_block, scale):
    j = pl.program_id(1)

    @pl.when(j == 0)
    def _():
        top_ref[...] = jnp.full(top_ref.shape, -1e30, jnp.float32)
        total_ref[...] = jnp.zeros(total_ref.shape, jnp.float32)
        acc_ref[...] = jnp.zeros(acc_ref.shape, jnp.float32)

    first = first_ref[0]

    @pl.when(j * key_block <= first + row_count - 1)
    def _():
        scores = (
            lax.dot_general(
                q_ref[...], k_ref[...], (((1,), (1,)), ((), ())), preferred_element_type=jnp.float32
            )
            * scale
        )
        rows = lax.broadcasted_iota(jnp.int32, scores.shape, 0) % row_count + first
        cols = lax.broadcasted_iota(jnp.int32, scores.shape, 1) + j * key_block
        allowed = rows >= cols
        masked = jnp.where(allowed, scores, -1e30)
        row_top = top_ref[...]
        new_top = jnp.maximum(row_top, jnp.max(masked, axis=1, keepdims=True))
        raw_weight = jnp.where(allowed, jnp.exp(masked - new_top), 0.0)
        factor = jnp.exp(row_top - new_top)
        total_ref[...] = total_ref[...] * factor + jnp.sum(raw_weight, axis=1, keepdims=True)
        acc_ref[...] = acc_ref[...] * factor + jnp.dot(
            raw_weight.astype(jnp.bfloat16), v_ref[...], preferred_element_type=jnp.float32
        )
        top_ref[...] = new_top

    @pl.when(j == pl.num_programs(1) - 1)
    def _():
        o_ref[...] = (acc_ref[...] / total_ref[...]).astype(o_ref.dtype)


def attention_half(queries, keys, values, first_row):
    row_count, q_heads, head_width = queries.shape
    kv_heads = keys.shape[1]
    group_size = q_heads // kv_heads
    score_scale = 1.0 / math.sqrt(head_width)
    grouped = (
        queries.reshape(row_count, kv_heads, group_size, head_width)
        .transpose(1, 2, 0, 3)
        .reshape(kv_heads, group_size * row_count, head_width)
    )
    both = jnp.concatenate([keys, values], axis=1).transpose(1, 0, 2)
    both_all = lax.all_gather(both, "ctx", axis=1, tiled=True)
    key_count = both_all.shape[1]
    key_block = math.gcd(key_count, 512)
    rows = group_size * row_count

    def key_index(h, j, first_ref):
        return (h, jnp.minimum(j, (first_ref[0] + row_count - 1) // key_block), 0)

    def value_index(h, j, first_ref):
        return (kv_heads + h, jnp.minimum(j, (first_ref[0] + row_count - 1) // key_block), 0)

    out = pl.pallas_call(
        functools.partial(flash_kernel, row_count=row_count, key_block=key_block, scale=score_scale),
        out_shape=jax.ShapeDtypeStruct((kv_heads, rows, head_width), jnp.bfloat16),
        grid_spec=pltpu.PrefetchScalarGridSpec(
            num_scalar_prefetch=1,
            grid=(kv_heads, key_count // key_block),
            in_specs=[
                pl.BlockSpec((None, rows, head_width), lambda h, j, f: (h, 0, 0)),
                pl.BlockSpec((None, key_block, head_width), key_index),
                pl.BlockSpec((None, key_block, head_width), value_index),
            ],
            out_specs=pl.BlockSpec((None, rows, head_width), lambda h, j, f: (h, 0, 0)),
            scratch_shapes=[
                pltpu.VMEM((rows, 1), jnp.float32),
                pltpu.VMEM((rows, 1), jnp.float32),
                pltpu.VMEM((rows, head_width), jnp.float32),
            ],
        ),
        compiler_params=pltpu.CompilerParams(dimension_semantics=("parallel", "arbitrary")),
    )(jnp.reshape(first_row, (1,)).astype(jnp.int32), grouped, both_all, both_all)
    return (
        out.reshape(kv_heads, group_size, row_count, head_width)
        .transpose(2, 0, 1, 3)
        .reshape(row_count, q_heads * head_width)
    )


def body(queries, keys, values, layer_in, w_bc, w_dt, dt_bias, decay_rate, skip_gain, out_gain):
    seg = lax.axis_index("segment")
    seg_count = lax.axis_size("segment")
    tp = lax.axis_index("tp")
    tp_count = lax.axis_size("tp")
    row_count, q_heads, head_width = queries.shape
    kv_heads = keys.shape[1]
    first_row = lax.axis_index("ctx") * row_count

    q_share = q_heads // seg_count
    kv_share = kv_heads // seg_count
    q_part = lax.dynamic_slice_in_dim(queries, seg * q_share, q_share, 1)
    k_part = lax.dynamic_slice_in_dim(keys, seg * kv_share, kv_share, 1)
    v_part = lax.dynamic_slice_in_dim(values, seg * kv_share, kv_share, 1)
    attended = attention_half(q_part, k_part, v_part, first_row)

    current = layer_in
    channel_count = current.shape[1]
    heads_dev = dt_bias.shape[1]
    state_width = channel_count // heads_dev
    groups_dev = GROUPS // tp_count
    groups_core = groups_dev // seg_count
    heads_core = heads_dev // seg_count
    half_cols = GROUPS * STATE
    wide_rows = current.astype(jnp.float32)
    part_bc = jnp.dot(current, w_bc[0], preferred_element_type=jnp.float32)
    part_dt = jnp.dot(current, w_dt[0], preferred_element_type=jnp.float32)
    part_sq = jnp.sum(wide_rows * wide_rows, axis=1)

    def columns_for(tp_index):
        group_start = (tp_index * groups_dev + seg * groups_core) * STATE
        head_start = tp_index * heads_dev + seg * heads_core
        return jnp.concatenate(
            [
                lax.dynamic_slice_in_dim(part_bc, group_start, groups_core * STATE, 1),
                lax.dynamic_slice_in_dim(part_bc, half_cols + group_start, groups_core * STATE, 1),
                lax.dynamic_slice_in_dim(part_dt, head_start, heads_core, 1),
                part_sq[:, None],
            ],
            axis=1,
        )

    mine = columns_for(tp)
    theirs = columns_for(tp_count - 1 - tp)
    total = mine + swapped(theirs, "tp")
    width_bc = groups_core * STATE
    sum_b = total[:, :width_bc]
    sum_c = total[:, width_bc : 2 * width_bc]
    sum_dt = total[:, 2 * width_bc : 2 * width_bc + heads_core]
    sum_sq = total[:, 2 * width_bc + heads_core]
    inv_rms = lax.rsqrt(sum_sq / (channel_count * tp_count) + EPSILON)
    own_rows = lax.dynamic_slice_in_dim(wide_rows, seg * heads_core * state_width, heads_core * state_width, 1)
    normed = (own_rows * inv_rms[:, None]).reshape(row_count, heads_core, state_width)
    b_rows = (sum_b * inv_rms[:, None]).reshape(row_count, groups_core, STATE)
    c_rows = (sum_c * inv_rms[:, None]).reshape(row_count, groups_core, STATE)
    bias = lax.dynamic_slice_in_dim(dt_bias[0], seg * heads_core, heads_core, 0)
    rate = lax.dynamic_slice_in_dim(decay_rate[0], seg * heads_core, heads_core, 0)
    skip = lax.dynamic_slice_in_dim(skip_gain[0], seg * heads_core, heads_core, 0)
    gain = lax.dynamic_slice_in_dim(out_gain[0], seg * heads_core, heads_core, 0)
    step_sizes = jax.nn.softplus(sum_dt * inv_rms[:, None] + bias[None, :])

    log_decay, local_part, ending, span_decay = span_terms(
        normed, b_rows, c_rows, step_sizes, rate, skip
    )
    _, state_in = exclusive_scan(span_decay, ending, "ctx")
    mixed_out = local_part + span_inflow(log_decay, c_rows, state_in)
    power = jnp.mean(mixed_out * mixed_out, axis=2, keepdims=True)
    result = own_rows.reshape(row_count, heads_core, state_width) + gain[None] * mixed_out * lax.rsqrt(
        power + EPSILON
    )
    state_part = result.reshape(row_count, heads_core * state_width).astype(jnp.bfloat16)

    keep_state = seg == 0
    outgoing = jnp.where(keep_state, attended, state_part)
    incoming = swapped(outgoing, "segment")
    first = jnp.where(keep_state, state_part, incoming)
    second = jnp.where(keep_state, incoming, attended)
    return jnp.concatenate([first, second], axis=1)[None]


def solution(mesh):
    in_specs = (
        P("ctx", "tp", None),
        P("ctx", "tp", None),
        P("ctx", "tp", None),
        P("ctx", "tp"),
        P(None, "tp", None),
        P(None, "tp", None),
        P(None, "tp"),
        P(None, "tp"),
        P(None, "tp"),
        P(None, "tp", None),
    )
    out_specs = P("segment", "ctx", "tp")
    return jax.shard_map(body, mesh=mesh, in_specs=in_specs, out_specs=out_specs, check_vma=False)
```

profile of v0, /device:TPU:231, one launch (start us, length us, event | category | flops | bytes accessed | tf_op | source)
XLA Modules:
  0.0 258.6 jit_solution(11203124559340485338)
XLA Ops:
  8.5 1.3 copy.42
  9.8 1.4 fusion.37
  11.2 4.1 %fusion = f32[128,1024]{0,1:T(8,128)S(1)} fusion(bf16[128,2048]{1,0:T(8,128)(2,1)} %param.13, bf16[1,2048,1024]{2,1,0:T(8,128)(2,1)} %param.14), kind=kOutput, calls=%fused_computation | convolution fusion | flops 536870912 | bytes 5242880 | tf_op jit(solution)/shard_map/dot_general | solution.py:221
  15.7 1.4 collective-permute-start
  18.3 2.2 collective-permute-done
  21.7 4.8 %collective-permute-start.11 = (f32[16,64,128]{2,1,0:T(8,128)S(1)}, f32[16,64,128]{2,1,0:T(8,128)S(1)}, u32[]{:S(2)}, u32[]{:S(2)}) collective-permute-start(f32[16,64,128]{2,1,0:T(8,128)S(1)} %fusion.49), channel_id=1, source_target_pairs={{0,2},{2,4},{4,6},{6,8},{8,10},{10,12},{12,14},{14,16},{16,18},{18... | collective-permute-start | bytes 1572872 | tf_op jit(solution)/shard_map/ppermute | solution.py:21
  26.5 1.3 collective-permute-start.10
  27.8 1.3 collective-permute-start.9
  30.5 1.9 collective-permute-start.3
  32.4 45.7 %collective-permute-done.1 = f32[16]{0:T(128)S(1)} collective-permute-done((f32[16]{0:T(128)S(1)}, f32[16]{0:T(128)S(1)}, u32[]{:S(2)}, u32[]{:S(2)}) %collective-permute-start.1) | collective-permute-done | bytes 96 | tf_op jit(solution)/shard_map/ppermute | solution.py:21
  79.4 3.0 %collective-permute-done.2 = f32[16]{0:T(128)S(1)} collective-permute-done((f32[16]{0:T(128)S(1)}, f32[16]{0:T(128)S(1)}, u32[]{:S(2)}, u32[]{:S(2)}) %collective-permute-start.2) | collective-permute-done | bytes 96 | tf_op jit(solution)/shard_map/ppermute | solution.py:21
  83.2 2.4 multiply_add_fusion.1
  85.7 1.4 collective-permute-start.14
  87.1 1.3 collective-permute-start.13
  88.4 1.3 collective-permute-start.12
  90.1 1.3 collective-permute-start.4
  91.4 1.3 collective-permute-start.6
  92.7 38.3 %collective-permute-done.4 = f32[16]{0:T(128)S(1)} collective-permute-done((f32[16]{0:T(128)S(1)}, f32[16]{0:T(128)S(1)}, u32[]{:S(2)}, u32[]{:S(2)}) %collective-permute-start.4) | collective-permute-done | bytes 96 | tf_op jit(solution)/shard_map/ppermute | solution.py:21
  132.3 6.9 %collective-permute-done.5 = f32[16]{0:T(128)S(1)} collective-permute-done((f32[16]{0:T(128)S(1)}, f32[16]{0:T(128)S(1)}, u32[]{:S(2)}, u32[]{:S(2)}) %collective-permute-start.5) | collective-permute-done | bytes 96 | tf_op jit(solution)/shard_map/ppermute | solution.py:21
  139.2 3.1 %multiply_add_fusion = (f32[16,64,128]{2,1,0:T(8,128)}, f32[16,64,128]{2,1,0:T(8,128)}) fusion(f32[16,64,128]{2,1,0:T(8,128)S(1)} %get-tuple-element.17, f32[16]{0:T(128)S(1)} %get-tuple-element.13, f32[16,64,128]{2,1,0:T(8,128)} %collective-permute-done.14, pred[]{:T(512)S(6)} %ge.58, f32[16,64,128]{2,1,0:T(8,128)} %collective-permute-done.13, pred[]{:T(512)S(6)} %ge.57, ...), kind=kLoop, calls=%fused_computation.39 | loop fusion | flops 1179648 | bytes 3145923 | tf_op jit(solution)/shard_map/add | solution.py:83
  143.6 1.3 collective-permute-start.16
  144.9 1.3 collective-permute-start.15
  146.2 2.2 fusion.2
  148.6 1.3 collective-permute-start.8
  149.9 1.3 collective-permute-start.7
  151.2 12.8 %collective-permute-done.8 = f32[16]{0:T(128)S(1)} collective-permute-done((f32[16]{0:T(128)S(1)}, f32[16]{0:T(128)S(1)}, u32[]{:S(2)}, u32[]{:S(2)}) %collective-permute-start.8) | collective-permute-done | bytes 96 | tf_op jit(solution)/shard_map/ppermute | solution.py:21
  164.0 20.2 %collective-permute-done.15 = f32[16,64,128]{2,1,0:T(8,128)} collective-permute-done((f32[16,64,128]{2,1,0:T(8,128)}, f32[16,64,128]{2,1,0:T(8,128)}, u32[]{:S(2)}, u32[]{:S(2)}) %collective-permute-start.15) | collective-permute-done | bytes 524320 | tf_op jit(solution)/shard_map/ppermute | solution.py:21
  184.2 3.1 %fusion.12 = (f32[128,16]{0,1:T(8,128)S(1)}, f32[16,64,128]{2,1,0:T(8,128)}) fusion(f32[16,64,128]{2,1,0:T(8,128)S(1)} %fusion.2, f32[16]{0:T(128)S(1)} %fusion.61, f32[128,16]{0,1:T(8,128)S(1)} %copy.50, f32[128,1024]{0,1:T(8,128)S(1)} %get-tuple-element.20, f32[128,273]{0,1:T(8,128)S(1)} %fusion.47, f32[128]{0:T(128)S(1)} %fusion.64, ...), kind=kOutput, calls=%fused_computation.16 | convolution fusion | flops 203700224 | bytes 4279299 | tf_op jit(solution)/shard_map/tgn,gkpn->tgkp/dot_general | solution.py:69
  187.3 13.0 %all-gather.2.cloned.1.call-done.k_ref.v_ref = bf16[4,8192,128]{2,1,0:T(8,128)(2,1)} async-done(((bf16[4,128,128]{2,1,0:T(8,128)(2,1)}), bf16[4,8192,128]{2,1,0:T(8,128)(2,1)}) %all-gather.2.cloned.1.call-update) | async-done | bytes 8388624 | tf_op jit(solution)/shard_map/all_gather | solution.py:158
  200.3 45.0 %shard_map.100 = bf16[2,512,128]{2,1,0:T(8,128)(2,1)} custom-call(s32[1]{0:T(128)} %bitcast.27.first_ref, bf16[2,512,128]{2,1,0:T(8,128)(2,1)} %bitcast.110, bf16[4,8192,128]{2,1,0:T(8,128)(2,1)} %all-gather.2.cloned.1.call-done.k_ref.v_ref, bf16[4,8192,128]{2,1,0:T(8,128)(2,1)} %all-gather.2.cloned.1.call-done.k_ref.v_ref), custom_call_target="tpu_custom_call" | custom-call | tf_op jit(solution)/shard_map/pallas_call | solution.py:169
  246.4 1.4 bitcast_select_fusion.1
  247.9 1.6 collective-permute-start.18
  (75 shorter events, 14.5 us)
Async XLA Ops:
  6.5 10.6 %copy-start = (bf16[128,16,128]{2,1,0:T(8,128)(2,1)S(1)}, bf16[128,16,128]{2,1,0:T(8,128)(2,1)}, u32[]{:S(2)}) copy-start(bf16[128,16,128]{2,1,0:T(8,128)(2,1)} %param.10) | copy-start | bytes 1572868
  6.5 193.8 %all-gather.2.cloned.1.call-start = ((), (), s32[]{:S(2)}) async-start(), calls=%async_computation | async-start | bytes 8519680 | tf_op jit(solution)/shard_map/all_gather | solution.py:158
  9.8 7.3 %copy-start.6 = (f32[1,32]{1,0:T(1,128)S(1)}, f32[1,32]{1,0:T(1,128)}, u32[]{:S(2)}) copy-start(f32[1,32]{1,0:T(1,128)} %param.18) | copy-start | bytes 388
  11.2 7.0 %copy-start.4 = (f32[1,32]{1,0:T(1,128)S(1)}, f32[1,32]{1,0:T(1,128)}, u32[]{:S(2)}) copy-start(f32[1,32]{1,0:T(1,128)} %param.16) | copy-start | bytes 388
  11.2 6.9 %copy-start.5 = (f32[1,32]{1,0:T(1,128)S(1)}, f32[1,32]{1,0:T(1,128)}, u32[]{:S(2)}) copy-start(f32[1,32]{1,0:T(1,128)} %param.17) | copy-start | bytes 388
  15.4 13.8 %copy-start.3 = (f32[1,32,64]{2,1,0:T(8,128)S(1)}, f32[1,32,64]{2,1,0:T(8,128)}, u32[]{:S(2)}) copy-start(f32[1,32,64]{2,1,0:T(8,128)} %param.19) | copy-start | bytes 24580
  15.7 4.7 %collective-permute-start = (f32[128,273]{0,1:T(8,128)S(1)}, f32[128,273]{0,1:T(8,128)S(1)}, u32[]{:S(2)}, u32[]{:S(2)}) collective-permute-start(f32[128,273]{0,1:T(8,128)S(1)} %pad_maximum_fusion), channel_id=1, source_target_pairs={{0,1},{1,0},{2,3},{3,2},{4,5},{5,4},{6,7},{7,6},{8,9},{9,8},{10,11... | collective-permute-start | bytes 419336 | tf_op jit(solution)/shard_map/ppermute | solution.py:25
  21.7 60.7 %collective-permute-start.11 = (f32[16,64,128]{2,1,0:T(8,128)S(1)}, f32[16,64,128]{2,1,0:T(8,128)S(1)}, u32[]{:S(2)}, u32[]{:S(2)}) collective-permute-start(f32[16,64,128]{2,1,0:T(8,128)S(1)} %fusion.49), channel_id=1, source_target_pairs={{0,2},{2,4},{4,6},{6,8},{8,10},{10,12},{12,14},{14,16},{16,18},{18... | collective-permute-start | bytes 1572872 | tf_op jit(solution)/shard_map/ppermute | solution.py:21
  26.5 55.9 %collective-permute-start.10 = (f32[16,64,128]{2,1,0:T(8,128)S(1)}, f32[16,64,128]{2,1,0:T(8,128)}, u32[]{:S(2)}, u32[]{:S(2)}) collective-permute-start(f32[16,64,128]{2,1,0:T(8,128)S(1)} %fusion.49), channel_id=1, source_target_pairs={{0,4},{2,6},{4,8},{6,10},{8,12},{10,14},{12,16},{14,18},{16,20},{1... | collective-permute-start | bytes 1572872 | tf_op jit(solution)/shard_map/ppermute | solution.py:21
  27.8 54.6 %collective-permute-start.9 = (f32[16,64,128]{2,1,0:T(8,128)S(1)}, f32[16,64,128]{2,1,0:T(8,128)}, u32[]{:S(2)}, u32[]{:S(2)}) collective-permute-start(f32[16,64,128]{2,1,0:T(8,128)S(1)} %fusion.49), channel_id=1, source_target_pairs={{0,6},{2,8},{4,10},{6,12},{8,14},{10,16},{12,18},{14,20},{16,22},{... | collective-permute-start | bytes 1572872 | tf_op jit(solution)/shard_map/ppermute | solution.py:21
  29.2 48.9 %collective-permute-start.1 = (f32[16]{0:T(128)S(1)}, f32[16]{0:T(128)S(1)}, u32[]{:S(2)}, u32[]{:S(2)}) collective-permute-start(f32[16]{0:T(128)S(1)} %fusion.67), channel_id=1, source_target_pairs={{0,6},{2,8},{4,10},{6,12},{8,14},{10,16},{12,18},{14,20},{16,22},{... | collective-permute-start | bytes 200 | tf_op jit(solution)/shard_map/ppermute | solution.py:21
  30.5 48.9 %collective-permute-start.3 = (f32[16]{0:T(128)S(1)}, f32[16]{0:T(128)S(1)}, u32[]{:S(2)}, u32[]{:S(2)}) collective-permute-start(f32[16]{0:T(128)S(1)} %fusion.67), channel_id=1, source_target_pairs={{0,2},{2,4},{4,6},{6,8},{8,10},{10,12},{12,14},{14,16},{16,18},{18... | collective-permute-start | bytes 200 | tf_op jit(solution)/shard_map/ppermute | solution.py:21
  78.1 4.3 %collective-permute-start.2 = (f32[16]{0:T(128)S(1)}, f32[16]{0:T(128)S(1)}, u32[]{:S(2)}, u32[]{:S(2)}) collective-permute-start(f32[16]{0:T(128)S(1)} %fusion.67), channel_id=1, source_target_pairs={{0,4},{2,6},{4,8},{6,10},{8,12},{10,14},{12,16},{14,18},{16,20},{1... | collective-permute-start | bytes 200 | tf_op jit(solution)/shard_map/ppermute | solution.py:21
  82.4 0.8 copy-start.2
  85.6 98.5 %copy-start.1 = (f32[16,64,128]{2,1,0:T(8,128)S(1)}, f32[16,64,128]{2,1,0:T(8,128)}, u32[]{:S(2)}) copy-start(f32[16,64,128]{2,1,0:T(8,128)} %get-tuple-element.18) | copy-start | bytes 1572868
  85.7 53.5 %collective-permute-start.14 = (f32[16,64,128]{2,1,0:T(8,128)S(1)}, f32[16,64,128]{2,1,0:T(8,128)}, u32[]{:S(2)}, u32[]{:S(2)}) collective-permute-start(f32[16,64,128]{2,1,0:T(8,128)S(1)} %get-tuple-element.17), channel_id=1, source_target_pairs={{0,8},{2,10},{4,12},{6,14},{8,16},{10,18},{12,20},{14,22},{16,24},... | collective-permute-start | bytes 1572872 | tf_op jit(solution)/shard_map/ppermute | solution.py:21
  87.1 52.1 %collective-permute-start.13 = (f32[16,64,128]{2,1,0:T(8,128)S(1)}, f32[16,64,128]{2,1,0:T(8,128)}, u32[]{:S(2)}, u32[]{:S(2)}) collective-permute-start(f32[16,64,128]{2,1,0:T(8,128)S(1)} %get-tuple-element.17), channel_id=1, source_target_pairs={{0,16},{2,18},{4,20},{6,22},{8,24},{10,26},{12,28},{14,30},{16,32}... | collective-permute-start | bytes 1572872 | tf_op jit(solution)/shard_map/ppermute | solution.py:21
  88.4 50.8 %collective-permute-start.12 = (f32[16,64,128]{2,1,0:T(8,128)S(1)}, f32[16,64,128]{2,1,0:T(8,128)}, u32[]{:S(2)}, u32[]{:S(2)}) collective-permute-start(f32[16,64,128]{2,1,0:T(8,128)S(1)} %get-tuple-element.17), channel_id=1, source_target_pairs={{0,24},{2,26},{4,28},{6,30},{8,32},{10,34},{12,36},{14,38},{16,40}... | collective-permute-start | bytes 1572872 | tf_op jit(solution)/shard_map/ppermute | solution.py:21
  90.1 40.9 %collective-permute-start.4 = (f32[16]{0:T(128)S(1)}, f32[16]{0:T(128)S(1)}, u32[]{:S(2)}, u32[]{:S(2)}) collective-permute-start(f32[16]{0:T(128)S(1)} %get-tuple-element.13), channel_id=1, source_target_pairs={{0,24},{2,26},{4,28},{6,30},{8,32},{10,34},{12,36},{14,38},{16,40}... | collective-permute-start | bytes 200 | tf_op jit(solution)/shard_map/ppermute | solution.py:21
  91.4 40.9 %collective-permute-start.6 = (f32[16]{0:T(128)S(1)}, f32[16]{0:T(128)S(1)}, u32[]{:S(2)}, u32[]{:S(2)}) collective-permute-start(f32[16]{0:T(128)S(1)} %get-tuple-element.13), channel_id=1, source_target_pairs={{0,8},{2,10},{4,12},{6,14},{8,16},{10,18},{12,20},{14,22},{16,24},... | collective-permute-start | bytes 200 | tf_op jit(solution)/shard_map/ppermute | solution.py:21
  131.0 8.2 %collective-permute-start.5 = (f32[16]{0:T(128)S(1)}, f32[16]{0:T(128)S(1)}, u32[]{:S(2)}, u32[]{:S(2)}) collective-permute-start(f32[16]{0:T(128)S(1)} %get-tuple-element.13), channel_id=1, source_target_pairs={{0,16},{2,18},{4,20},{6,22},{8,24},{10,26},{12,28},{14,30},{16,32}... | collective-permute-start | bytes 200 | tf_op jit(solution)/shard_map/ppermute | solution.py:21
  142.4 21.6 %collective-permute-start.17 = (f32[16,64,128]{2,1,0:T(8,128)}, f32[16,64,128]{2,1,0:T(8,128)}, u32[]{:S(2)}, u32[]{:S(2)}) collective-permute-start(f32[16,64,128]{2,1,0:T(8,128)} %get-tuple-element.11), channel_id=1, source_target_pairs={{0,32},{2,34},{4,36},{6,38},{8,40},{10,42},{12,44},{14,46},{16,48}... | collective-permute-start | bytes 1572872 | tf_op jit(solution)/shard_map/ppermute | solution.py:21
  143.6 20.3 %collective-permute-start.16 = (f32[16,64,128]{2,1,0:T(8,128)}, f32[16,64,128]{2,1,0:T(8,128)}, u32[]{:S(2)}, u32[]{:S(2)}) collective-permute-start(f32[16,64,128]{2,1,0:T(8,128)} %get-tuple-element.11), channel_id=1, source_target_pairs={{0,64},{2,66},{4,68},{6,70},{8,72},{10,74},{12,76},{14,78},{16,80}... | collective-permute-start | bytes 1572872 | tf_op jit(solution)/shard_map/ppermute | solution.py:21
  144.9 39.2 %collective-permute-start.15 = (f32[16,64,128]{2,1,0:T(8,128)}, f32[16,64,128]{2,1,0:T(8,128)}, u32[]{:S(2)}, u32[]{:S(2)}) collective-permute-start(f32[16,64,128]{2,1,0:T(8,128)} %get-tuple-element.11), channel_id=1, source_target_pairs={{0,96},{2,98},{4,100},{6,102},{8,104},{10,106},{12,108},{14,110},{... | collective-permute-start | bytes 1572872 | tf_op jit(solution)/shard_map/ppermute | solution.py:21
  148.6 15.4 %collective-permute-start.8 = (f32[16]{0:T(128)S(1)}, f32[16]{0:T(128)S(1)}, u32[]{:S(2)}, u32[]{:S(2)}) collective-permute-start(f32[16]{0:T(128)S(1)} %mul.322), channel_id=1, source_target_pairs={{0,64},{2,66},{4,68},{6,70},{8,72},{10,74},{12,76},{14,78},{16,80}... | collective-permute-start | bytes 200 | tf_op jit(solution)/shard_map/ppermute | solution.py:21
  149.9 14.1 %collective-permute-start.7 = (f32[16]{0:T(128)S(1)}, f32[16]{0:T(128)S(1)}, u32[]{:S(2)}, u32[]{:S(2)}) collective-permute-start(f32[16]{0:T(128)S(1)} %mul.322), channel_id=1, source_target_pairs={{0,32},{2,34},{4,36},{6,38},{8,40},{10,42},{12,44},{14,46},{16,48}... | collective-permute-start | bytes 200 | tf_op jit(solution)/shard_map/ppermute | solution.py:21
  247.9 2.7 %collective-permute-start.18 = (bf16[128,1024]{0,1:T(8,128)(2,1)S(1)}, bf16[128,1024]{0,1:T(8,128)(2,1)S(1)}, u32[]{:S(2)}, u32[]{:S(2)}) collective-permute-start(bf16[128,1024]{0,1:T(8,128)(2,1)S(1)} %get-tuple-element.5), channel_id=1, source_target_pairs={{0,128},{128,0},{1,129},{129,1},{2,130},{130,2},{3,131},{131,3},{4... | collective-permute-start | bytes 786440 | tf_op jit(solution)/shard_map/ppermute | solution.py:25
Sparse Core Ops, SparseCore 0:
  10.9 189.4 all-gather.1
where the time goes:
time: 259 us
  waiting for transfers between devices  143 us (55%)
  Pallas kernels  45 us (17%)
  starting transfers between devices  29.2 us (11%)
  between operations  13.9 us (5%)
  matrix products  11.7 us (5%)
  other arithmetic  8.66 us (3%)
  local copies, waits for them, and re-layouts  6.87 us (3%)
    ppermute x17, waiting for transfers between devices, shifted_up(): return lax.ppermute(value, axis, pairs)  127 us
    pallas_call x1, Pallas kernels, attention_half(): pl.pallas_call(functools.partial(flash_kernel, row_count=row_count, key_b...  45 us
    ppermute x17, starting transfers between devices, shifted_up(): return lax.ppermute(value, axis, pairs)  26.2 us
    all_gather x1, waiting for transfers between devices, attention_half(): both_all = lax.all_gather(both, 'ctx', axis=1, tiled=True)  13 us
    add x2, other arithmetic, merge_states(): later[0][:, None, None] * earlier[1] + later[1]  5.57 us
  transfers between devices with their start and end apart: 20, of which 9 were waited for; matrix products, arithmetic and copies ran while one was open for 8% of the time, Pallas kernels for 0%

commit v1 on v0

--- a/solution.py
+++ b/solution.py
@@ -83,7 +83,7 @@
     return (earlier[0] * later[0], later[0][:, None, None] * earlier[1] + later[1])
 
 
-def exclusive_scan(decay, state, axis, radix=4):
+def exclusive_scan(decay, state, axis, radix=2):
     place = lax.axis_index(axis)
     size = lax.axis_size(axis)
     incl = (decay, state)
@@ -108,6 +108,8 @@
 
 def flash_kernel(first_ref, q_ref, k_ref, v_ref, o_ref, top_ref, total_ref, acc_ref, *, row_count, key_block, scale):
     j = pl.program_id(1)
+    first = first_ref[0]
+    block_start = j * key_block
 
     @pl.when(j == 0)
     def _():
@@ -115,29 +117,39 @@
         total_ref[...] = jnp.zeros(total_ref.shape, jnp.float32)
         acc_ref[...] = jnp.zeros(acc_ref.shape, jnp.float32)
 
-    first = first_ref[0]
-
-    @pl.when(j * key_block <= first + row_count - 1)
-    def _():
+    def update(with_mask):
         scores = (
             lax.dot_general(
                 q_ref[...], k_ref[...], (((1,), (1,)), ((), ())), preferred_element_type=jnp.float32
             )
             * scale
         )
-        rows = lax.broadcasted_iota(jnp.int32, scores.shape, 0) % row_count + first
-        cols = lax.broadcasted_iota(jnp.int32, scores.shape, 1) + j * key_block
-        allowed = rows >= cols
-        masked = jnp.where(allowed, scores, -1e30)
+        if with_mask:
+            rows = lax.broadcasted_iota(jnp.int32, (scores.shape[0], 1), 0) % row_count + first
+            cols = lax.broadcasted_iota(jnp.int32, (1, scores.shape[1]), 1) + block_start
+            allowed = rows >= cols
+            scores = jnp.where(allowed, scores, -1e30)
         row_top = top_ref[...]
-        new_top = jnp.maximum(row_top, jnp.max(masked, axis=1, keepdims=True))
-        raw_weight = jnp.where(allowed, jnp.exp(masked - new_top), 0.0)
+        new_top = jnp.maximum(row_top, jnp.max(scores, axis=1, keepdims=True))
+        raw_weight = jnp.exp(scores - new_top)
+        if with_mask:
+            raw_weight = jnp.where(allowed, raw_weight, 0.0)
         factor = jnp.exp(row_top - new_top)
         total_ref[...] = total_ref[...] * factor + jnp.sum(raw_weight, axis=1, keepdims=True)
         acc_ref[...] = acc_ref[...] * factor + jnp.dot(
             raw_weight.astype(jnp.bfloat16), v_ref[...], preferred_element_type=jnp.float32
         )
         top_ref[...] = new_top
+
+    @pl.when(block_start + key_block - 1 <= first)
+    def _():
+        update(False)
+
+    @pl.when(
+        jnp.logical_and(block_start + key_block - 1 > first, block_start <= first + row_count - 1)
+    )
+    def _():
+        update(True)
 
     @pl.when(j == pl.num_programs(1) - 1)
     def _():
@@ -157,7 +169,7 @@
     both = jnp.concatenate([keys, values], axis=1).transpose(1, 0, 2)
     both_all = lax.all_gather(both, "ctx", axis=1, tiled=True)
     key_count = both_all.shape[1]
-    key_block = math.gcd(key_count, 512)
+    key_block = math.gcd(key_count, 1024)
     rows = group_size * row_count
 
     def key_index(h, j, first_ref):

time: 259 us -> 235 us (0.907)
  Pallas kernels: 45 us -> 33.2 us
  starting transfers between devices: 29.2 us -> 21.4 us
  waiting for transfers between devices: 143 us -> 136 us
    ppermute x17 -> x11, waiting for transfers between devices: 127 us -> 108 us  [shifted_up(): return lax.ppermute(value, axis, pairs)]
    pallas_call x1, Pallas kernels: 45 us -> 33.2 us  [attention_half(): pl.pallas_call(functools.partial(flash_kernel, row_count=row_count, key_b...]
    all_gather x1, waiting for transfers between devices: 13 us -> 24 us  [attention_half(): both_all = lax.all_gather(both, 'ctx', axis=1, tiled=True)]
    ppermute x17 -> x11, starting transfers between devices: 26.2 us -> 18.7 us  [shifted_up(): return lax.ppermute(value, axis, pairs)]
    add x2 -> x5, other arithmetic: 5.57 us -> 6.78 us  [merge_states(): later[0][:, None, None] * earlier[1] + later[1]]
  transfers between devices with their start and end apart: 20 -> 14, of which waited for: 9 -> 14; matrix products, arithmetic and copies ran while one was open for 8% -> 10% of each run, Pallas kernels for 0% -> 0%
where the time goes in v1:
time: 235 us; the launch traced here: 234 us
  waiting for transfers between devices  136 us (58%)
  Pallas kernels  33.2 us (14%)
  starting transfers between devices  21.4 us (9%)
  between operations  13.8 us (6%)
  matrix products  12 us (5%)
  other arithmetic  9.86 us (4%)
  local copies, waits for them, and re-layouts  6.92 us (3%)
    ppermute x11, waiting for transfers between devices, shifted_up(): return lax.ppermute(value, axis, pairs)  108 us
    pallas_call x1, Pallas kernels, attention_half(): pl.pallas_call(functools.partial(flash_kernel, row_count=row_count, key_b...  33.2 us
    all_gather x1, waiting for transfers between devices, attention_half(): both_all = lax.all_gather(both, 'ctx', axis=1, tiled=True)  24 us
    ppermute x11, starting transfers between devices, shifted_up(): return lax.ppermute(value, axis, pairs)  18.7 us
    add x5, other arithmetic, merge_states(): later[0][:, None, None] * earlier[1] + later[1]  6.78 us
  transfers between devices with their start and end apart: 14, of which 14 were waited for; matrix products, arithmetic and copies ran while one was open for 10% of the time, Pallas kernels for 0%

profile of v1, /device:TPU:231, one launch (start us, length us, event | category | flops | bytes accessed | tf_op | source)
XLA Modules:
  0.0 233.6 jit_solution(747249023533060424)
XLA Ops:
  8.5 1.3 copy.42
  9.8 1.4 fusion.42
  11.2 4.1 %fusion = f32[128,1024]{0,1:T(8,128)S(1)} fusion(bf16[128,2048]{1,0:T(8,128)(2,1)} %param.13, bf16[1,2048,1024]{2,1,0:T(8,128)(2,1)} %param.14), kind=kOutput, calls=%fused_computation | convolution fusion | flops 536870912 | bytes 5242880 | tf_op jit(solution)/shard_map/dot_general | solution.py:233
  15.7 1.4 collective-permute-start
  17.2 3.2 %collective-permute-done = f32[128,273]{0,1:T(8,128)S(1)} collective-permute-done((f32[128,273]{0,1:T(8,128)S(1)}, f32[128,273]{0,1:T(8,128)S(1)}, u32[]{:S(2)}, u32[]{:S(2)}) %collective-permute-start) | collective-permute-done | bytes 139808 | tf_op jit(solution)/shard_map/ppermute | solution.py:25
  21.7 4.8 %collective-permute-start.6 = (f32[16,64,128]{2,1,0:T(8,128)S(1)}, f32[16,64,128]{2,1,0:T(8,128)}, u32[]{:S(2)}, u32[]{:S(2)}) collective-permute-start(f32[16,64,128]{2,1,0:T(8,128)S(1)} %fusion.58), channel_id=1, source_target_pairs={{0,2},{2,4},{4,6},{6,8},{8,10},{10,12},{12,14},{14,16},{16,18},{18... | collective-permute-start | bytes 1572872 | tf_op jit(solution)/shard_map/ppermute | solution.py:21
  26.5 13.7 %collective-permute-done.6 = f32[16,64,128]{2,1,0:T(8,128)} collective-permute-done((f32[16,64,128]{2,1,0:T(8,128)S(1)}, f32[16,64,128]{2,1,0:T(8,128)}, u32[]{:S(2)}, u32[]{:S(2)}) %collective-permute-start.6) | collective-permute-done | bytes 524320 | tf_op jit(solution)/shard_map/ppermute | solution.py:21
  41.4 1.3 collective-permute-start.7
  42.7 1.9 collective-permute-start.1
  44.6 9.9 %collective-permute-done.1 = f32[16]{0:T(128)S(1)} collective-permute-done((f32[16]{0:T(128)S(1)}, f32[16]{0:T(128)S(1)}, u32[]{:S(2)}, u32[]{:S(2)}) %collective-permute-start.1) | collective-permute-done | bytes 96 | tf_op jit(solution)/shard_map/ppermute | solution.py:21
  54.5 1.4 collective-permute-done.7
  57.9 1.3 collective-permute-start.8
  59.2 1.3 collective-permute-start.2
  60.5 3.1 %collective-permute-done.2 = f32[16]{0:T(128)S(1)} collective-permute-done((f32[16]{0:T(128)S(1)}, f32[16]{0:T(128)S(1)}, u32[]{:S(2)}, u32[]{:S(2)}) %collective-permute-start.2) | collective-permute-done | bytes 96 | tf_op jit(solution)/shard_map/ppermute | solution.py:21
  63.6 24.6 %collective-permute-done.8 = f32[16,64,128]{2,1,0:T(8,128)S(1)} collective-permute-done((f32[16,64,128]{2,1,0:T(8,128)S(1)}, f32[16,64,128]{2,1,0:T(8,128)S(1)}, u32[]{:S(2)}, u32[]{:S(2)}) %collective-permute-start.8) | collective-permute-done | bytes 524320 | tf_op jit(solution)/shard_map/ppermute | solution.py:21
  88.2 1.3 multiply_add_fusion.2
  89.5 1.3 collective-permute-start.9
  92.9 5.8 %collective-permute-done.3 = f32[16]{0:T(128)S(1)} collective-permute-done((f32[16]{0:T(128)S(1)}, f32[16]{0:T(128)S(1)}, u32[]{:S(2)}, u32[]{:S(2)}) %collective-permute-start.3) | collective-permute-done | bytes 96 | tf_op jit(solution)/shard_map/ppermute | solution.py:21
  98.7 8.3 %collective-permute-done.9 = f32[16,64,128]{2,1,0:T(8,128)} collective-permute-done((f32[16,64,128]{2,1,0:T(8,128)S(1)}, f32[16,64,128]{2,1,0:T(8,128)}, u32[]{:S(2)}, u32[]{:S(2)}) %collective-permute-start.9) | collective-permute-done | bytes 524320 | tf_op jit(solution)/shard_map/ppermute | solution.py:21
  108.2 1.4 collective-permute-start.10
  111.3 14.8 %collective-permute-done.4 = f32[16]{0:T(128)S(1)} collective-permute-done((f32[16]{0:T(128)S(1)}, f32[16]{0:T(128)S(1)}, u32[]{:S(2)}, u32[]{:S(2)}) %collective-permute-start.4) | collective-permute-done | bytes 96 | tf_op jit(solution)/shard_map/ppermute | solution.py:21
  126.1 15.8 %collective-permute-done.10 = f32[16,64,128]{2,1,0:T(8,128)} collective-permute-done((f32[16,64,128]{2,1,0:T(8,128)S(1)}, f32[16,64,128]{2,1,0:T(8,128)}, u32[]{:S(2)}, u32[]{:S(2)}) %collective-permute-start.10) | collective-permute-done | bytes 524320 | tf_op jit(solution)/shard_map/ppermute | solution.py:21
  141.9 2.0 multiply_add_fusion
  145.6 2.2 fusion.2
  147.8 1.5 collective-permute-start.5
  149.3 3.8 %collective-permute-done.5 = f32[16]{0:T(128)S(1)} collective-permute-done((f32[16]{0:T(128)S(1)}, f32[16]{0:T(128)S(1)}, u32[]{:S(2)}, u32[]{:S(2)}) %collective-permute-start.5) | collective-permute-done | bytes 96 | tf_op jit(solution)/shard_map/ppermute | solution.py:21
  153.1 6.9 %collective-permute-done.11 = f32[16,64,128]{2,1,0:T(8,128)} collective-permute-done((f32[16,64,128]{2,1,0:T(8,128)}, f32[16,64,128]{2,1,0:T(8,128)}, u32[]{:S(2)}, u32[]{:S(2)}) %collective-permute-start.11) | collective-permute-done | bytes 524320 | tf_op jit(solution)/shard_map/ppermute | solution.py:21
  160.1 3.4 %fusion.12 = (f32[128,16]{0,1:T(8,128)S(1)}, f32[16,64,128]{2,1,0:T(8,128)}) fusion(f32[16,64,128]{2,1,0:T(8,128)S(1)} %fusion.2, f32[16]{0:T(128)S(1)} %fusion.67, f32[128,16]{0,1:T(8,128)S(1)} %copy.50, f32[128,1024]{0,1:T(8,128)S(1)} %get-tuple-element.14, f32[128,273]{0,1:T(8,128)S(1)} %fusion.56, f32[128]{0:T(128)S(1)} %fusion.70, ...), kind=kOutput, calls=%fused_computation.16 | convolution fusion | flops 204355584 | bytes 4804102 | tf_op jit(solution)/shard_map/tgn,gkpn->tgkp/dot_general | solution.py:69
  163.4 24.0 %all-gather.2.cloned.1.call-done.k_ref.v_ref = bf16[4,8192,128]{2,1,0:T(8,128)(2,1)} async-done(((bf16[4,128,128]{2,1,0:T(8,128)(2,1)}), bf16[4,8192,128]{2,1,0:T(8,128)(2,1)}) %all-gather.2.cloned.1.call-update) | async-done | bytes 8388624 | tf_op jit(solution)/shard_map/all_gather | solution.py:170
  187.4 33.2 %shard_map.100 = bf16[2,512,128]{2,1,0:T(8,128)(2,1)} custom-call(s32[1]{0:T(128)} %bitcast.27.first_ref, bf16[2,512,128]{2,1,0:T(8,128)(2,1)} %bitcast.110, bf16[4,8192,128]{2,1,0:T(8,128)(2,1)} %all-gather.2.cloned.1.call-done.k_ref.v_ref, bf16[4,8192,128]{2,1,0:T(8,128)(2,1)} %all-gather.2.cloned.1.call-done.k_ref.v_ref), custom_call_target="tpu_custom_call" | custom-call | tf_op jit(solution)/shard_map/pallas_call | solution.py:181
  221.7 1.4 bitcast_select_fusion.1
  223.2 1.4 collective-permute-start.12
  (70 shorter events, 16.7 us)
Async XLA Ops:
  6.5 84.3 %copy-start = (bf16[128,16,128]{2,1,0:T(8,128)(2,1)S(1)}, bf16[128,16,128]{2,1,0:T(8,128)(2,1)}, u32[]{:S(2)}) copy-start(bf16[128,16,128]{2,1,0:T(8,128)(2,1)} %param.10) | copy-start | bytes 1572868
  6.5 180.9 %all-gather.2.cloned.1.call-start = ((), (), s32[]{:S(2)}) async-start(), calls=%async_computation | async-start | bytes 8519680 | tf_op jit(solution)/shard_map/all_gather | solution.py:170
  11.2 5.9 %copy-start.6 = (f32[1,32]{1,0:T(1,128)S(1)}, f32[1,32]{1,0:T(1,128)}, u32[]{:S(2)}) copy-start(f32[1,32]{1,0:T(1,128)} %param.16) | copy-start | bytes 388
  11.2 5.9 %copy-start.7 = (f32[1,32]{1,0:T(1,128)S(1)}, f32[1,32]{1,0:T(1,128)}, u32[]{:S(2)}) copy-start(f32[1,32]{1,0:T(1,128)} %param.17) | copy-start | bytes 388
  15.7 4.7 %collective-permute-start = (f32[128,273]{0,1:T(8,128)S(1)}, f32[128,273]{0,1:T(8,128)S(1)}, u32[]{:S(2)}, u32[]{:S(2)}) collective-permute-start(f32[128,273]{0,1:T(8,128)S(1)} %pad_maximum_fusion), channel_id=1, source_target_pairs={{0,1},{1,0},{2,3},{3,2},{4,5},{5,4},{6,7},{7,6},{8,9},{9,8},{10,11... | collective-permute-start | bytes 419336 | tf_op jit(solution)/shard_map/ppermute | solution.py:25
  21.1 88.6 %copy-start.8 = (f32[1,32]{1,0:T(1,128)S(1)}, f32[1,32]{1,0:T(1,128)}, u32[]{:S(2)}) copy-start(f32[1,32]{1,0:T(1,128)} %param.18) | copy-start | bytes 388
  21.1 88.8 %copy-start.5 = (f32[1,32,64]{2,1,0:T(8,128)S(1)}, f32[1,32,64]{2,1,0:T(8,128)}, u32[]{:S(2)}) copy-start(f32[1,32,64]{2,1,0:T(8,128)} %param.19) | copy-start | bytes 24580
  21.7 18.5 %collective-permute-start.6 = (f32[16,64,128]{2,1,0:T(8,128)S(1)}, f32[16,64,128]{2,1,0:T(8,128)}, u32[]{:S(2)}, u32[]{:S(2)}) collective-permute-start(f32[16,64,128]{2,1,0:T(8,128)S(1)} %fusion.58), channel_id=1, source_target_pairs={{0,2},{2,4},{4,6},{6,8},{8,10},{10,12},{12,14},{14,16},{16,18},{18... | collective-permute-start | bytes 1572872 | tf_op jit(solution)/shard_map/ppermute | solution.py:21
  41.4 14.6 %collective-permute-start.7 = (f32[16,64,128]{2,1,0:T(8,128)S(1)}, f32[16,64,128]{2,1,0:T(8,128)S(1)}, u32[]{:S(2)}, u32[]{:S(2)}) collective-permute-start(f32[16,64,128]{2,1,0:T(8,128)S(1)} %multiply_add_fusion.4), channel_id=1, source_target_pairs={{0,4},{2,6},{4,8},{6,10},{8,12},{10,14},{12,16},{14,18},{16,20},{1... | collective-permute-start | bytes 1572872 | tf_op jit(solution)/shard_map/ppermute | solution.py:21
  42.7 11.9 %collective-permute-start.1 = (f32[16]{0:T(128)S(1)}, f32[16]{0:T(128)S(1)}, u32[]{:S(2)}, u32[]{:S(2)}) collective-permute-start(f32[16]{0:T(128)S(1)} %fusion.79), channel_id=1, source_target_pairs={{0,2},{2,4},{4,6},{6,8},{8,10},{10,12},{12,14},{14,16},{16,18},{18... | collective-permute-start | bytes 200 | tf_op jit(solution)/shard_map/ppermute | solution.py:21
  55.9 0.8 copy-start.2
  57.9 5.7 %copy-start.1 = (f32[16,64,128]{2,1,0:T(8,128)}, f32[16,64,128]{2,1,0:T(8,128)S(1)}, u32[]{:S(2)}) copy-start(f32[16,64,128]{2,1,0:T(8,128)S(1)} %multiply_add_fusion.3) | copy-start | bytes 1572868
  57.9 30.3 %collective-permute-start.8 = (f32[16,64,128]{2,1,0:T(8,128)S(1)}, f32[16,64,128]{2,1,0:T(8,128)S(1)}, u32[]{:S(2)}, u32[]{:S(2)}) collective-permute-start(f32[16,64,128]{2,1,0:T(8,128)S(1)} %multiply_add_fusion.3), channel_id=1, source_target_pairs={{0,8},{2,10},{4,12},{6,14},{8,16},{10,18},{12,20},{14,22},{16,24},... | collective-permute-start | bytes 1572872 | tf_op jit(solution)/shard_map/ppermute | solution.py:21
  59.2 4.4 %collective-permute-start.2 = (f32[16]{0:T(128)S(1)}, f32[16]{0:T(128)S(1)}, u32[]{:S(2)}, u32[]{:S(2)}) collective-permute-start(f32[16]{0:T(128)S(1)} %get-tuple-element.11), channel_id=1, source_target_pairs={{0,4},{2,6},{4,8},{6,10},{8,12},{10,14},{12,16},{14,18},{16,20},{1... | collective-permute-start | bytes 200 | tf_op jit(solution)/shard_map/ppermute | solution.py:21
  88.2 10.5 %copy-start.3 = (f32[16,64,128]{2,1,0:T(8,128)}, f32[16,64,128]{2,1,0:T(8,128)S(1)}, u32[]{:S(2)}) copy-start(f32[16,64,128]{2,1,0:T(8,128)S(1)} %collective-permute-done.8) | copy-start | bytes 1572868
  89.5 17.5 %collective-permute-start.9 = (f32[16,64,128]{2,1,0:T(8,128)S(1)}, f32[16,64,128]{2,1,0:T(8,128)}, u32[]{:S(2)}, u32[]{:S(2)}) collective-permute-start(f32[16,64,128]{2,1,0:T(8,128)S(1)} %multiply_add_fusion.2), channel_id=1, source_target_pairs={{0,16},{2,18},{4,20},{6,22},{8,24},{10,26},{12,28},{14,30},{16,32}... | collective-permute-start | bytes 1572872 | tf_op jit(solution)/shard_map/ppermute | solution.py:21
  90.9 7.8 %collective-permute-start.3 = (f32[16]{0:T(128)S(1)}, f32[16]{0:T(128)S(1)}, u32[]{:S(2)}, u32[]{:S(2)}) collective-permute-start(f32[16]{0:T(128)S(1)} %fusion.76), channel_id=1, source_target_pairs={{0,8},{2,10},{4,12},{6,14},{8,16},{10,18},{12,20},{14,22},{16,24},... | collective-permute-start | bytes 200 | tf_op jit(solution)/shard_map/ppermute | solution.py:21
  108.2 51.9 %copy-start.4 = (f32[16,64,128]{2,1,0:T(8,128)S(1)}, f32[16,64,128]{2,1,0:T(8,128)}, u32[]{:S(2)}) copy-start(f32[16,64,128]{2,1,0:T(8,128)} %copy-done.3) | copy-start | bytes 1572868
  108.2 33.7 %collective-permute-start.10 = (f32[16,64,128]{2,1,0:T(8,128)S(1)}, f32[16,64,128]{2,1,0:T(8,128)}, u32[]{:S(2)}, u32[]{:S(2)}) collective-permute-start(f32[16,64,128]{2,1,0:T(8,128)S(1)} %multiply_add_fusion.1), channel_id=1, source_target_pairs={{0,32},{2,34},{4,36},{6,38},{8,40},{10,42},{12,44},{14,46},{16,48}... | collective-permute-start | bytes 1572872 | tf_op jit(solution)/shard_map/ppermute | solution.py:21
  109.9 16.2 %collective-permute-start.4 = (f32[16]{0:T(128)S(1)}, f32[16]{0:T(128)S(1)}, u32[]{:S(2)}, u32[]{:S(2)}) collective-permute-start(f32[16]{0:T(128)S(1)} %fusion.74), channel_id=1, source_target_pairs={{0,16},{2,18},{4,20},{6,22},{8,24},{10,26},{12,28},{14,30},{16,32}... | collective-permute-start | bytes 200 | tf_op jit(solution)/shard_map/ppermute | solution.py:21
  143.9 16.2 %collective-permute-start.11 = (f32[16,64,128]{2,1,0:T(8,128)}, f32[16,64,128]{2,1,0:T(8,128)}, u32[]{:S(2)}, u32[]{:S(2)}) collective-permute-start(f32[16,64,128]{2,1,0:T(8,128)} %multiply_add_fusion), channel_id=1, source_target_pairs={{0,64},{2,66},{4,68},{6,70},{8,72},{10,74},{12,76},{14,78},{16,80}... | collective-permute-start | bytes 1572872 | tf_op jit(solution)/shard_map/ppermute | solution.py:21
  147.8 5.3 %collective-permute-start.5 = (f32[16]{0:T(128)S(1)}, f32[16]{0:T(128)S(1)}, u32[]{:S(2)}, u32[]{:S(2)}) collective-permute-start(f32[16]{0:T(128)S(1)} %fusion.72), channel_id=1, source_target_pairs={{0,32},{2,34},{4,36},{6,38},{8,40},{10,42},{12,44},{14,46},{16,48}... | collective-permute-start | bytes 200 | tf_op jit(solution)/shard_map/ppermute | solution.py:21
  223.2 2.5 %collective-permute-start.12 = (bf16[128,1024]{0,1:T(8,128)(2,1)S(1)}, bf16[128,1024]{0,1:T(8,128)(2,1)S(1)}, u32[]{:S(2)}, u32[]{:S(2)}) collective-permute-start(bf16[128,1024]{0,1:T(8,128)(2,1)S(1)} %get-tuple-element.5), channel_id=1, source_target_pairs={{0,128},{128,0},{1,129},{129,1},{2,130},{130,2},{3,131},{131,3},{4... | collective-permute-start | bytes 786440 | tf_op jit(solution)/shard_map/ppermute | solution.py:25
Sparse Core Ops, SparseCore 0:
  10.9 176.5 all-gather.1

commit v2 on v1

--- a/solution.py
+++ b/solution.py
@@ -13,6 +13,7 @@
 
 
 EPSILON = 1e-05
+CTX = ("cx", "cr")
 
 
 def shifted_up(value, axis, distance):
@@ -106,16 +107,16 @@
     return excl
 
 
-def flash_kernel(first_ref, q_ref, k_ref, v_ref, o_ref, top_ref, total_ref, acc_ref, *, row_count, key_block, scale):
+def flash_kernel(place_ref, q_ref, k_ref, v_ref, top_in, total_in, acc_in, top_ref, total_ref, acc_ref, *, row_count, key_block, scale):
     j = pl.program_id(1)
-    first = first_ref[0]
-    block_start = j * key_block
+    first = place_ref[0]
+    block_start = place_ref[1] + j * key_block
 
     @pl.when(j == 0)
     def _():
-        top_ref[...] = jnp.full(top_ref.shape, -1e30, jnp.float32)
-        total_ref[...] = jnp.zeros(total_ref.shape, jnp.float32)
-        acc_ref[...] = jnp.zeros(acc_ref.shape, jnp.float32)
+        top_ref[...] = top_in[...]
+        total_ref[...] = total_in[...]
+        acc_ref[...] = acc_in[...]
 
     def update(with_mask):
         scores = (
@@ -141,19 +142,67 @@
         )
         top_ref[...] = new_top
 
-    @pl.when(block_start + key_block - 1 <= first)
+    present = block_start >= 0
+
+    @pl.when(jnp.logical_and(present, block_start + key_block - 1 <= first))
     def _():
         update(False)
 
     @pl.when(
-        jnp.logical_and(block_start + key_block - 1 > first, block_start <= first + row_count - 1)
+        jnp.logical_and(
+            jnp.logical_and(present, block_start + key_block - 1 > first),
+            block_start <= first + row_count - 1,
+        )
     )
     def _():
         update(True)
 
-    @pl.when(j == pl.num_programs(1) - 1)
-    def _():
-        o_ref[...] = (acc_ref[...] / total_ref[...]).astype(o_ref.dtype)
+
+def flash_step(grouped, both, first_row, key_start, carried, row_count, scale):
+    kv_heads, rows, head_width = grouped.shape
+    key_count = both.shape[1]
+    key_block = math.gcd(key_count, 1024)
+    block_total = key_count // key_block
+
+    def block_of(j, place_ref):
+        limit = jnp.clip((place_ref[0] + row_count - 1 - place_ref[1]) // key_block, 0, block_total - 1)
+        return jnp.where(place_ref[1] < 0, 0, jnp.minimum(j, limit))
+
+    def key_index(h, j, place_ref):
+        return (h, block_of(j, place_ref), 0)
+
+    def value_index(h, j, place_ref):
+        return (kv_heads + h, block_of(j, place_ref), 0)
+
+    state_spec = lambda width: pl.BlockSpec((None, rows, width), lambda h, j, f: (h, 0, 0))
+    return pl.pallas_call(
+        functools.partial(flash_kernel, row_count=row_count, key_block=key_block, scale=scale),
+        out_shape=(
+            jax.ShapeDtypeStruct((kv_heads, rows, 1), jnp.float32),
+            jax.ShapeDtypeStruct((kv_heads, rows, 1), jnp.float32),
+            jax.ShapeDtypeStruct((kv_heads, rows, head_width), jnp.float32),
+        ),
+        grid_spec=pltpu.PrefetchScalarGridSpec(
+            num_scalar_prefetch=1,
+            grid=(kv_heads, block_total),
+            in_specs=[
+                pl.BlockSpec((None, rows, head_width), lambda h, j, f: (h, 0, 0)),
+                pl.BlockSpec((None, key_block, head_width), key_index),
+                pl.BlockSpec((None, key_block, head_width), value_index),
+                state_spec(1),
+                state_spec(1),
+                state_spec(head_width),
+            ],
+            out_specs=[state_spec(1), state_spec(1), state_spec(head_width)],
+        ),
+        compiler_params=pltpu.CompilerParams(dimension_semantics=("parallel", "arbitrary")),
+    )(
+        jnp.stack([first_row, key_start]).astype(jnp.int32),
+        grouped,
+        both,
+        both,
+        *carried,
+    )
 
 
 def attention_half(queries, keys, values, first_row):
@@ -161,43 +210,31 @@
     kv_heads = keys.shape[1]
     group_size = q_heads // kv_heads
     score_scale = 1.0 / math.sqrt(head_width)
+    rows = group_size * row_count
     grouped = (
         queries.reshape(row_count, kv_heads, group_size, head_width)
         .transpose(1, 2, 0, 3)
-        .reshape(kv_heads, group_size * row_count, head_width)
+        .reshape(kv_heads, rows, head_width)
     )
     both = jnp.concatenate([keys, values], axis=1).transpose(1, 0, 2)
-    both_all = lax.all_gather(both, "ctx", axis=1, tiled=True)
-    key_count = both_all.shape[1]
-    key_block = math.gcd(key_count, 1024)
-    rows = group_size * row_count
-
-    def key_index(h, j, first_ref):
-        return (h, jnp.minimum(j, (first_ref[0] + row_count - 1) // key_block), 0)
-
-    def value_index(h, j, first_ref):
-        return (kv_heads + h, jnp.minimum(j, (first_ref[0] + row_count - 1) // key_block), 0)
-
-    out = pl.pallas_call(
-        functools.partial(flash_kernel, row_count=row_count, key_block=key_block, scale=score_scale),
-        out_shape=jax.ShapeDtypeStruct((kv_heads, rows, head_width), jnp.bfloat16),
-        grid_spec=pltpu.PrefetchScalarGridSpec(
-            num_scalar_prefetch=1,
-            grid=(kv_heads, key_count // key_block),
-            in_specs=[
-                pl.BlockSpec((None, rows, head_width), lambda h, j, f: (h, 0, 0)),
-                pl.BlockSpec((None, key_block, head_width), key_index),
-                pl.BlockSpec((None, key_block, head_width), value_index),
-            ],
-            out_specs=pl.BlockSpec((None, rows, head_width), lambda h, j, f: (h, 0, 0)),
-            scratch_shapes=[
-                pltpu.VMEM((rows, 1), jnp.float32),
-                pltpu.VMEM((rows, 1), jnp.float32),
-                pltpu.VMEM((rows, head_width), jnp.float32),
-            ],
-        ),
-        compiler_params=pltpu.CompilerParams(dimension_semantics=("parallel", "arbitrary")),
-    )(jnp.reshape(first_row, (1,)).astype(jnp.int32), grouped, both_all, both_all)
+    slab = lax.all_gather(both, "cr", axis=1, tiled=True)
+    slab_rows = slab.shape[1]
+    outer = lax.axis_index("cx")
+    outer_count = lax.axis_size("cx")
+    pieces = [shifted_up(slab, "cx", distance) for distance in range(outer_count - 1, 0, -1)]
+    carried = (
+        jnp.full((kv_heads, rows, 1), -1e30, jnp.float32),
+        jnp.zeros((kv_heads, rows, 1), jnp.float32),
+        jnp.zeros((kv_heads, rows, head_width), jnp.float32),
+    )
+    carried = flash_step(grouped, slab, first_row, outer * slab_rows, carried, row_count, score_scale)
+    for index, piece in enumerate(reversed(pieces)):
+        distance = index + 1
+        carried = flash_step(
+            grouped, piece, first_row, (outer - distance) * slab_rows, carried, row_count, score_scale
+        )
+    _, row_total, row_sum = carried
+    out = (row_sum / row_total).astype(jnp.bfloat16)
     return (
         out.reshape(kv_heads, group_size, row_count, head_width)
         .transpose(2, 0, 1, 3)
@@ -212,7 +249,7 @@
     tp_count = lax.axis_size("tp")
     row_count, q_heads, head_width = queries.shape
     kv_heads = keys.shape[1]
-    first_row = lax.axis_index("ctx") * row_count
+    first_row = lax.axis_index(CTX) * row_count
 
     q_share = q_heads // seg_count
     kv_share = kv_heads // seg_count
@@ -269,7 +306,7 @@
     log_decay, local_part, ending, span_decay = span_terms(
         normed, b_rows, c_rows, step_sizes, rate, skip
     )
-    _, state_in = exclusive_scan(span_decay, ending, "ctx")
+    _, state_in = exclusive_scan(span_decay, ending, CTX)
     mixed_out = local_part + span_inflow(log_decay, c_rows, state_in)
     power = jnp.mean(mixed_out * mixed_out, axis=2, keepdims=True)
     result = own_rows.reshape(row_count, heads_core, state_width) + gain[None] * mixed_out * lax.rsqrt(
@@ -286,11 +323,17 @@
 
 
 def solution(mesh):
+    ctx_count = mesh.shape["ctx"]
+    outer_count = 4 if ctx_count % 4 == 0 else 1
+    devices = mesh.devices.reshape(
+        mesh.shape["segment"], outer_count, ctx_count // outer_count, mesh.shape["tp"]
+    )
+    fine = jax.sharding.Mesh(devices, ("segment", "cx", "cr", "tp"))
     in_specs = (
-        P("ctx", "tp", None),
-        P("ctx", "tp", None),
-        P("ctx", "tp", None),
-        P("ctx", "tp"),
+        P(CTX, "tp", None),
+        P(CTX, "tp", None),
+        P(CTX, "tp", None),
+        P(CTX, "tp"),
         P(None, "tp", None),
         P(None, "tp", None),
         P(None, "tp"),
@@ -298,5 +341,5 @@
         P(None, "tp"),
         P(None, "tp", None),
     )
-    out_specs = P("segment", "ctx", "tp")
-    return jax.shard_map(body, mesh=mesh, in_specs=in_specs, out_specs=out_specs, check_vma=False)
+    out_specs = P("segment", CTX, "tp")
+    return jax.shard_map(body, mesh=fine, in_specs=in_specs, out_specs=out_specs, check_vma=False)

time: 235 us -> 305 us (1.30)
  the two profiles are of different devices: /device:TPU:231 before, /device:TPU:13 now
where the time goes in v2:
time: 305 us; the launch traced here: 304 us
  waiting for transfers between devices  188 us (62%)
  Pallas kernels  35 us (11%)
  starting transfers between devices  31.6 us (10%)
  other arithmetic  14.9 us (5%)
  between operations  13.9 us (5%)
  matrix products  12 us (4%)
  local copies, waits for them, and re-layouts  8.92 us (3%)
    ppermute x14, waiting for transfers between devices, shifted_up(): return lax.ppermute(value, axis, pairs)  183 us
    pallas_call x4, Pallas kernels, flash_step(): pl.pallas_call(functools.partial(flash_kernel, row_count=row_count, key_b...  35 us
    ppermute x14, starting transfers between devices, shifted_up(): return lax.ppermute(value, axis, pairs)  29.8 us
    add x5, other arithmetic, merge_states(): later[0][:, None, None] * earlier[1] + later[1]  6.64 us
  transfers between devices with their start and end apart: 17, of which 12 were waited for; matrix products, arithmetic and copies ran while one was open for 7% of the time, Pallas kernels for 10%

profile of v2, /device:TPU:13, one launch (start us, length us, event | category | flops | bytes accessed | tf_op | source)
XLA Modules:
  0.0 303.9 jit_solution(1151021943359360309)
XLA Ops:
  6.6 1.4 copy.42
  8.0 4.1 %fusion = f32[128,1024]{0,1:T(8,128)S(1)} fusion(bf16[128,2048]{1,0:T(8,128)(2,1)} %param.13, bf16[1,2048,1024]{2,1,0:T(8,128)(2,1)} %param.14), kind=kOutput, calls=%fused_computation | convolution fusion | flops 536870912 | bytes 5242880 | tf_op jit(solution)/shard_map/dot_general | solution.py:270
  14.2 3.4 %collective-permute-done = f32[128,273]{0,1:T(8,128)S(1)} collective-permute-done((f32[128,273]{0,1:T(8,128)S(1)}, f32[128,273]{0,1:T(8,128)S(1)}, u32[]{:S(2)}, u32[]{:S(2)}) %collective-permute-start) | collective-permute-done | bytes 139808 | tf_op jit(solution)/shard_map/ppermute | solution.py:26
  18.8 3.9 %collective-permute-start.6 = (f32[16,64,128]{2,1,0:T(8,128)S(1)}, f32[16,64,128]{2,1,0:T(8,128)}, u32[]{:S(2)}, u32[]{:S(2)}) collective-permute-start(f32[16,64,128]{2,1,0:T(8,128)S(1)} %fusion.58), channel_id=1, source_target_pairs={{0,2},{2,4},{4,6},{6,8},{8,10},{10,12},{12,14},{14,16},{16,18},{18... | collective-permute-start | bytes 1572872 | tf_op jit(solution)/shard_map/ppermute | solution.py:22
  22.8 16.8 %collective-permute-done.6 = f32[16,64,128]{2,1,0:T(8,128)} collective-permute-done((f32[16,64,128]{2,1,0:T(8,128)S(1)}, f32[16,64,128]{2,1,0:T(8,128)}, u32[]{:S(2)}, u32[]{:S(2)}) %collective-permute-start.6) | collective-permute-done | bytes 524320 | tf_op jit(solution)/shard_map/ppermute | solution.py:22
  40.8 1.9 collective-permute-start.7
  42.7 1.9 collective-permute-start.1
  44.6 14.1 %collective-permute-done.1 = f32[16]{0:T(128)S(1)} collective-permute-done((f32[16]{0:T(128)S(1)}, f32[16]{0:T(128)S(1)}, u32[]{:S(2)}, u32[]{:S(2)}) %collective-permute-start.1) | collective-permute-done | bytes 96 | tf_op jit(solution)/shard_map/ppermute | solution.py:22
  61.3 1.9 collective-permute-start.8
  64.1 1.9 collective-permute-start.2
  66.1 23.1 %collective-permute-done.2 = f32[16]{0:T(128)S(1)} collective-permute-done((f32[16]{0:T(128)S(1)}, f32[16]{0:T(128)S(1)}, u32[]{:S(2)}, u32[]{:S(2)}) %collective-permute-start.2) | collective-permute-done | bytes 96 | tf_op jit(solution)/shard_map/ppermute | solution.py:22
  89.2 7.3 %collective-permute-done.8 = f32[16,64,128]{2,1,0:T(8,128)} collective-permute-done((f32[16,64,128]{2,1,0:T(8,128)S(1)}, f32[16,64,128]{2,1,0:T(8,128)}, u32[]{:S(2)}, u32[]{:S(2)}) %collective-permute-start.8) | collective-permute-done | bytes 524320 | tf_op jit(solution)/shard_map/ppermute | solution.py:22
  97.7 2.5 collective-permute-start.9
  101.9 2.9 collective-permute-start.3
  105.0 18.7 %collective-permute-done.3 = f32[16]{0:T(128)S(1)} collective-permute-done((f32[16]{0:T(128)S(1)}, f32[16]{0:T(128)S(1)}, u32[]{:S(2)}, u32[]{:S(2)}) %collective-permute-start.3) | collective-permute-done | bytes 96 | tf_op jit(solution)/shard_map/ppermute | solution.py:22
  123.6 4.8 %collective-permute-done.9 = f32[16,64,128]{2,1,0:T(8,128)S(1)} collective-permute-done((f32[16,64,128]{2,1,0:T(8,128)S(1)}, f32[16,64,128]{2,1,0:T(8,128)S(1)}, u32[]{:S(2)}, u32[]{:S(2)}) %collective-permute-start.9) | collective-permute-done | bytes 524320 | tf_op jit(solution)/shard_map/ppermute | solution.py:22
  129.4 3.6 %collective-permute-start.10 = (f32[16,64,128]{2,1,0:T(8,128)}, f32[16,64,128]{2,1,0:T(8,128)}, u32[]{:S(2)}, u32[]{:S(2)}) collective-permute-start(f32[16,64,128]{2,1,0:T(8,128)} %multiply_add_fusion.1), channel_id=1, source_target_pairs={{0,32},{2,34},{4,36},{6,38},{8,40},{10,42},{12,44},{14,46},{16,48}... | collective-permute-start | bytes 1572872 | tf_op jit(solution)/shard_map/ppermute | solution.py:22
  133.0 1.9 collective-permute-start.14
  137.7 1.9 collective-permute-start.4
  139.7 7.1 %collective-permute-done.4 = f32[16]{0:T(128)S(1)} collective-permute-done((f32[16]{0:T(128)S(1)}, f32[16]{0:T(128)S(1)}, u32[]{:S(2)}, u32[]{:S(2)}) %collective-permute-start.4) | collective-permute-done | bytes 96 | tf_op jit(solution)/shard_map/ppermute | solution.py:22
  146.8 2.1 multiply_add_fusion
  150.6 3.1 %fusion.2 = f32[16,64,128]{2,1,0:T(8,128)} fusion(f32[128,16,64]{0,2,1:T(8,128)S(1)} %bitcast.115, f32[16,128]{1,0:T(8,128)S(1)} %get-tuple-element.43, f32[128,128]{1,0:T(8,128)S(1)} %convolution_multiply_fusion, f32[16,128]{1,0:T(8,128)S(1)} %copy.48, pred[128,128]{1,0:T(8,128)(4,1)S(1)} %iota_compare_fusion), kind=kOutput, calls=%fused_computation.3 | convolution fusion | flops 202637312 | bytes 1146880 | tf_op jit(solution)/shard_map/gkts,sgkp->tgkp/dot_general | solution.py:47
  153.7 2.1 collective-permute-start.5
  155.8 33.4 %collective-permute-done.5 = f32[16]{0:T(128)S(1)} collective-permute-done((f32[16]{0:T(128)S(1)}, f32[16]{0:T(128)S(1)}, u32[]{:S(2)}, u32[]{:S(2)}) %collective-permute-start.5) | collective-permute-done | bytes 96 | tf_op jit(solution)/shard_map/ppermute | solution.py:22
  189.3 56.9 %collective-permute-done.11 = f32[16,64,128]{2,1,0:T(8,128)} collective-permute-done((f32[16,64,128]{2,1,0:T(8,128)}, f32[16,64,128]{2,1,0:T(8,128)}, u32[]{:S(2)}, u32[]{:S(2)}) %collective-permute-start.11) | collective-permute-done | bytes 524320 | tf_op jit(solution)/shard_map/ppermute | solution.py:22
  246.2 3.7 %fusion.12 = (f32[128,16]{0,1:T(8,128)S(1)}, f32[16,64,128]{2,1,0:T(8,128)}) fusion(f32[16,64,128]{2,1,0:T(8,128)} %fusion.2, f32[16]{0:T(128)S(1)} %fusion.67, f32[128,16]{0,1:T(8,128)S(1)} %copy.50, f32[128,1024]{0,1:T(8,128)S(1)} %get-tuple-element.36, f32[128,273]{0,1:T(8,128)S(1)} %fusion.56, f32[128]{0:T(128)S(1)} %fusion.70, ...), kind=kOutput, calls=%fused_computation.16 | convolution fusion | flops 204355584 | bytes 4804102 | tf_op jit(solution)/shard_map/tgn,gkpn->tgkp/dot_general | solution.py:70
  252.4 8.6 %shard_map.100 = (f32[2,512,1]{2,1,0:T(8,128)}, f32[2,512,1]{2,1,0:T(8,128)}, f32[2,512,128]{2,1,0:T(8,128)}) custom-call(s32[2]{0:T(128)} %pad_add_fusion.3.place_ref, bf16[2,512,128]{2,1,0:T(8,128)(2,1)} %bitcast.111, bf16[4,2048,128]{2,1,0:T(8,128)(2,1)} %all-gather.2.cloned.1.call-done.k_ref.v_ref, ...), custom_call_target="tpu_custom_call" | custom-call | tf_op jit(solution)/shard_map/pallas_call | solution.py:178
  261.0 10.7 %shard_map.101 = (f32[2,512,1]{2,1,0:T(8,128)}, f32[2,512,1]{2,1,0:T(8,128)}, f32[2,512,128]{2,1,0:T(8,128)}) custom-call(s32[2]{0:T(128)} %pad_add_fusion.2.place_ref, bf16[2,512,128]{2,1,0:T(8,128)(2,1)} %bitcast.112, bf16[4,2048,128]{2,1,0:T(8,128)(2,1)} %collective-permute-done.14.k_ref.v_ref, bf16[4,2048,128]{2,1,0:T(8,128)(2,1)} %collective-permute-done.14.k_ref.v_ref, ...), custom_call_target="tpu_custom_call" | custom-call | tf_op jit(solution)/shard_map/pallas_call | solution.py:178
  271.7 10.8 %shard_map.102 = (f32[2,512,1]{2,1,0:T(8,128)}, f32[2,512,1]{2,1,0:T(8,128)}, f32[2,512,128]{2,1,0:T(8,128)}) custom-call(s32[2]{0:T(128)} %pad_add_fusion.1.place_ref, bf16[2,512,128]{2,1,0:T(8,128)(2,1)} %bitcast.113, bf16[4,2048,128]{2,1,0:T(8,128)(2,1)} %collective-permute-done.13.k_ref.v_ref, bf16[4,2048,128]{2,1,0:T(8,128)(2,1)} %collective-permute-done.13.k_ref.v_ref, ...), custom_call_target="tpu_custom_call" | custom-call | tf_op jit(solution)/shard_map/pallas_call | solution.py:178
  283.9 5.0 %shard_map.103 = (f32[2,512,1]{2,1,0:T(8,128)}, f32[2,512,1]{2,1,0:T(8,128)}, f32[2,512,128]{2,1,0:T(8,128)}) custom-call(s32[2]{0:T(128)} %pad_add_fusion.place_ref, bf16[2,512,128]{2,1,0:T(8,128)(2,1)} %bitcast.114, bf16[4,2048,128]{2,1,0:T(8,128)(2,1)} %copy-done.1, bf16[4,2048,128]{2,1,0:T(8,128)(2,1)} %copy-done.1, ...), custom_call_target="tpu_custom_call" | custom-call | tf_op jit(solution)/shard_map/pallas_call | solution.py:178
  291.5 1.7 bitcast_select_fusion.1
  293.3 1.5 collective-permute-start.15
  (96 shorter events, 25.2 us)
Async XLA Ops:
  6.5 56.8 %copy-start = (bf16[128,16,128]{2,1,0:T(8,128)(2,1)S(1)}, bf16[128,16,128]{2,1,0:T(8,128)(2,1)}, u32[]{:S(2)}) copy-start(bf16[128,16,128]{2,1,0:T(8,128)(2,1)} %param.10) | copy-start | bytes 1572868
  6.5 5.6 %copy-start.2 = (bf16[128,2048]{1,0:T(8,128)(2,1)S(1)}, bf16[128,2048]{1,0:T(8,128)(2,1)}, u32[]{:S(2)}) copy-start(bf16[128,2048]{1,0:T(8,128)(2,1)} %param.13) | copy-start | bytes 1572868
  6.5 5.6 %copy-start.6 = (bf16[1,2048,64]{1,2,0:T(8,128)(2,1)S(1)}, bf16[1,2048,64]{1,2,0:T(8,128)(2,1)}, u32[]{:S(2)}) copy-start(bf16[1,2048,64]{1,2,0:T(8,128)(2,1)} %param.15) | copy-start | bytes 786436
  6.5 126.5 %all-gather.2.cloned.1.call-start = ((), (), s32[]{:S(2)}) async-start(), calls=%async_computation | async-start | bytes 2228224 | tf_op jit(solution)/shard_map/all_gather | solution.py:220
  6.6 6.5 %copy-start.7 = (bf16[128,4,128]{2,1,0:T(4,128)(2,1)S(1)}, bf16[128,4,128]{2,1,0:T(4,128)(2,1)}, u32[]{:S(2)}) copy-start(bf16[128,4,128]{2,1,0:T(4,128)(2,1)} %param.12) | copy-start | bytes 393220
  6.6 6.5 %copy-start.8 = (bf16[128,4,128]{2,1,0:T(4,128)(2,1)S(1)}, bf16[128,4,128]{2,1,0:T(4,128)(2,1)}, u32[]{:S(2)}) copy-start(bf16[128,4,128]{2,1,0:T(4,128)(2,1)} %param.11) | copy-start | bytes 393220
  8.0 6.1 %copy-start.10 = (f32[1,32]{1,0:T(1,128)S(1)}, f32[1,32]{1,0:T(1,128)}, u32[]{:S(2)}) copy-start(f32[1,32]{1,0:T(1,128)} %param.16) | copy-start | bytes 388
  8.0 6.1 %copy-start.11 = (f32[1,32]{1,0:T(1,128)S(1)}, f32[1,32]{1,0:T(1,128)}, u32[]{:S(2)}) copy-start(f32[1,32]{1,0:T(1,128)} %param.17) | copy-start | bytes 388
  12.8 4.7 %collective-permute-start = (f32[128,273]{0,1:T(8,128)S(1)}, f32[128,273]{0,1:T(8,128)S(1)}, u32[]{:S(2)}, u32[]{:S(2)}) collective-permute-start(f32[128,273]{0,1:T(8,128)S(1)} %pad_maximum_fusion), channel_id=1, source_target_pairs={{0,1},{1,0},{2,3},{3,2},{4,5},{5,4},{6,7},{7,6},{8,9},{9,8},{10,11... | collective-permute-start | bytes 419336 | tf_op jit(solution)/shard_map/ppermute | solution.py:26
  14.0 83.6 %copy-start.3 = (f32[128,2048]{0,1:T(8,128)}, f32[128,2048]{0,1:T(8,128)S(1)}, u32[]{:S(2)}) copy-start(f32[128,2048]{0,1:T(8,128)S(1)} %convert_element_type.9) | copy-start | bytes 3145732
  14.1 50.0 %copy-start.12 = (f32[1,32]{1,0:T(1,128)S(1)}, f32[1,32]{1,0:T(1,128)}, u32[]{:S(2)}) copy-start(f32[1,32]{1,0:T(1,128)} %param.18) | copy-start | bytes 388
  18.2 119.4 %copy-start.9 = (f32[1,32,64]{2,1,0:T(8,128)S(1)}, f32[1,32,64]{2,1,0:T(8,128)}, u32[]{:S(2)}) copy-start(f32[1,32,64]{2,1,0:T(8,128)} %param.19) | copy-start | bytes 24580
  18.8 20.8 %collective-permute-start.6 = (f32[16,64,128]{2,1,0:T(8,128)S(1)}, f32[16,64,128]{2,1,0:T(8,128)}, u32[]{:S(2)}, u32[]{:S(2)}) collective-permute-start(f32[16,64,128]{2,1,0:T(8,128)S(1)} %fusion.58), channel_id=1, source_target_pairs={{0,2},{2,4},{4,6},{6,8},{8,10},{10,12},{12,14},{14,16},{16,18},{18... | collective-permute-start | bytes 1572872 | tf_op jit(solution)/shard_map/ppermute | solution.py:22
  40.8 18.6 %collective-permute-start.7 = (f32[16,64,128]{2,1,0:T(8,128)S(1)}, f32[16,64,128]{2,1,0:T(8,128)S(1)}, u32[]{:S(2)}, u32[]{:S(2)}) collective-permute-start(f32[16,64,128]{2,1,0:T(8,128)S(1)} %multiply_add_fusion.4), channel_id=1, source_target_pairs={{0,4},{2,6},{4,8},{6,10},{8,12},{10,14},{12,16},{14,18},{16,20},{1... | collective-permute-start | bytes 1572872 | tf_op jit(solution)/shard_map/ppermute | solution.py:22
  42.7 16.1 %collective-permute-start.1 = (f32[16]{0:T(128)S(1)}, f32[16]{0:T(128)S(1)}, u32[]{:S(2)}, u32[]{:S(2)}) collective-permute-start(f32[16]{0:T(128)S(1)} %fusion.79), channel_id=1, source_target_pairs={{0,2},{2,4},{4,6},{6,8},{8,10},{10,12},{12,14},{14,16},{16,18},{18... | collective-permute-start | bytes 200 | tf_op jit(solution)/shard_map/ppermute | solution.py:22
  59.4 0.8 copy-start.4
  61.3 35.2 %collective-permute-start.8 = (f32[16,64,128]{2,1,0:T(8,128)S(1)}, f32[16,64,128]{2,1,0:T(8,128)}, u32[]{:S(2)}, u32[]{:S(2)}) collective-permute-start(f32[16,64,128]{2,1,0:T(8,128)S(1)} %multiply_add_fusion.3), channel_id=1, source_target_pairs={{0,8},{2,10},{4,12},{6,14},{8,16},{10,18},{12,20},{14,22},{16,24},... | collective-permute-start | bytes 1572872 | tf_op jit(solution)/shard_map/ppermute | solution.py:22
  64.1 25.1 %collective-permute-start.2 = (f32[16]{0:T(128)S(1)}, f32[16]{0:T(128)S(1)}, u32[]{:S(2)}, u32[]{:S(2)}) collective-permute-start(f32[16]{0:T(128)S(1)} %get-tuple-element.33), channel_id=1, source_target_pairs={{0,4},{2,6},{4,8},{6,10},{8,12},{10,14},{12,16},{14,18},{16,20},{1... | collective-permute-start | bytes 200 | tf_op jit(solution)/shard_map/ppermute | solution.py:22
  97.7 30.7 %collective-permute-start.9 = (f32[16,64,128]{2,1,0:T(8,128)S(1)}, f32[16,64,128]{2,1,0:T(8,128)S(1)}, u32[]{:S(2)}, u32[]{:S(2)}) collective-permute-start(f32[16,64,128]{2,1,0:T(8,128)S(1)} %multiply_add_fusion.2), channel_id=1, source_target_pairs={{0,16},{2,18},{4,20},{6,22},{8,24},{10,26},{12,28},{14,30},{16,32}... | collective-permute-start | bytes 1572872 | tf_op jit(solution)/shard_map/ppermute | solution.py:22
  101.9 21.7 %collective-permute-start.3 = (f32[16]{0:T(128)S(1)}, f32[16]{0:T(128)S(1)}, u32[]{:S(2)}, u32[]{:S(2)}) collective-permute-start(f32[16]{0:T(128)S(1)} %fusion.76), channel_id=1, source_target_pairs={{0,8},{2,10},{4,12},{6,14},{8,16},{10,18},{12,20},{14,22},{16,24},... | collective-permute-start | bytes 200 | tf_op jit(solution)/shard_map/ppermute | solution.py:22
  128.4 6.5 %copy-start.5 = (f32[16,64,128]{2,1,0:T(8,128)}, f32[16,64,128]{2,1,0:T(8,128)S(1)}, u32[]{:S(2)}) copy-start(f32[16,64,128]{2,1,0:T(8,128)S(1)} %collective-permute-done.9) | copy-start | bytes 1572868
  129.4 17.4 %collective-permute-start.10 = (f32[16,64,128]{2,1,0:T(8,128)}, f32[16,64,128]{2,1,0:T(8,128)}, u32[]{:S(2)}, u32[]{:S(2)}) collective-permute-start(f32[16,64,128]{2,1,0:T(8,128)} %multiply_add_fusion.1), channel_id=1, source_target_pairs={{0,32},{2,34},{4,36},{6,38},{8,40},{10,42},{12,44},{14,46},{16,48}... | collective-permute-start | bytes 1572872 | tf_op jit(solution)/shard_map/ppermute | solution.py:22
  133.0 128.0 %collective-permute-start.14 = (bf16[4,2048,128]{2,1,0:T(8,128)(2,1)}, bf16[4,2048,128]{2,1,0:T(8,128)(2,1)}, u32[]{:S(2)}, u32[]{:S(2)}) collective-permute-start(bf16[4,2048,128]{2,1,0:T(8,128)(2,1)} %all-gather.2.cloned.1.call-done.k_ref.v_ref), channel_id=1, source_target_pairs={{0,32},{32,64},{64,96},{1,33},{33,65},{65,97},{2,34},{34,66},{66,9... | collective-permute-start | bytes 6291464 | tf_op jit(solution)/shard_map/ppermute | solution.py:22
  134.9 136.8 %collective-permute-start.13 = (bf16[4,2048,128]{2,1,0:T(8,128)(2,1)}, bf16[4,2048,128]{2,1,0:T(8,128)(2,1)}, u32[]{:S(2)}, u32[]{:S(2)}) collective-permute-start(bf16[4,2048,128]{2,1,0:T(8,128)(2,1)} %all-gather.2.cloned.1.call-done.k_ref.v_ref), channel_id=1, source_target_pairs={{0,64},{32,96},{1,65},{33,97},{2,66},{34,98},{3,67},{35,99},{4,68}... | collective-permute-start | bytes 6291464 | tf_op jit(solution)/shard_map/ppermute | solution.py:22
  136.2 146.3 %collective-permute-start.12 = (bf16[4,2048,128]{2,1,0:T(8,128)(2,1)}, bf16[4,2048,128]{2,1,0:T(8,128)(2,1)S(1)}, u32[]{:S(2)}, u32[]{:S(2)}) collective-permute-start(bf16[4,2048,128]{2,1,0:T(8,128)(2,1)} %all-gather.2.cloned.1.call-done.k_ref.v_ref), channel_id=1, source_target_pairs={{0,96},{1,97},{2,98},{3,99},{4,100},{5,101},{6,102},{7,103},{8,104... | collective-permute-start | bytes 6291464 | tf_op jit(solution)/shard_map/ppermute | solution.py:22
  137.7 9.1 %collective-permute-start.4 = (f32[16]{0:T(128)S(1)}, f32[16]{0:T(128)S(1)}, u32[]{:S(2)}, u32[]{:S(2)}) collective-permute-start(f32[16]{0:T(128)S(1)} %fusion.74), channel_id=1, source_target_pairs={{0,16},{2,18},{4,20},{6,22},{8,24},{10,26},{12,28},{14,30},{16,32}... | collective-permute-start | bytes 200 | tf_op jit(solution)/shard_map/ppermute | solution.py:22
  149.0 97.3 %collective-permute-start.11 = (f32[16,64,128]{2,1,0:T(8,128)}, f32[16,64,128]{2,1,0:T(8,128)}, u32[]{:S(2)}, u32[]{:S(2)}) collective-permute-start(f32[16,64,128]{2,1,0:T(8,128)} %multiply_add_fusion), channel_id=1, source_target_pairs={{0,64},{2,66},{4,68},{6,70},{8,72},{10,74},{12,76},{14,78},{16,80}... | collective-permute-start | bytes 1572872 | tf_op jit(solution)/shard_map/ppermute | solution.py:22
  153.7 35.6 %collective-permute-start.5 = (f32[16]{0:T(128)S(1)}, f32[16]{0:T(128)S(1)}, u32[]{:S(2)}, u32[]{:S(2)}) collective-permute-start(f32[16]{0:T(128)S(1)} %fusion.72), channel_id=1, source_target_pairs={{0,32},{2,34},{4,36},{6,38},{8,40},{10,42},{12,44},{14,46},{16,48}... | collective-permute-start | bytes 200 | tf_op jit(solution)/shard_map/ppermute | solution.py:22
  282.5 1.3 copy-start.1
  293.3 2.7 collective-permute-start.15
Sparse Core Ops, SparseCore 0:
  14.1 101.7 all-gather.1

commit v3 on v1

--- a/solution.py
+++ b/solution.py
@@ -13,6 +13,7 @@
 
 
 EPSILON = 1e-05
+CTX = ("cx", "cz", "cy")
 
 
 def shifted_up(value, axis, distance):
@@ -167,7 +168,9 @@
         .reshape(kv_heads, group_size * row_count, head_width)
     )
     both = jnp.concatenate([keys, values], axis=1).transpose(1, 0, 2)
-    both_all = lax.all_gather(both, "ctx", axis=1, tiled=True)
+    both_all = both
+    for axis in reversed(CTX):
+        both_all = lax.all_gather(both_all, axis, axis=1, tiled=True)
     key_count = both_all.shape[1]
     key_block = math.gcd(key_count, 1024)
     rows = group_size * row_count
@@ -212,7 +215,7 @@
     tp_count = lax.axis_size("tp")
     row_count, q_heads, head_width = queries.shape
     kv_heads = keys.shape[1]
-    first_row = lax.axis_index("ctx") * row_count
+    first_row = lax.axis_index(CTX) * row_count
 
     q_share = q_heads // seg_count
     kv_share = kv_heads // seg_count
@@ -269,7 +272,7 @@
     log_decay, local_part, ending, span_decay = span_terms(
         normed, b_rows, c_rows, step_sizes, rate, skip
     )
-    _, state_in = exclusive_scan(span_decay, ending, "ctx")
+    _, state_in = exclusive_scan(span_decay, ending, CTX)
     mixed_out = local_part + span_inflow(log_decay, c_rows, state_in)
     power = jnp.mean(mixed_out * mixed_out, axis=2, keepdims=True)
     result = own_rows.reshape(row_count, heads_core, state_width) + gain[None] * mixed_out * lax.rsqrt(
@@ -286,11 +289,22 @@
 
 
 def solution(mesh):
+    ctx_count = mesh.shape["ctx"]
+    outer_count = 4 if ctx_count % 4 == 0 else 1
+    inner_count = 2 if (ctx_count // outer_count) % 2 == 0 else 1
+    devices = mesh.devices.reshape(
+        mesh.shape["segment"],
+        outer_count,
+        ctx_count // (outer_count * inner_count),
+        inner_count,
+        mesh.shape["tp"],
+    )
+    fine = jax.sharding.Mesh(devices, ("segment", "cx", "cz", "cy", "tp"))
     in_specs = (
-        P("ctx", "tp", None),
-        P("ctx", "tp", None),
-        P("ctx", "tp", None),
-        P("ctx", "tp"),
+        P(CTX, "tp", None),
+        P(CTX, "tp", None),
+        P(CTX, "tp", None),
+        P(CTX, "tp"),
         P(None, "tp", None),
         P(None, "tp", None),
         P(None, "tp"),
@@ -298,5 +312,5 @@
         P(None, "tp"),
         P(None, "tp", None),
     )
-    out_specs = P("segment", "ctx", "tp")
-    return jax.shard_map(body, mesh=mesh, in_specs=in_specs, out_specs=out_specs, check_vma=False)
+    out_specs = P("segment", CTX, "tp")
+    return jax.shard_map(body, mesh=fine, in_specs=in_specs, out_specs=out_specs, check_vma=False)

time: 235 us -> 248 us (1.055)
  the two profiles are of different devices: /device:TPU:231 before, /device:TPU:29 now
where the time goes in v3:
time: 248 us; the launch traced here: 247 us
  waiting for transfers between devices  128 us (52%)
  starting transfers between devices  48.1 us (19%)
  Pallas kernels  22.9 us (9%)
  between operations  13.9 us (6%)
  matrix products  10.7 us (4%)
  other arithmetic  9.25 us (4%)
  local copies, waits for them, and re-layouts  6.99 us (3%)
  blocking collectives  6.65 us (3%)
    ppermute x11, waiting for transfers between devices, shifted_up(): return lax.ppermute(value, axis, pairs)  83.4 us
    ppermute x11, starting transfers between devices, shifted_up(): return lax.ppermute(value, axis, pairs)  44.2 us
    all_gather x2, waiting for transfers between devices, attention_half(): both_all = lax.all_gather(both_all, axis, axis=1, tiled=True)  40.4 us
    pallas_call x1, Pallas kernels, attention_half(): pl.pallas_call(functools.partial(flash_kernel, row_count=row_count, key_b...  22.9 us
    add x5, other arithmetic, merge_states(): later[0][:, None, None] * earlier[1] + later[1]  6.82 us
    all_gather x1, blocking collectives, attention_half(): both_all = lax.all_gather(both_all, axis, axis=1, tiled=True)  6.65 us
  transfers between devices with their start and end apart: 15, of which 15 were waited for; matrix products, arithmetic and copies ran while one was open for 9% of the time, Pallas kernels for 0%

profile of v3, /device:TPU:29, one launch (start us, length us, event | category | flops | bytes accessed | tf_op | source)
XLA Modules:
  0.0 246.7 jit_solution(10518450902680785811)
XLA Ops:
  7.8 6.7 %all_gather.9 = bf16[4,256,128]{2,1,0:T(8,128)(2,1)} all-gather(bf16[4,128,128]{2,1,0:T(8,128)(2,1)S(1)} %maximum_bitcast_fusion.1), channel_id=1, replica_groups=mesh['segment'=2,'cx'=4,'cz'=8,'cy'=2,'tp'=2] {'cy'}, dimensions={1}, use_global_device_ids=true | all-gather | bytes 393216 | tf_op jit(solution)/shard_map/all_gather | solution.py:173
  14.6 40.3 %all-gather.3.cloned.1.call-done = bf16[4,2048,128]{2,1,0:T(8,128)(2,1)} async-done(((bf16[4,256,128]{2,1,0:T(8,128)(2,1)}), bf16[4,2048,128]{2,1,0:T(8,128)(2,1)}) %all-gather.3.cloned.1.call-update) | async-done | bytes 2097168 | tf_op jit(solution)/shard_map/all_gather | solution.py:173
  56.6 3.9 %fusion = f32[128,1024]{0,1:T(8,128)S(1)} fusion(bf16[128,2048]{1,0:T(8,128)(2,1)S(1)} %copy-done.1, bf16[1,2048,1024]{2,1,0:T(8,128)(2,1)} %param.14), kind=kOutput, calls=%fused_computation | convolution fusion | flops 536870912 | bytes 5242880 | tf_op jit(solution)/shard_map/dot_general | solution.py:236
  61.7 3.2 %collective-permute-done = f32[128,273]{0,1:T(8,128)S(1)} collective-permute-done((f32[128,273]{0,1:T(8,128)S(1)}, f32[128,273]{0,1:T(8,128)S(1)}, u32[]{:S(2)}, u32[]{:S(2)}) %collective-permute-start) | collective-permute-done | bytes 139808 | tf_op jit(solution)/shard_map/ppermute | solution.py:26
  66.2 3.4 %collective-permute-start.6 = (f32[16,64,128]{2,1,0:T(8,128)S(1)}, f32[16,64,128]{2,1,0:T(8,128)}, u32[]{:S(2)}, u32[]{:S(2)}) collective-permute-start(f32[16,64,128]{2,1,0:T(8,128)S(1)} %fusion.58), channel_id=1, source_target_pairs={{0,2},{2,4},{4,6},{6,8},{8,10},{10,12},{12,14},{14,16},{16,18},{18... | collective-permute-start | bytes 1572872 | tf_op jit(solution)/shard_map/ppermute | solution.py:22
  69.6 8.1 %collective-permute-done.6 = f32[16,64,128]{2,1,0:T(8,128)} collective-permute-done((f32[16,64,128]{2,1,0:T(8,128)S(1)}, f32[16,64,128]{2,1,0:T(8,128)}, u32[]{:S(2)}, u32[]{:S(2)}) %collective-permute-start.6) | collective-permute-done | bytes 524320 | tf_op jit(solution)/shard_map/ppermute | solution.py:22
  78.9 2.6 %collective-permute-start.7 = (f32[16,64,128]{2,1,0:T(8,128)S(1)}, f32[16,64,128]{2,1,0:T(8,128)S(1)}, u32[]{:S(2)}, u32[]{:S(2)}) collective-permute-start(f32[16,64,128]{2,1,0:T(8,128)S(1)} %multiply_add_fusion.4), channel_id=1, source_target_pairs={{0,4},{2,6},{4,8},{6,10},{8,12},{10,14},{12,16},{14,18},{16,20},{1... | collective-permute-start | bytes 1572872 | tf_op jit(solution)/shard_map/ppermute | solution.py:22
  81.5 4.8 %collective-permute-start.1 = (f32[16]{0:T(128)S(1)}, f32[16]{0:T(128)S(1)}, u32[]{:S(2)}, u32[]{:S(2)}) collective-permute-start(f32[16]{0:T(128)S(1)} %fusion.79), channel_id=1, source_target_pairs={{0,2},{2,4},{4,6},{6,8},{8,10},{10,12},{12,14},{14,16},{16,18},{18... | collective-permute-start | bytes 200 | tf_op jit(solution)/shard_map/ppermute | solution.py:22
  86.3 1.9 collective-permute-done.1
  88.2 3.1 %collective-permute-done.7 = f32[16,64,128]{2,1,0:T(8,128)S(1)} collective-permute-done((f32[16,64,128]{2,1,0:T(8,128)S(1)}, f32[16,64,128]{2,1,0:T(8,128)S(1)}, u32[]{:S(2)}, u32[]{:S(2)}) %collective-permute-start.7) | collective-permute-done | bytes 524320 | tf_op jit(solution)/shard_map/ppermute | solution.py:22
  93.2 1.9 collective-permute-start.8
  95.2 2.9 %collective-permute-start.2 = (f32[16]{0:T(128)S(1)}, f32[16]{0:T(128)S(1)}, u32[]{:S(2)}, u32[]{:S(2)}) collective-permute-start(f32[16]{0:T(128)S(1)} %get-tuple-element.11), channel_id=1, source_target_pairs={{0,4},{2,6},{4,8},{6,10},{8,12},{10,14},{12,16},{14,18},{16,20},{1... | collective-permute-start | bytes 200 | tf_op jit(solution)/shard_map/ppermute | solution.py:22
  98.1 13.5 %collective-permute-done.2 = f32[16]{0:T(128)S(1)} collective-permute-done((f32[16]{0:T(128)S(1)}, f32[16]{0:T(128)S(1)}, u32[]{:S(2)}, u32[]{:S(2)}) %collective-permute-start.2) | collective-permute-done | bytes 96 | tf_op jit(solution)/shard_map/ppermute | solution.py:22
  111.6 2.9 %collective-permute-done.8 = f32[16,64,128]{2,1,0:T(8,128)S(1)} collective-permute-done((f32[16,64,128]{2,1,0:T(8,128)S(1)}, f32[16,64,128]{2,1,0:T(8,128)S(1)}, u32[]{:S(2)}, u32[]{:S(2)}) %collective-permute-start.8) | collective-permute-done | bytes 524320 | tf_op jit(solution)/shard_map/ppermute | solution.py:22
  114.5 1.4 multiply_add_fusion.2
  115.9 5.4 %collective-permute-start.9 = (f32[16,64,128]{2,1,0:T(8,128)S(1)}, f32[16,64,128]{2,1,0:T(8,128)}, u32[]{:S(2)}, u32[]{:S(2)}) collective-permute-start(f32[16,64,128]{2,1,0:T(8,128)S(1)} %multiply_add_fusion.2), channel_id=1, source_target_pairs={{0,16},{2,18},{4,20},{6,22},{8,24},{10,26},{12,28},{14,30},{16,32}... | collective-permute-start | bytes 1572872 | tf_op jit(solution)/shard_map/ppermute | solution.py:22
  121.3 3.2 %collective-permute-start.3 = (f32[16]{0:T(128)S(1)}, f32[16]{0:T(128)S(1)}, u32[]{:S(2)}, u32[]{:S(2)}) collective-permute-start(f32[16]{0:T(128)S(1)} %fusion.76), channel_id=1, source_target_pairs={{0,8},{2,10},{4,12},{6,14},{8,16},{10,18},{12,20},{14,22},{16,24},... | collective-permute-start | bytes 200 | tf_op jit(solution)/shard_map/ppermute | solution.py:22
  124.5 5.2 %collective-permute-done.3 = f32[16]{0:T(128)S(1)} collective-permute-done((f32[16]{0:T(128)S(1)}, f32[16]{0:T(128)S(1)}, u32[]{:S(2)}, u32[]{:S(2)}) %collective-permute-start.3) | collective-permute-done | bytes 96 | tf_op jit(solution)/shard_map/ppermute | solution.py:22
  129.7 8.5 %collective-permute-done.9 = f32[16,64,128]{2,1,0:T(8,128)} collective-permute-done((f32[16,64,128]{2,1,0:T(8,128)S(1)}, f32[16,64,128]{2,1,0:T(8,128)}, u32[]{:S(2)}, u32[]{:S(2)}) %collective-permute-start.9) | collective-permute-done | bytes 524320 | tf_op jit(solution)/shard_map/ppermute | solution.py:22
  139.4 12.3 %collective-permute-start.10 = (f32[16,64,128]{2,1,0:T(8,128)S(1)}, f32[16,64,128]{2,1,0:T(8,128)}, u32[]{:S(2)}, u32[]{:S(2)}) collective-permute-start(f32[16,64,128]{2,1,0:T(8,128)S(1)} %multiply_add_fusion.1), channel_id=1, source_target_pairs={{0,32},{2,34},{4,36},{6,38},{8,40},{10,42},{12,44},{14,46},{16,48}... | collective-permute-start | bytes 1572872 | tf_op jit(solution)/shard_map/ppermute | solution.py:22
  152.1 3.8 %collective-permute-start.4 = (f32[16]{0:T(128)S(1)}, f32[16]{0:T(128)S(1)}, u32[]{:S(2)}, u32[]{:S(2)}) collective-permute-start(f32[16]{0:T(128)S(1)} %fusion.74), channel_id=1, source_target_pairs={{0,16},{2,18},{4,20},{6,22},{8,24},{10,26},{12,28},{14,30},{16,32}... | collective-permute-start | bytes 200 | tf_op jit(solution)/shard_map/ppermute | solution.py:22
  156.6 4.6 %collective-permute-done.4 = f32[16]{0:T(128)S(1)} collective-permute-done((f32[16]{0:T(128)S(1)}, f32[16]{0:T(128)S(1)}, u32[]{:S(2)}, u32[]{:S(2)}) %collective-permute-start.4) | collective-permute-done | bytes 96 | tf_op jit(solution)/shard_map/ppermute | solution.py:22
  161.2 14.2 %collective-permute-done.10 = f32[16,64,128]{2,1,0:T(8,128)} collective-permute-done((f32[16,64,128]{2,1,0:T(8,128)S(1)}, f32[16,64,128]{2,1,0:T(8,128)}, u32[]{:S(2)}, u32[]{:S(2)}) %collective-permute-start.10) | collective-permute-done | bytes 524320 | tf_op jit(solution)/shard_map/ppermute | solution.py:22
  175.4 1.9 multiply_add_fusion
  179.0 2.2 fusion.2
  181.2 2.6 %collective-permute-start.5 = (f32[16]{0:T(128)S(1)}, f32[16]{0:T(128)S(1)}, u32[]{:S(2)}, u32[]{:S(2)}) collective-permute-start(f32[16]{0:T(128)S(1)} %fusion.72), channel_id=1, source_target_pairs={{0,32},{2,34},{4,36},{6,38},{8,40},{10,42},{12,44},{14,46},{16,48}... | collective-permute-start | bytes 200 | tf_op jit(solution)/shard_map/ppermute | solution.py:22
  183.9 4.0 %collective-permute-done.5 = f32[16]{0:T(128)S(1)} collective-permute-done((f32[16]{0:T(128)S(1)}, f32[16]{0:T(128)S(1)}, u32[]{:S(2)}, u32[]{:S(2)}) %collective-permute-start.5) | collective-permute-done | bytes 96 | tf_op jit(solution)/shard_map/ppermute | solution.py:22
  187.9 17.5 %collective-permute-done.11 = f32[16,64,128]{2,1,0:T(8,128)} collective-permute-done((f32[16,64,128]{2,1,0:T(8,128)}, f32[16,64,128]{2,1,0:T(8,128)}, u32[]{:S(2)}, u32[]{:S(2)}) %collective-permute-start.11) | collective-permute-done | bytes 524320 | tf_op jit(solution)/shard_map/ppermute | solution.py:22
  205.4 3.4 %fusion.12 = (f32[128,16]{0,1:T(8,128)S(1)}, f32[16,64,128]{2,1,0:T(8,128)}) fusion(f32[16,64,128]{2,1,0:T(8,128)S(1)} %fusion.2, f32[16]{0:T(128)S(1)} %fusion.67, f32[128,16]{0,1:T(8,128)S(1)} %copy.50, f32[128,1024]{0,1:T(8,128)S(1)} %get-tuple-element.14, f32[128,273]{0,1:T(8,128)S(1)} %fusion.56, f32[128]{0:T(128)S(1)} %fusion.70, ...), kind=kOutput, calls=%fused_computation.16 | convolution fusion | flops 204355584 | bytes 4804102 | tf_op jit(solution)/shard_map/tgn,gkpn->tgkp/dot_general | solution.py:70
  208.9 22.9 %shard_map.100 = bf16[2,512,128]{2,1,0:T(8,128)(2,1)} custom-call(s32[1]{0:T(128)} %bitcast.27.first_ref, bf16[2,512,128]{2,1,0:T(8,128)(2,1)} %bitcast.110, bf16[4,8192,128]{2,1,0:T(8,128)(2,1)} %all-gather.5.cloned.1.call-done.k_ref.v_ref, bf16[4,8192,128]{2,1,0:T(8,128)(2,1)} %all-gather.5.cloned.1.call-done.k_ref.v_ref), custom_call_target="tpu_custom_call" | custom-call | tf_op jit(solution)/shard_map/pallas_call | solution.py:184
  232.9 1.4 bitcast_select_fusion.1
  234.3 3.3 %collective-permute-start.12 = (bf16[128,1024]{0,1:T(8,128)(2,1)S(1)}, bf16[128,1024]{0,1:T(8,128)(2,1)S(1)}, u32[]{:S(2)}, u32[]{:S(2)}) collective-permute-start(bf16[128,1024]{0,1:T(8,128)(2,1)S(1)} %get-tuple-element.5), channel_id=1, source_target_pairs={{0,128},{128,0},{1,129},{129,1},{2,130},{130,2},{3,131},{131,3},{4... | collective-permute-start | bytes 786440 | tf_op jit(solution)/shard_map/ppermute | solution.py:26
  (78 shorter events, 15.9 us)
Async XLA Ops:
  6.5 145.5 %copy-start = (bf16[128,16,128]{2,1,0:T(8,128)(2,1)S(1)}, bf16[128,16,128]{2,1,0:T(8,128)(2,1)}, u32[]{:S(2)}) copy-start(bf16[128,16,128]{2,1,0:T(8,128)(2,1)} %param.10) | copy-start | bytes 1572868
  6.5 49.7 %copy-start.1 = (bf16[128,2048]{1,0:T(8,128)(2,1)S(1)}, bf16[128,2048]{1,0:T(8,128)(2,1)}, u32[]{:S(2)}) copy-start(bf16[128,2048]{1,0:T(8,128)(2,1)} %param.13) | copy-start | bytes 1572868
  6.5 49.7 %copy-start.6 = (bf16[1,2048,64]{1,2,0:T(8,128)(2,1)S(1)}, bf16[1,2048,64]{1,2,0:T(8,128)(2,1)}, u32[]{:S(2)}) copy-start(bf16[1,2048,64]{1,2,0:T(8,128)(2,1)} %param.15) | copy-start | bytes 786436
  6.5 48.3 %all-gather.3.cloned.1.call-start = ((), (), s32[]{:S(2)}) async-start(), calls=%async_computation | async-start | bytes 2359296 | tf_op jit(solution)/shard_map/all_gather | solution.py:173
  14.5 194.4 %all-gather.5.cloned.1.call-start = ((), (), s32[]{:S(2)}) async-start(), calls=%async_computation.1 | async-start | bytes 10485760 | tf_op jit(solution)/shard_map/all_gather | solution.py:173
  56.5 5.0 %copy-start.8 = (f32[1,32]{1,0:T(1,128)S(1)}, f32[1,32]{1,0:T(1,128)}, u32[]{:S(2)}) copy-start(f32[1,32]{1,0:T(1,128)} %param.16) | copy-start | bytes 388
  56.6 5.0 %copy-start.9 = (f32[1,32]{1,0:T(1,128)S(1)}, f32[1,32]{1,0:T(1,128)}, u32[]{:S(2)}) copy-start(f32[1,32]{1,0:T(1,128)} %param.17) | copy-start | bytes 388
  60.9 4.0 %collective-permute-start = (f32[128,273]{0,1:T(8,128)S(1)}, f32[128,273]{0,1:T(8,128)S(1)}, u32[]{:S(2)}, u32[]{:S(2)}) collective-permute-start(f32[128,273]{0,1:T(8,128)S(1)} %pad_maximum_fusion), channel_id=1, source_target_pairs={{0,1},{1,0},{2,3},{3,2},{4,5},{5,4},{6,7},{7,6},{8,9},{9,8},{10,11... | collective-permute-start | bytes 419336 | tf_op jit(solution)/shard_map/ppermute | solution.py:26
  61.6 59.6 %copy-start.7 = (f32[1,32,64]{2,1,0:T(8,128)S(1)}, f32[1,32,64]{2,1,0:T(8,128)}, u32[]{:S(2)}) copy-start(f32[1,32,64]{2,1,0:T(8,128)} %param.19) | copy-start | bytes 24580
  65.5 86.3 %copy-start.10 = (f32[1,32]{1,0:T(1,128)S(1)}, f32[1,32]{1,0:T(1,128)}, u32[]{:S(2)}) copy-start(f32[1,32]{1,0:T(1,128)} %param.18) | copy-start | bytes 388
  66.2 11.5 %collective-permute-start.6 = (f32[16,64,128]{2,1,0:T(8,128)S(1)}, f32[16,64,128]{2,1,0:T(8,128)}, u32[]{:S(2)}, u32[]{:S(2)}) collective-permute-start(f32[16,64,128]{2,1,0:T(8,128)S(1)} %fusion.58), channel_id=1, source_target_pairs={{0,2},{2,4},{4,6},{6,8},{8,10},{10,12},{12,14},{14,16},{16,18},{18... | collective-permute-start | bytes 1572872 | tf_op jit(solution)/shard_map/ppermute | solution.py:22
  78.9 12.3 %collective-permute-start.7 = (f32[16,64,128]{2,1,0:T(8,128)S(1)}, f32[16,64,128]{2,1,0:T(8,128)S(1)}, u32[]{:S(2)}, u32[]{:S(2)}) collective-permute-start(f32[16,64,128]{2,1,0:T(8,128)S(1)} %multiply_add_fusion.4), channel_id=1, source_target_pairs={{0,4},{2,6},{4,8},{6,10},{8,12},{10,14},{12,16},{14,18},{16,20},{1... | collective-permute-start | bytes 1572872 | tf_op jit(solution)/shard_map/ppermute | solution.py:22
  81.5 6.7 %collective-permute-start.1 = (f32[16]{0:T(128)S(1)}, f32[16]{0:T(128)S(1)}, u32[]{:S(2)}, u32[]{:S(2)}) collective-permute-start(f32[16]{0:T(128)S(1)} %fusion.79), channel_id=1, source_target_pairs={{0,2},{2,4},{4,6},{6,8},{8,10},{10,12},{12,14},{14,16},{16,18},{18... | collective-permute-start | bytes 200 | tf_op jit(solution)/shard_map/ppermute | solution.py:22
  91.3 0.8 copy-start.3
  93.2 18.4 %copy-start.2 = (f32[16,64,128]{2,1,0:T(8,128)}, f32[16,64,128]{2,1,0:T(8,128)S(1)}, u32[]{:S(2)}) copy-start(f32[16,64,128]{2,1,0:T(8,128)S(1)} %multiply_add_fusion.3) | copy-start | bytes 1572868
  93.2 21.3 %collective-permute-start.8 = (f32[16,64,128]{2,1,0:T(8,128)S(1)}, f32[16,64,128]{2,1,0:T(8,128)S(1)}, u32[]{:S(2)}, u32[]{:S(2)}) collective-permute-start(f32[16,64,128]{2,1,0:T(8,128)S(1)} %multiply_add_fusion.3), channel_id=1, source_target_pairs={{0,8},{2,10},{4,12},{6,14},{8,16},{10,18},{12,20},{14,22},{16,24},... | collective-permute-start | bytes 1572872 | tf_op jit(solution)/shard_map/ppermute | solution.py:22
  95.2 16.5 %collective-permute-start.2 = (f32[16]{0:T(128)S(1)}, f32[16]{0:T(128)S(1)}, u32[]{:S(2)}, u32[]{:S(2)}) collective-permute-start(f32[16]{0:T(128)S(1)} %get-tuple-element.11), channel_id=1, source_target_pairs={{0,4},{2,6},{4,8},{6,10},{8,12},{10,14},{12,16},{14,18},{16,20},{1... | collective-permute-start | bytes 200 | tf_op jit(solution)/shard_map/ppermute | solution.py:22
  114.5 15.2 %copy-start.4 = (f32[16,64,128]{2,1,0:T(8,128)}, f32[16,64,128]{2,1,0:T(8,128)S(1)}, u32[]{:S(2)}) copy-start(f32[16,64,128]{2,1,0:T(8,128)S(1)} %collective-permute-done.8) | copy-start | bytes 1572868
  115.9 22.4 %collective-permute-start.9 = (f32[16,64,128]{2,1,0:T(8,128)S(1)}, f32[16,64,128]{2,1,0:T(8,128)}, u32[]{:S(2)}, u32[]{:S(2)}) collective-permute-start(f32[16,64,128]{2,1,0:T(8,128)S(1)} %multiply_add_fusion.2), channel_id=1, source_target_pairs={{0,16},{2,18},{4,20},{6,22},{8,24},{10,26},{12,28},{14,30},{16,32}... | collective-permute-start | bytes 1572872 | tf_op jit(solution)/shard_map/ppermute | solution.py:22
  121.3 8.5 %collective-permute-start.3 = (f32[16]{0:T(128)S(1)}, f32[16]{0:T(128)S(1)}, u32[]{:S(2)}, u32[]{:S(2)}) collective-permute-start(f32[16]{0:T(128)S(1)} %fusion.76), channel_id=1, source_target_pairs={{0,8},{2,10},{4,12},{6,14},{8,16},{10,18},{12,20},{14,22},{16,24},... | collective-permute-start | bytes 200 | tf_op jit(solution)/shard_map/ppermute | solution.py:22
  139.4 66.0 %copy-start.5 = (f32[16,64,128]{2,1,0:T(8,128)S(1)}, f32[16,64,128]{2,1,0:T(8,128)}, u32[]{:S(2)}) copy-start(f32[16,64,128]{2,1,0:T(8,128)} %copy-done.4) | copy-start | bytes 1572868
  139.4 36.0 %collective-permute-start.10 = (f32[16,64,128]{2,1,0:T(8,128)S(1)}, f32[16,64,128]{2,1,0:T(8,128)}, u32[]{:S(2)}, u32[]{:S(2)}) collective-permute-start(f32[16,64,128]{2,1,0:T(8,128)S(1)} %multiply_add_fusion.1), channel_id=1, source_target_pairs={{0,32},{2,34},{4,36},{6,38},{8,40},{10,42},{12,44},{14,46},{16,48}... | collective-permute-start | bytes 1572872 | tf_op jit(solution)/shard_map/ppermute | solution.py:22
  152.1 9.1 %collective-permute-start.4 = (f32[16]{0:T(128)S(1)}, f32[16]{0:T(128)S(1)}, u32[]{:S(2)}, u32[]{:S(2)}) collective-permute-start(f32[16]{0:T(128)S(1)} %fusion.74), channel_id=1, source_target_pairs={{0,16},{2,18},{4,20},{6,22},{8,24},{10,26},{12,28},{14,30},{16,32}... | collective-permute-start | bytes 200 | tf_op jit(solution)/shard_map/ppermute | solution.py:22
  177.3 28.1 %collective-permute-start.11 = (f32[16,64,128]{2,1,0:T(8,128)}, f32[16,64,128]{2,1,0:T(8,128)}, u32[]{:S(2)}, u32[]{:S(2)}) collective-permute-start(f32[16,64,128]{2,1,0:T(8,128)} %multiply_add_fusion), channel_id=1, source_target_pairs={{0,64},{2,66},{4,68},{6,70},{8,72},{10,74},{12,76},{14,78},{16,80}... | collective-permute-start | bytes 1572872 | tf_op jit(solution)/shard_map/ppermute | solution.py:22
  181.2 6.7 %collective-permute-start.5 = (f32[16]{0:T(128)S(1)}, f32[16]{0:T(128)S(1)}, u32[]{:S(2)}, u32[]{:S(2)}) collective-permute-start(f32[16]{0:T(128)S(1)} %fusion.72), channel_id=1, source_target_pairs={{0,32},{2,34},{4,36},{6,38},{8,40},{10,42},{12,44},{14,46},{16,48}... | collective-permute-start | bytes 200 | tf_op jit(solution)/shard_map/ppermute | solution.py:22
  234.3 4.4 %collective-permute-start.12 = (bf16[128,1024]{0,1:T(8,128)(2,1)S(1)}, bf16[128,1024]{0,1:T(8,128)(2,1)S(1)}, u32[]{:S(2)}, u32[]{:S(2)}) collective-permute-start(bf16[128,1024]{0,1:T(8,128)(2,1)S(1)} %get-tuple-element.5), channel_id=1, source_target_pairs={{0,128},{128,0},{1,129},{129,1},{2,130},{130,2},{3,131},{131,3},{4... | collective-permute-start | bytes 786440 | tf_op jit(solution)/shard_map/ppermute | solution.py:26
Sparse Core Ops, SparseCore 0:
  14.6 40.1 all-gather.2
  56.7 152.1 all-gather.4

commit v4 on v1

--- a/solution.py
+++ b/solution.py
@@ -169,7 +169,7 @@
     both = jnp.concatenate([keys, values], axis=1).transpose(1, 0, 2)
     both_all = lax.all_gather(both, "ctx", axis=1, tiled=True)
     key_count = both_all.shape[1]
-    key_block = math.gcd(key_count, 1024)
+    key_block = math.gcd(key_count, 2048)
     rows = group_size * row_count
 
     def key_index(h, j, first_ref):
@@ -278,10 +278,10 @@
     state_part = result.reshape(row_count, heads_core * state_width).astype(jnp.bfloat16)
 
     keep_state = seg == 0
-    outgoing = jnp.where(keep_state, attended, state_part)
-    incoming = swapped(outgoing, "segment")
-    first = jnp.where(keep_state, state_part, incoming)
-    second = jnp.where(keep_state, incoming, attended)
+    state_in_half = lax.ppermute(state_part, "segment", [(1, 0)])
+    attended_in_half = lax.ppermute(attended, "segment", [(0, 1)])
+    first = jnp.where(keep_state, state_part, attended_in_half)
+    second = jnp.where(keep_state, state_in_half, attended)
     return jnp.concatenate([first, second], axis=1)[None]
 
 

time: 235 us -> 230 us (0.979); the launches traced: 234 us -> 225 us
  Pallas kernels: 33.2 us -> 21 us
  starting transfers between devices: 21.4 us -> 24.5 us
    pallas_call x1, Pallas kernels: 33.2 us -> 21 us  [attention_half(): pl.pallas_call(functools.partial(flash_kernel, row_count=row_count, key_b...]
    all_gather x1, waiting for transfers between devices: 24 us -> 32.5 us  [attention_half(): both_all = lax.all_gather(both, 'ctx', axis=1, tiled=True)]
    ppermute x11, waiting for transfers between devices: 108 us -> 100 us  [shifted_up(): return lax.ppermute(value, axis, pairs)]
    ppermute x0 -> x2, starting transfers between devices: none -> 4.62 us  [the longest x1 3.2 us: body(): state_in_half = lax.ppermute(state_part, 'segment', [(1, 0)])]
  transfers between devices with their start and end apart: 14 -> 15, of which waited for: 14 -> 13; matrix products, arithmetic and copies ran while one was open for 10% -> 11% of each run, Pallas kernels for 0% -> 9%
where the time goes in v4:
time: 230 us; the launch traced here: 225 us
  waiting for transfers between devices  137 us (60%)
  starting transfers between devices  24.5 us (11%)
  Pallas kernels  21 us (9%)
  between operations  13.9 us (6%)
  matrix products  12 us (5%)
  local copies, waits for them, and re-layouts  8.75 us (4%)
  other arithmetic  8.33 us (4%)
    ppermute x11, waiting for transfers between devices, shifted_up(): return lax.ppermute(value, axis, pairs)  100 us
    all_gather x1, waiting for transfers between devices, attention_half(): both_all = lax.all_gather(both, 'ctx', axis=1, tiled=True)  32.5 us
    pallas_call x1, Pallas kernels, attention_half(): pl.pallas_call(functools.partial(flash_kernel, row_count=row_count, key_b...  21 us
    ppermute x11, starting transfers between devices, shifted_up(): return lax.ppermute(value, axis, pairs)  18.5 us
    add x5, other arithmetic, merge_states(): later[0][:, None, None] * earlier[1] + later[1]  5.77 us
  transfers between devices with their start and end apart: 15, of which 13 were waited for; matrix products, arithmetic and copies ran while one was open for 11% of the time, Pallas kernels for 9%

profile of v4, /device:TPU:231, one launch (start us, length us, event | category | flops | bytes accessed | tf_op | source)
XLA Modules:
  0.0 225.4 jit_solution(1646141869862308513)
XLA Ops:
  8.5 1.3 copy.42
  9.8 1.4 fusion.42
  11.2 4.1 %fusion = f32[128,1024]{0,1:T(8,128)S(1)} fusion(bf16[128,2048]{1,0:T(8,128)(2,1)} %param.13, bf16[1,2048,1024]{2,1,0:T(8,128)(2,1)} %param.14), kind=kOutput, calls=%fused_computation | convolution fusion | flops 536870912 | bytes 5242880 | tf_op jit(solution)/shard_map/dot_general | solution.py:233
  15.7 1.4 collective-permute-start
  17.2 3.2 %collective-permute-done = f32[128,273]{0,1:T(8,128)S(1)} collective-permute-done((f32[128,273]{0,1:T(8,128)S(1)}, f32[128,273]{0,1:T(8,128)S(1)}, u32[]{:S(2)}, u32[]{:S(2)}) %collective-permute-start) | collective-permute-done | bytes 139808 | tf_op jit(solution)/shard_map/ppermute | solution.py:25
  21.7 4.8 %collective-permute-start.6 = (f32[16,64,128]{2,1,0:T(8,128)S(1)}, f32[16,64,128]{2,1,0:T(8,128)}, u32[]{:S(2)}, u32[]{:S(2)}) collective-permute-start(f32[16,64,128]{2,1,0:T(8,128)S(1)} %fusion.58), channel_id=1, source_target_pairs={{0,2},{2,4},{4,6},{6,8},{8,10},{10,12},{12,14},{14,16},{16,18},{18... | collective-permute-start | bytes 1572872 | tf_op jit(solution)/shard_map/ppermute | solution.py:21
  26.5 13.7 %collective-permute-done.6 = f32[16,64,128]{2,1,0:T(8,128)} collective-permute-done((f32[16,64,128]{2,1,0:T(8,128)S(1)}, f32[16,64,128]{2,1,0:T(8,128)}, u32[]{:S(2)}, u32[]{:S(2)}) %collective-permute-start.6) | collective-permute-done | bytes 524320 | tf_op jit(solution)/shard_map/ppermute | solution.py:21
  41.4 1.3 collective-permute-start.7
  42.7 1.9 collective-permute-start.1
  44.6 9.9 %collective-permute-done.1 = f32[16]{0:T(128)S(1)} collective-permute-done((f32[16]{0:T(128)S(1)}, f32[16]{0:T(128)S(1)}, u32[]{:S(2)}, u32[]{:S(2)}) %collective-permute-start.1) | collective-permute-done | bytes 96 | tf_op jit(solution)/shard_map/ppermute | solution.py:21
  54.5 1.4 collective-permute-done.7
  57.9 1.3 collective-permute-start.8
  59.2 1.3 collective-permute-start.2
  60.5 3.1 %collective-permute-done.2 = f32[16]{0:T(128)S(1)} collective-permute-done((f32[16]{0:T(128)S(1)}, f32[16]{0:T(128)S(1)}, u32[]{:S(2)}, u32[]{:S(2)}) %collective-permute-start.2) | collective-permute-done | bytes 96 | tf_op jit(solution)/shard_map/ppermute | solution.py:21
  63.6 24.6 %collective-permute-done.8 = f32[16,64,128]{2,1,0:T(8,128)S(1)} collective-permute-done((f32[16,64,128]{2,1,0:T(8,128)S(1)}, f32[16,64,128]{2,1,0:T(8,128)S(1)}, u32[]{:S(2)}, u32[]{:S(2)}) %collective-permute-start.8) | collective-permute-done | bytes 524320 | tf_op jit(solution)/shard_map/ppermute | solution.py:21
  88.2 1.3 multiply_add_fusion.2
  89.6 1.3 collective-permute-start.9
  90.9 1.3 collective-permute-start.3
  93.0 5.7 %collective-permute-done.3 = f32[16]{0:T(128)S(1)} collective-permute-done((f32[16]{0:T(128)S(1)}, f32[16]{0:T(128)S(1)}, u32[]{:S(2)}, u32[]{:S(2)}) %collective-permute-start.3) | collective-permute-done | bytes 96 | tf_op jit(solution)/shard_map/ppermute | solution.py:21
  98.7 7.8 %collective-permute-done.9 = f32[16,64,128]{2,1,0:T(8,128)} collective-permute-done((f32[16,64,128]{2,1,0:T(8,128)S(1)}, f32[16,64,128]{2,1,0:T(8,128)}, u32[]{:S(2)}, u32[]{:S(2)}) %collective-permute-start.9) | collective-permute-done | bytes 524320 | tf_op jit(solution)/shard_map/ppermute | solution.py:21
  107.7 1.3 collective-permute-start.10
  109.9 1.3 collective-permute-start.4
  111.8 14.9 %collective-permute-done.4 = f32[16]{0:T(128)S(1)} collective-permute-done((f32[16]{0:T(128)S(1)}, f32[16]{0:T(128)S(1)}, u32[]{:S(2)}, u32[]{:S(2)}) %collective-permute-start.4) | collective-permute-done | bytes 96 | tf_op jit(solution)/shard_map/ppermute | solution.py:21
  126.8 15.6 %collective-permute-done.10 = f32[16,64,128]{2,1,0:T(8,128)S(1)} collective-permute-done((f32[16,64,128]{2,1,0:T(8,128)S(1)}, f32[16,64,128]{2,1,0:T(8,128)S(1)}, u32[]{:S(2)}, u32[]{:S(2)}) %collective-permute-start.10) | collective-permute-done | bytes 524320 | tf_op jit(solution)/shard_map/ppermute | solution.py:21
  145.0 3.0 %fusion.2 = f32[16,64,128]{2,1,0:T(8,128)} fusion(f32[128,16,64]{0,2,1:T(8,128)S(1)} %bitcast.106, f32[16,128]{1,0:T(8,128)S(1)} %get-tuple-element.19, f32[128,128]{1,0:T(8,128)S(1)} %convolution_multiply_fusion, f32[16,128]{1,0:T(8,128)S(1)} %copy.48, pred[128,128]{1,0:T(8,128)(4,1)S(1)} %iota_compare_fusion), kind=kOutput, calls=%fused_computation.3 | convolution fusion | flops 202637312 | bytes 1146880 | tf_op jit(solution)/shard_map/gkts,sgkp->tgkp/dot_general | solution.py:46
  148.0 1.5 collective-permute-start.5
  150.2 3.2 %collective-permute-done.5 = f32[16]{0:T(128)S(1)} collective-permute-done((f32[16]{0:T(128)S(1)}, f32[16]{0:T(128)S(1)}, u32[]{:S(2)}, u32[]{:S(2)}) %collective-permute-start.5) | collective-permute-done | bytes 96 | tf_op jit(solution)/shard_map/ppermute | solution.py:21
  153.9 32.5 %all-gather.2.cloned.1.call-done.k_ref.v_ref = bf16[4,8192,128]{2,1,0:T(8,128)(2,1)} async-done(((bf16[4,128,128]{2,1,0:T(8,128)(2,1)}), bf16[4,8192,128]{2,1,0:T(8,128)(2,1)}) %all-gather.2.cloned.1.call-update) | async-done | bytes 8388624 | tf_op jit(solution)/shard_map/all_gather | solution.py:170
  186.4 21.0 %shard_map.100 = bf16[2,512,128]{2,1,0:T(8,128)(2,1)} custom-call(s32[1]{0:T(128)} %bitcast.27.first_ref, bf16[2,512,128]{2,1,0:T(8,128)(2,1)} %bitcast.109, bf16[4,8192,128]{2,1,0:T(8,128)(2,1)} %all-gather.2.cloned.1.call-done.k_ref.v_ref, bf16[4,8192,128]{2,1,0:T(8,128)(2,1)} %all-gather.2.cloned.1.call-done.k_ref.v_ref), custom_call_target="tpu_custom_call" | custom-call | tf_op jit(solution)/shard_map/pallas_call | solution.py:181
  208.6 1.4 collective-permute-start.12
  210.1 2.6 %fusion.12 = (f32[128,16]{0,1:T(8,128)S(1)}, f32[16,64,128]{2,1,0:T(8,128)S(1)}) fusion(f32[16,64,128]{2,1,0:T(8,128)} %fusion.2, f32[16]{0:T(128)} %copy-done.13, f32[128,16]{0,1:T(8,128)} %copy.50, f32[128,1024]{0,1:T(8,128)S(1)} %get-tuple-element.14, f32[128,273]{0,1:T(8,128)S(1)} %fusion.56, f32[128]{0:T(128)S(1)} %fusion.70, ...), kind=kOutput, calls=%fused_computation.16 | convolution fusion | flops 204355584 | bytes 4801414 | tf_op jit(solution)/shard_map/tgn,gkpn->tgkp/dot_general | solution.py:69
  213.1 3.2 %collective-permute-start.13 = (bf16[128,1024]{0,1:T(8,128)(2,1)S(1)}, bf16[128,1024]{0,1:T(8,128)(2,1)S(1)}, u32[]{:S(2)}, u32[]{:S(2)}) collective-permute-start(bf16[128,1024]{0,1:T(8,128)(2,1)S(1)} %get-tuple-element.6), channel_id=1, source_target_pairs={{128,0},{129,1},{130,2},{131,3},{132,4},{133,5},{134,6},{135,7},{1... | collective-permute-start | bytes 786440 | tf_op jit(solution)/shard_map/ppermute | solution.py:281
  (88 shorter events, 17.7 us)
Async XLA Ops:
  6.5 84.4 %copy-start = (bf16[128,16,128]{2,1,0:T(8,128)(2,1)S(1)}, bf16[128,16,128]{2,1,0:T(8,128)(2,1)}, u32[]{:S(2)}) copy-start(bf16[128,16,128]{2,1,0:T(8,128)(2,1)} %param.10) | copy-start | bytes 1572868
  6.5 179.9 %all-gather.2.cloned.1.call-start = ((), (), s32[]{:S(2)}) async-start(), calls=%async_computation | async-start | bytes 8519680 | tf_op jit(solution)/shard_map/all_gather | solution.py:170
  11.2 5.9 %copy-start.14 = (f32[1,32]{1,0:T(1,128)S(1)}, f32[1,32]{1,0:T(1,128)}, u32[]{:S(2)}) copy-start(f32[1,32]{1,0:T(1,128)} %param.16) | copy-start | bytes 388
  11.2 5.9 %copy-start.15 = (f32[1,32]{1,0:T(1,128)S(1)}, f32[1,32]{1,0:T(1,128)}, u32[]{:S(2)}) copy-start(f32[1,32]{1,0:T(1,128)} %param.17) | copy-start | bytes 388
  15.7 4.7 %collective-permute-start = (f32[128,273]{0,1:T(8,128)S(1)}, f32[128,273]{0,1:T(8,128)S(1)}, u32[]{:S(2)}, u32[]{:S(2)}) collective-permute-start(f32[128,273]{0,1:T(8,128)S(1)} %pad_maximum_fusion), channel_id=1, source_target_pairs={{0,1},{1,0},{2,3},{3,2},{4,5},{5,4},{6,7},{7,6},{8,9},{9,8},{10,11... | collective-permute-start | bytes 419336 | tf_op jit(solution)/shard_map/ppermute | solution.py:25
  21.1 88.0 %copy-start.16 = (f32[1,32]{1,0:T(1,128)S(1)}, f32[1,32]{1,0:T(1,128)}, u32[]{:S(2)}) copy-start(f32[1,32]{1,0:T(1,128)} %param.18) | copy-start | bytes 388
  21.1 88.8 %copy-start.12 = (f32[1,32,64]{2,1,0:T(8,128)S(1)}, f32[1,32,64]{2,1,0:T(8,128)}, u32[]{:S(2)}) copy-start(f32[1,32,64]{2,1,0:T(8,128)} %param.19) | copy-start | bytes 24580
  21.7 18.5 %collective-permute-start.6 = (f32[16,64,128]{2,1,0:T(8,128)S(1)}, f32[16,64,128]{2,1,0:T(8,128)}, u32[]{:S(2)}, u32[]{:S(2)}) collective-permute-start(f32[16,64,128]{2,1,0:T(8,128)S(1)} %fusion.58), channel_id=1, source_target_pairs={{0,2},{2,4},{4,6},{6,8},{8,10},{10,12},{12,14},{14,16},{16,18},{18... | collective-permute-start | bytes 1572872 | tf_op jit(solution)/shard_map/ppermute | solution.py:21
  41.4 14.6 %collective-permute-start.7 = (f32[16,64,128]{2,1,0:T(8,128)S(1)}, f32[16,64,128]{2,1,0:T(8,128)S(1)}, u32[]{:S(2)}, u32[]{:S(2)}) collective-permute-start(f32[16,64,128]{2,1,0:T(8,128)S(1)} %multiply_add_fusion.4), channel_id=1, source_target_pairs={{0,4},{2,6},{4,8},{6,10},{8,12},{10,14},{12,16},{14,18},{16,20},{1... | collective-permute-start | bytes 1572872 | tf_op jit(solution)/shard_map/ppermute | solution.py:21
  42.7 11.9 %collective-permute-start.1 = (f32[16]{0:T(128)S(1)}, f32[16]{0:T(128)S(1)}, u32[]{:S(2)}, u32[]{:S(2)}) collective-permute-start(f32[16]{0:T(128)S(1)} %fusion.79), channel_id=1, source_target_pairs={{0,2},{2,4},{4,6},{6,8},{8,10},{10,12},{12,14},{14,16},{16,18},{18... | collective-permute-start | bytes 200 | tf_op jit(solution)/shard_map/ppermute | solution.py:21
  54.5 152.9 %copy-start.11 = (f32[16]{0:T(128)}, f32[16]{0:T(128)S(1)}, u32[]{:S(2)}) copy-start(f32[16]{0:T(128)S(1)} %get-tuple-element.12) | copy-start | bytes 196
  56.0 0.8 copy-start.2
  57.9 5.7 %copy-start.1 = (f32[16,64,128]{2,1,0:T(8,128)}, f32[16,64,128]{2,1,0:T(8,128)S(1)}, u32[]{:S(2)}) copy-start(f32[16,64,128]{2,1,0:T(8,128)S(1)} %multiply_add_fusion.3) | copy-start | bytes 1572868
  57.9 30.3 %collective-permute-start.8 = (f32[16,64,128]{2,1,0:T(8,128)S(1)}, f32[16,64,128]{2,1,0:T(8,128)S(1)}, u32[]{:S(2)}, u32[]{:S(2)}) collective-permute-start(f32[16,64,128]{2,1,0:T(8,128)S(1)} %multiply_add_fusion.3), channel_id=1, source_target_pairs={{0,8},{2,10},{4,12},{6,14},{8,16},{10,18},{12,20},{14,22},{16,24},... | collective-permute-start | bytes 1572872 | tf_op jit(solution)/shard_map/ppermute | solution.py:21
  59.2 4.4 %collective-permute-start.2 = (f32[16]{0:T(128)S(1)}, f32[16]{0:T(128)S(1)}, u32[]{:S(2)}, u32[]{:S(2)}) collective-permute-start(f32[16]{0:T(128)S(1)} %get-tuple-element.11), channel_id=1, source_target_pairs={{0,4},{2,6},{4,8},{6,10},{8,12},{10,14},{12,16},{14,18},{16,20},{1... | collective-permute-start | bytes 200 | tf_op jit(solution)/shard_map/ppermute | solution.py:21
  88.2 10.5 %copy-start.4 = (f32[16,64,128]{2,1,0:T(8,128)}, f32[16,64,128]{2,1,0:T(8,128)S(1)}, u32[]{:S(2)}) copy-start(f32[16,64,128]{2,1,0:T(8,128)S(1)} %collective-permute-done.8) | copy-start | bytes 1572868
  89.6 17.0 %collective-permute-start.9 = (f32[16,64,128]{2,1,0:T(8,128)S(1)}, f32[16,64,128]{2,1,0:T(8,128)}, u32[]{:S(2)}, u32[]{:S(2)}) collective-permute-start(f32[16,64,128]{2,1,0:T(8,128)S(1)} %multiply_add_fusion.2), channel_id=1, source_target_pairs={{0,16},{2,18},{4,20},{6,22},{8,24},{10,26},{12,28},{14,30},{16,32}... | collective-permute-start | bytes 1572872 | tf_op jit(solution)/shard_map/ppermute | solution.py:21
  90.9 7.8 %collective-permute-start.3 = (f32[16]{0:T(128)S(1)}, f32[16]{0:T(128)S(1)}, u32[]{:S(2)}, u32[]{:S(2)}) collective-permute-start(f32[16]{0:T(128)S(1)} %fusion.76), channel_id=1, source_target_pairs={{0,8},{2,10},{4,12},{6,14},{8,16},{10,18},{12,20},{14,22},{16,24},... | collective-permute-start | bytes 200 | tf_op jit(solution)/shard_map/ppermute | solution.py:21
  107.7 34.7 %collective-permute-start.10 = (f32[16,64,128]{2,1,0:T(8,128)S(1)}, f32[16,64,128]{2,1,0:T(8,128)S(1)}, u32[]{:S(2)}, u32[]{:S(2)}) collective-permute-start(f32[16,64,128]{2,1,0:T(8,128)S(1)} %multiply_add_fusion.1), channel_id=1, source_target_pairs={{0,32},{2,34},{4,36},{6,38},{8,40},{10,42},{12,44},{14,46},{16,48}... | collective-permute-start | bytes 1572872 | tf_op jit(solution)/shard_map/ppermute | solution.py:21
  109.1 2.7 %copy-start.13 = (f32[16]{0:T(128)}, f32[16]{0:T(128)S(1)}, u32[]{:S(2)}) copy-start(f32[16]{0:T(128)S(1)} %fusion.67) | copy-start | bytes 196
  109.9 16.9 %collective-permute-start.4 = (f32[16]{0:T(128)S(1)}, f32[16]{0:T(128)S(1)}, u32[]{:S(2)}, u32[]{:S(2)}) collective-permute-start(f32[16]{0:T(128)S(1)} %fusion.74), channel_id=1, source_target_pairs={{0,16},{2,18},{4,20},{6,22},{8,24},{10,26},{12,28},{14,30},{16,32}... | collective-permute-start | bytes 200 | tf_op jit(solution)/shard_map/ppermute | solution.py:21
  142.4 44.0 %copy-start.6 = (f32[16,64,128]{2,1,0:T(8,128)}, f32[16,64,128]{2,1,0:T(8,128)S(1)}, u32[]{:S(2)}) copy-start(f32[16,64,128]{2,1,0:T(8,128)S(1)} %collective-permute-done.10) | copy-start | bytes 1572868
  143.3 66.7 %collective-permute-start.11 = (f32[16,64,128]{2,1,0:T(8,128)}, f32[16,64,128]{2,1,0:T(8,128)}, u32[]{:S(2)}, u32[]{:S(2)}) collective-permute-start(f32[16,64,128]{2,1,0:T(8,128)} %multiply_add_fusion), channel_id=1, source_target_pairs={{0,64},{2,66},{4,68},{6,70},{8,72},{10,74},{12,76},{14,78},{16,80}... | collective-permute-start | bytes 1572872 | tf_op jit(solution)/shard_map/ppermute | solution.py:21
  148.0 5.3 %collective-permute-start.5 = (f32[16]{0:T(128)S(1)}, f32[16]{0:T(128)S(1)}, u32[]{:S(2)}, u32[]{:S(2)}) collective-permute-start(f32[16]{0:T(128)S(1)} %fusion.72), channel_id=1, source_target_pairs={{0,32},{2,34},{4,36},{6,38},{8,40},{10,42},{12,44},{14,46},{16,48}... | collective-permute-start | bytes 200 | tf_op jit(solution)/shard_map/ppermute | solution.py:21
  186.4 23.7 %copy-start.3 = (f32[16,64,128]{2,1,0:T(8,128)S(1)}, f32[16,64,128]{2,1,0:T(8,128)}, u32[]{:S(2)}) copy-start(f32[16,64,128]{2,1,0:T(8,128)} %copy-done.2) | copy-start | bytes 1572868
  186.4 23.7 %copy-start.5 = (f32[16,64,128]{2,1,0:T(8,128)S(1)}, f32[16,64,128]{2,1,0:T(8,128)}, u32[]{:S(2)}) copy-start(f32[16,64,128]{2,1,0:T(8,128)} %copy-done.4) | copy-start | bytes 1572868
  208.6 4.1 %copy-start.7 = (f32[16,64,128]{2,1,0:T(8,128)S(1)}, f32[16,64,128]{2,1,0:T(8,128)}, u32[]{:S(2)}) copy-start(f32[16,64,128]{2,1,0:T(8,128)} %fusion.2) | copy-start | bytes 1572868
  208.6 4.1 %copy-start.8 = (f32[128,16]{0,1:T(8,128)S(1)}, f32[128,16]{0,1:T(8,128)}, u32[]{:S(2)}) copy-start(f32[128,16]{0,1:T(8,128)} %copy.50) | copy-start | bytes 24580
  208.6 4.1 %copy-start.9 = (f32[1024]{0:T(1024)S(1)}, f32[1024]{0:T(1024)}, u32[]{:S(2)}) copy-start(f32[1024]{0:T(1024)} %mul.314) | copy-start | bytes 12292
  208.6 4.1 %copy-start.10 = (f32[1024]{0:T(1024)S(1)}, f32[1024]{0:T(1024)}, u32[]{:S(2)}) copy-start(f32[1024]{0:T(1024)} %mul.288) | copy-start | bytes 12292
  208.6 4.1 %collective-permute-start.12 = (bf16[128,1024]{0,1:T(8,128)(2,1)S(1)}, bf16[128,1024]{0,1:T(8,128)(2,1)S(1)}, u32[]{:S(2)}, u32[]{:S(2)}) collective-permute-start(bf16[128,1024]{0,1:T(8,128)(2,1)S(1)} %bitcast.111), channel_id=1, source_target_pairs={{0,128},{1,129},{2,130},{3,131},{4,132},{5,133},{6,134},{7,135},{8... | collective-permute-start | bytes 786440 | tf_op jit(solution)/shard_map/ppermute | solution.py:282
  213.1 4.3 %collective-permute-start.13 = (bf16[128,1024]{0,1:T(8,128)(2,1)S(1)}, bf16[128,1024]{0,1:T(8,128)(2,1)S(1)}, u32[]{:S(2)}, u32[]{:S(2)}) collective-permute-start(bf16[128,1024]{0,1:T(8,128)(2,1)S(1)} %get-tuple-element.6), channel_id=1, source_target_pairs={{128,0},{129,1},{130,2},{131,3},{132,4},{133,5},{134,6},{135,7},{1... | collective-permute-start | bytes 786440 | tf_op jit(solution)/shard_map/ppermute | solution.py:281
Sparse Core Ops, SparseCore 0:
  10.9 175.4 all-gather.1

commit v5 on v4

--- a/solution.py
+++ b/solution.py
@@ -169,7 +169,7 @@
     both = jnp.concatenate([keys, values], axis=1).transpose(1, 0, 2)
     both_all = lax.all_gather(both, "ctx", axis=1, tiled=True)
     key_count = both_all.shape[1]
-    key_block = math.gcd(key_count, 2048)
+    key_block = math.gcd(key_count, 4096)
     rows = group_size * row_count
 
     def key_index(h, j, first_ref):

time: 230 us -> 229 us (level)
  no operation moved by 1% of the time
where the time goes in v5:
time: 229 us; the launch traced here: 225 us
  waiting for transfers between devices  137 us (60%)
  starting transfers between devices  24.5 us (11%)
  Pallas kernels  20.3 us (9%)
  between operations  13.9 us (6%)
  matrix products  12 us (5%)
  local copies, waits for them, and re-layouts  8.75 us (4%)
  other arithmetic  8.33 us (4%)
    ppermute x11, waiting for transfers between devices, shifted_up(): return lax.ppermute(value, axis, pairs)  100 us
    all_gather x1, waiting for transfers between devices, attention_half(): both_all = lax.all_gather(both, 'ctx', axis=1, tiled=True)  32.5 us
    pallas_call x1, Pallas kernels, attention_half(): pl.pallas_call(functools.partial(flash_kernel, row_count=row_count, key_b...  20.3 us
    ppermute x11, starting transfers between devices, shifted_up(): return lax.ppermute(value, axis, pairs)  18.5 us
    add x5, other arithmetic, merge_states(): later[0][:, None, None] * earlier[1] + later[1]  5.77 us
  transfers between devices with their start and end apart: 15, of which 13 were waited for; matrix products, arithmetic and copies ran while one was open for 11% of the time, Pallas kernels for 9%

profile of v5, /device:TPU:231, one launch (start us, length us, event | category | flops | bytes accessed | tf_op | source)
XLA Modules:
  0.0 224.6 jit_solution(4305482337992902492)
XLA Ops:
  8.5 1.3 copy.42
  9.8 1.4 fusion.42
  11.2 4.1 %fusion = f32[128,1024]{0,1:T(8,128)S(1)} fusion(bf16[128,2048]{1,0:T(8,128)(2,1)} %param.13, bf16[1,2048,1024]{2,1,0:T(8,128)(2,1)} %param.14), kind=kOutput, calls=%fused_computation | convolution fusion | flops 536870912 | bytes 5242880 | tf_op jit(solution)/shard_map/dot_general | solution.py:233
  15.7 1.4 collective-permute-start
  17.2 3.2 %collective-permute-done = f32[128,273]{0,1:T(8,128)S(1)} collective-permute-done((f32[128,273]{0,1:T(8,128)S(1)}, f32[128,273]{0,1:T(8,128)S(1)}, u32[]{:S(2)}, u32[]{:S(2)}) %collective-permute-start) | collective-permute-done | bytes 139808 | tf_op jit(solution)/shard_map/ppermute | solution.py:25
  21.7 4.8 %collective-permute-start.6 = (f32[16,64,128]{2,1,0:T(8,128)S(1)}, f32[16,64,128]{2,1,0:T(8,128)}, u32[]{:S(2)}, u32[]{:S(2)}) collective-permute-start(f32[16,64,128]{2,1,0:T(8,128)S(1)} %fusion.58), channel_id=1, source_target_pairs={{0,2},{2,4},{4,6},{6,8},{8,10},{10,12},{12,14},{14,16},{16,18},{18... | collective-permute-start | bytes 1572872 | tf_op jit(solution)/shard_map/ppermute | solution.py:21
  26.5 13.7 %collective-permute-done.6 = f32[16,64,128]{2,1,0:T(8,128)} collective-permute-done((f32[16,64,128]{2,1,0:T(8,128)S(1)}, f32[16,64,128]{2,1,0:T(8,128)}, u32[]{:S(2)}, u32[]{:S(2)}) %collective-permute-start.6) | collective-permute-done | bytes 524320 | tf_op jit(solution)/shard_map/ppermute | solution.py:21
  41.4 1.3 collective-permute-start.7
  42.7 1.9 collective-permute-start.1
  44.6 9.9 %collective-permute-done.1 = f32[16]{0:T(128)S(1)} collective-permute-done((f32[16]{0:T(128)S(1)}, f32[16]{0:T(128)S(1)}, u32[]{:S(2)}, u32[]{:S(2)}) %collective-permute-start.1) | collective-permute-done | bytes 96 | tf_op jit(solution)/shard_map/ppermute | solution.py:21
  54.5 1.4 collective-permute-done.7
  57.9 1.3 collective-permute-start.8
  59.2 1.3 collective-permute-start.2
  60.5 3.1 %collective-permute-done.2 = f32[16]{0:T(128)S(1)} collective-permute-done((f32[16]{0:T(128)S(1)}, f32[16]{0:T(128)S(1)}, u32[]{:S(2)}, u32[]{:S(2)}) %collective-permute-start.2) | collective-permute-done | bytes 96 | tf_op jit(solution)/shard_map/ppermute | solution.py:21
  63.6 24.6 %collective-permute-done.8 = f32[16,64,128]{2,1,0:T(8,128)S(1)} collective-permute-done((f32[16,64,128]{2,1,0:T(8,128)S(1)}, f32[16,64,128]{2,1,0:T(8,128)S(1)}, u32[]{:S(2)}, u32[]{:S(2)}) %collective-permute-start.8) | collective-permute-done | bytes 524320 | tf_op jit(solution)/shard_map/ppermute | solution.py:21
  88.2 1.3 multiply_add_fusion.2
  89.6 1.3 collective-permute-start.9
  90.9 1.3 collective-permute-start.3
  93.0 5.7 %collective-permute-done.3 = f32[16]{0:T(128)S(1)} collective-permute-done((f32[16]{0:T(128)S(1)}, f32[16]{0:T(128)S(1)}, u32[]{:S(2)}, u32[]{:S(2)}) %collective-permute-start.3) | collective-permute-done | bytes 96 | tf_op jit(solution)/shard_map/ppermute | solution.py:21
  98.7 7.8 %collective-permute-done.9 = f32[16,64,128]{2,1,0:T(8,128)} collective-permute-done((f32[16,64,128]{2,1,0:T(8,128)S(1)}, f32[16,64,128]{2,1,0:T(8,128)}, u32[]{:S(2)}, u32[]{:S(2)}) %collective-permute-start.9) | collective-permute-done | bytes 524320 | tf_op jit(solution)/shard_map/ppermute | solution.py:21
  107.7 1.3 collective-permute-start.10
  109.9 1.3 collective-permute-start.4
  111.8 14.9 %collective-permute-done.4 = f32[16]{0:T(128)S(1)} collective-permute-done((f32[16]{0:T(128)S(1)}, f32[16]{0:T(128)S(1)}, u32[]{:S(2)}, u32[]{:S(2)}) %collective-permute-start.4) | collective-permute-done | bytes 96 | tf_op jit(solution)/shard_map/ppermute | solution.py:21
  126.8 15.6 %collective-permute-done.10 = f32[16,64,128]{2,1,0:T(8,128)S(1)} collective-permute-done((f32[16,64,128]{2,1,0:T(8,128)S(1)}, f32[16,64,128]{2,1,0:T(8,128)S(1)}, u32[]{:S(2)}, u32[]{:S(2)}) %collective-permute-start.10) | collective-permute-done | bytes 524320 | tf_op jit(solution)/shard_map/ppermute | solution.py:21
  145.0 3.0 %fusion.2 = f32[16,64,128]{2,1,0:T(8,128)} fusion(f32[128,16,64]{0,2,1:T(8,128)S(1)} %bitcast.106, f32[16,128]{1,0:T(8,128)S(1)} %get-tuple-element.19, f32[128,128]{1,0:T(8,128)S(1)} %convolution_multiply_fusion, f32[16,128]{1,0:T(8,128)S(1)} %copy.48, pred[128,128]{1,0:T(8,128)(4,1)S(1)} %iota_compare_fusion), kind=kOutput, calls=%fused_computation.3 | convolution fusion | flops 202637312 | bytes 1146880 | tf_op jit(solution)/shard_map/gkts,sgkp->tgkp/dot_general | solution.py:46
  148.0 1.5 collective-permute-start.5
  150.2 3.2 %collective-permute-done.5 = f32[16]{0:T(128)S(1)} collective-permute-done((f32[16]{0:T(128)S(1)}, f32[16]{0:T(128)S(1)}, u32[]{:S(2)}, u32[]{:S(2)}) %collective-permute-start.5) | collective-permute-done | bytes 96 | tf_op jit(solution)/shard_map/ppermute | solution.py:21
  153.9 32.5 %all-gather.2.cloned.1.call-done.k_ref.v_ref = bf16[4,8192,128]{2,1,0:T(8,128)(2,1)} async-done(((bf16[4,128,128]{2,1,0:T(8,128)(2,1)}), bf16[4,8192,128]{2,1,0:T(8,128)(2,1)}) %all-gather.2.cloned.1.call-update) | async-done | bytes 8388624 | tf_op jit(solution)/shard_map/all_gather | solution.py:170
  186.4 20.3 %shard_map.100 = bf16[2,512,128]{2,1,0:T(8,128)(2,1)} custom-call(s32[1]{0:T(128)} %bitcast.27.first_ref, bf16[2,512,128]{2,1,0:T(8,128)(2,1)} %bitcast.109, bf16[4,8192,128]{2,1,0:T(8,128)(2,1)} %all-gather.2.cloned.1.call-done.k_ref.v_ref, bf16[4,8192,128]{2,1,0:T(8,128)(2,1)} %all-gather.2.cloned.1.call-done.k_ref.v_ref), custom_call_target="tpu_custom_call" | custom-call | tf_op jit(solution)/shard_map/pallas_call | solution.py:181
  207.9 1.4 collective-permute-start.12
  209.3 2.6 %fusion.12 = (f32[128,16]{0,1:T(8,128)S(1)}, f32[16,64,128]{2,1,0:T(8,128)S(1)}) fusion(f32[16,64,128]{2,1,0:T(8,128)} %fusion.2, f32[16]{0:T(128)} %copy-done.13, f32[128,16]{0,1:T(8,128)} %copy.50, f32[128,1024]{0,1:T(8,128)S(1)} %get-tuple-element.14, f32[128,273]{0,1:T(8,128)S(1)} %fusion.56, f32[128]{0:T(128)S(1)} %fusion.70, ...), kind=kOutput, calls=%fused_computation.16 | convolution fusion | flops 204355584 | bytes 4801414 | tf_op jit(solution)/shard_map/tgn,gkpn->tgkp/dot_general | solution.py:69
  212.4 3.2 %collective-permute-start.13 = (bf16[128,1024]{0,1:T(8,128)(2,1)S(1)}, bf16[128,1024]{0,1:T(8,128)(2,1)S(1)}, u32[]{:S(2)}, u32[]{:S(2)}) collective-permute-start(bf16[128,1024]{0,1:T(8,128)(2,1)S(1)} %get-tuple-element.6), channel_id=1, source_target_pairs={{128,0},{129,1},{130,2},{131,3},{132,4},{133,5},{134,6},{135,7},{1... | collective-permute-start | bytes 786440 | tf_op jit(solution)/shard_map/ppermute | solution.py:281
  (88 shorter events, 17.7 us)
Async XLA Ops:
  6.5 84.4 %copy-start = (bf16[128,16,128]{2,1,0:T(8,128)(2,1)S(1)}, bf16[128,16,128]{2,1,0:T(8,128)(2,1)}, u32[]{:S(2)}) copy-start(bf16[128,16,128]{2,1,0:T(8,128)(2,1)} %param.10) | copy-start | bytes 1572868
  6.5 179.9 %all-gather.2.cloned.1.call-start = ((), (), s32[]{:S(2)}) async-start(), calls=%async_computation | async-start | bytes 8519680 | tf_op jit(solution)/shard_map/all_gather | solution.py:170
  11.2 5.9 %copy-start.14 = (f32[1,32]{1,0:T(1,128)S(1)}, f32[1,32]{1,0:T(1,128)}, u32[]{:S(2)}) copy-start(f32[1,32]{1,0:T(1,128)} %param.16) | copy-start | bytes 388
  11.2 5.9 %copy-start.15 = (f32[1,32]{1,0:T(1,128)S(1)}, f32[1,32]{1,0:T(1,128)}, u32[]{:S(2)}) copy-start(f32[1,32]{1,0:T(1,128)} %param.17) | copy-start | bytes 388
  15.7 4.7 %collective-permute-start = (f32[128,273]{0,1:T(8,128)S(1)}, f32[128,273]{0,1:T(8,128)S(1)}, u32[]{:S(2)}, u32[]{:S(2)}) collective-permute-start(f32[128,273]{0,1:T(8,128)S(1)} %pad_maximum_fusion), channel_id=1, source_target_pairs={{0,1},{1,0},{2,3},{3,2},{4,5},{5,4},{6,7},{7,6},{8,9},{9,8},{10,11... | collective-permute-start | bytes 419336 | tf_op jit(solution)/shard_map/ppermute | solution.py:25
  21.1 88.0 %copy-start.16 = (f32[1,32]{1,0:T(1,128)S(1)}, f32[1,32]{1,0:T(1,128)}, u32[]{:S(2)}) copy-start(f32[1,32]{1,0:T(1,128)} %param.18) | copy-start | bytes 388
  21.1 88.8 %copy-start.12 = (f32[1,32,64]{2,1,0:T(8,128)S(1)}, f32[1,32,64]{2,1,0:T(8,128)}, u32[]{:S(2)}) copy-start(f32[1,32,64]{2,1,0:T(8,128)} %param.19) | copy-start | bytes 24580
  21.7 18.5 %collective-permute-start.6 = (f32[16,64,128]{2,1,0:T(8,128)S(1)}, f32[16,64,128]{2,1,0:T(8,128)}, u32[]{:S(2)}, u32[]{:S(2)}) collective-permute-start(f32[16,64,128]{2,1,0:T(8,128)S(1)} %fusion.58), channel_id=1, source_target_pairs={{0,2},{2,4},{4,6},{6,8},{8,10},{10,12},{12,14},{14,16},{16,18},{18... | collective-permute-start | bytes 1572872 | tf_op jit(solution)/shard_map/ppermute | solution.py:21
  41.4 14.6 %collective-permute-start.7 = (f32[16,64,128]{2,1,0:T(8,128)S(1)}, f32[16,64,128]{2,1,0:T(8,128)S(1)}, u32[]{:S(2)}, u32[]{:S(2)}) collective-permute-start(f32[16,64,128]{2,1,0:T(8,128)S(1)} %multiply_add_fusion.4), channel_id=1, source_target_pairs={{0,4},{2,6},{4,8},{6,10},{8,12},{10,14},{12,16},{14,18},{16,20},{1... | collective-permute-start | bytes 1572872 | tf_op jit(solution)/shard_map/ppermute | solution.py:21
  42.7 11.9 %collective-permute-start.1 = (f32[16]{0:T(128)S(1)}, f32[16]{0:T(128)S(1)}, u32[]{:S(2)}, u32[]{:S(2)}) collective-permute-start(f32[16]{0:T(128)S(1)} %fusion.79), channel_id=1, source_target_pairs={{0,2},{2,4},{4,6},{6,8},{8,10},{10,12},{12,14},{14,16},{16,18},{18... | collective-permute-start | bytes 200 | tf_op jit(solution)/shard_map/ppermute | solution.py:21
  54.5 152.2 %copy-start.11 = (f32[16]{0:T(128)}, f32[16]{0:T(128)S(1)}, u32[]{:S(2)}) copy-start(f32[16]{0:T(128)S(1)} %get-tuple-element.12) | copy-start | bytes 196
  56.0 0.8 copy-start.2
  57.9 5.7 %copy-start.1 = (f32[16,64,128]{2,1,0:T(8,128)}, f32[16,64,128]{2,1,0:T(8,128)S(1)}, u32[]{:S(2)}) copy-start(f32[16,64,128]{2,1,0:T(8,128)S(1)} %multiply_add_fusion.3) | copy-start | bytes 1572868
  57.9 30.3 %collective-permute-start.8 = (f32[16,64,128]{2,1,0:T(8,128)S(1)}, f32[16,64,128]{2,1,0:T(8,128)S(1)}, u32[]{:S(2)}, u32[]{:S(2)}) collective-permute-start(f32[16,64,128]{2,1,0:T(8,128)S(1)} %multiply_add_fusion.3), channel_id=1, source_target_pairs={{0,8},{2,10},{4,12},{6,14},{8,16},{10,18},{12,20},{14,22},{16,24},... | collective-permute-start | bytes 1572872 | tf_op jit(solution)/shard_map/ppermute | solution.py:21
  59.2 4.4 %collective-permute-start.2 = (f32[16]{0:T(128)S(1)}, f32[16]{0:T(128)S(1)}, u32[]{:S(2)}, u32[]{:S(2)}) collective-permute-start(f32[16]{0:T(128)S(1)} %get-tuple-element.11), channel_id=1, source_target_pairs={{0,4},{2,6},{4,8},{6,10},{8,12},{10,14},{12,16},{14,18},{16,20},{1... | collective-permute-start | bytes 200 | tf_op jit(solution)/shard_map/ppermute | solution.py:21
  88.2 10.5 %copy-start.4 = (f32[16,64,128]{2,1,0:T(8,128)}, f32[16,64,128]{2,1,0:T(8,128)S(1)}, u32[]{:S(2)}) copy-start(f32[16,64,128]{2,1,0:T(8,128)S(1)} %collective-permute-done.8) | copy-start | bytes 1572868
  89.6 17.0 %collective-permute-start.9 = (f32[16,64,128]{2,1,0:T(8,128)S(1)}, f32[16,64,128]{2,1,0:T(8,128)}, u32[]{:S(2)}, u32[]{:S(2)}) collective-permute-start(f32[16,64,128]{2,1,0:T(8,128)S(1)} %multiply_add_fusion.2), channel_id=1, source_target_pairs={{0,16},{2,18},{4,20},{6,22},{8,24},{10,26},{12,28},{14,30},{16,32}... | collective-permute-start | bytes 1572872 | tf_op jit(solution)/shard_map/ppermute | solution.py:21
  90.9 7.8 %collective-permute-start.3 = (f32[16]{0:T(128)S(1)}, f32[16]{0:T(128)S(1)}, u32[]{:S(2)}, u32[]{:S(2)}) collective-permute-start(f32[16]{0:T(128)S(1)} %fusion.76), channel_id=1, source_target_pairs={{0,8},{2,10},{4,12},{6,14},{8,16},{10,18},{12,20},{14,22},{16,24},... | collective-permute-start | bytes 200 | tf_op jit(solution)/shard_map/ppermute | solution.py:21
  107.7 34.7 %collective-permute-start.10 = (f32[16,64,128]{2,1,0:T(8,128)S(1)}, f32[16,64,128]{2,1,0:T(8,128)S(1)}, u32[]{:S(2)}, u32[]{:S(2)}) collective-permute-start(f32[16,64,128]{2,1,0:T(8,128)S(1)} %multiply_add_fusion.1), channel_id=1, source_target_pairs={{0,32},{2,34},{4,36},{6,38},{8,40},{10,42},{12,44},{14,46},{16,48}... | collective-permute-start | bytes 1572872 | tf_op jit(solution)/shard_map/ppermute | solution.py:21
  109.1 2.7 %copy-start.13 = (f32[16]{0:T(128)}, f32[16]{0:T(128)S(1)}, u32[]{:S(2)}) copy-start(f32[16]{0:T(128)S(1)} %fusion.67) | copy-start | bytes 196
  109.9 16.9 %collective-permute-start.4 = (f32[16]{0:T(128)S(1)}, f32[16]{0:T(128)S(1)}, u32[]{:S(2)}, u32[]{:S(2)}) collective-permute-start(f32[16]{0:T(128)S(1)} %fusion.74), channel_id=1, source_target_pairs={{0,16},{2,18},{4,20},{6,22},{8,24},{10,26},{12,28},{14,30},{16,32}... | collective-permute-start | bytes 200 | tf_op jit(solution)/shard_map/ppermute | solution.py:21
  142.4 44.0 %copy-start.6 = (f32[16,64,128]{2,1,0:T(8,128)}, f32[16,64,128]{2,1,0:T(8,128)S(1)}, u32[]{:S(2)}) copy-start(f32[16,64,128]{2,1,0:T(8,128)S(1)} %collective-permute-done.10) | copy-start | bytes 1572868
  143.3 66.0 %collective-permute-start.11 = (f32[16,64,128]{2,1,0:T(8,128)}, f32[16,64,128]{2,1,0:T(8,128)}, u32[]{:S(2)}, u32[]{:S(2)}) collective-permute-start(f32[16,64,128]{2,1,0:T(8,128)} %multiply_add_fusion), channel_id=1, source_target_pairs={{0,64},{2,66},{4,68},{6,70},{8,72},{10,74},{12,76},{14,78},{16,80}... | collective-permute-start | bytes 1572872 | tf_op jit(solution)/shard_map/ppermute | solution.py:21
  148.0 5.3 %collective-permute-start.5 = (f32[16]{0:T(128)S(1)}, f32[16]{0:T(128)S(1)}, u32[]{:S(2)}, u32[]{:S(2)}) collective-permute-start(f32[16]{0:T(128)S(1)} %fusion.72), channel_id=1, source_target_pairs={{0,32},{2,34},{4,36},{6,38},{8,40},{10,42},{12,44},{14,46},{16,48}... | collective-permute-start | bytes 200 | tf_op jit(solution)/shard_map/ppermute | solution.py:21
  186.4 22.9 %copy-start.3 = (f32[16,64,128]{2,1,0:T(8,128)S(1)}, f32[16,64,128]{2,1,0:T(8,128)}, u32[]{:S(2)}) copy-start(f32[16,64,128]{2,1,0:T(8,128)} %copy-done.2) | copy-start | bytes 1572868
  186.4 22.9 %copy-start.5 = (f32[16,64,128]{2,1,0:T(8,128)S(1)}, f32[16,64,128]{2,1,0:T(8,128)}, u32[]{:S(2)}) copy-start(f32[16,64,128]{2,1,0:T(8,128)} %copy-done.4) | copy-start | bytes 1572868
  207.8 4.1 %copy-start.7 = (f32[16,64,128]{2,1,0:T(8,128)S(1)}, f32[16,64,128]{2,1,0:T(8,128)}, u32[]{:S(2)}) copy-start(f32[16,64,128]{2,1,0:T(8,128)} %fusion.2) | copy-start | bytes 1572868
  207.8 4.1 %copy-start.8 = (f32[128,16]{0,1:T(8,128)S(1)}, f32[128,16]{0,1:T(8,128)}, u32[]{:S(2)}) copy-start(f32[128,16]{0,1:T(8,128)} %copy.50) | copy-start | bytes 24580
  207.9 4.1 %copy-start.9 = (f32[1024]{0:T(1024)S(1)}, f32[1024]{0:T(1024)}, u32[]{:S(2)}) copy-start(f32[1024]{0:T(1024)} %mul.314) | copy-start | bytes 12292
  207.9 4.1 %copy-start.10 = (f32[1024]{0:T(1024)S(1)}, f32[1024]{0:T(1024)}, u32[]{:S(2)}) copy-start(f32[1024]{0:T(1024)} %mul.288) | copy-start | bytes 12292
  207.9 4.1 %collective-permute-start.12 = (bf16[128,1024]{0,1:T(8,128)(2,1)S(1)}, bf16[128,1024]{0,1:T(8,128)(2,1)S(1)}, u32[]{:S(2)}, u32[]{:S(2)}) collective-permute-start(bf16[128,1024]{0,1:T(8,128)(2,1)S(1)} %bitcast.111), channel_id=1, source_target_pairs={{0,128},{1,129},{2,130},{3,131},{4,132},{5,133},{6,134},{7,135},{8... | collective-permute-start | bytes 786440 | tf_op jit(solution)/shard_map/ppermute | solution.py:282
  212.4 4.3 %collective-permute-start.13 = (bf16[128,1024]{0,1:T(8,128)(2,1)S(1)}, bf16[128,1024]{0,1:T(8,128)(2,1)S(1)}, u32[]{:S(2)}, u32[]{:S(2)}) collective-permute-start(bf16[128,1024]{0,1:T(8,128)(2,1)S(1)} %get-tuple-element.6), channel_id=1, source_target_pairs={{128,0},{129,1},{130,2},{131,3},{132,4},{133,5},{134,6},{135,7},{1... | collective-permute-start | bytes 786440 | tf_op jit(solution)/shard_map/ppermute | solution.py:281
Sparse Core Ops, SparseCore 0:
  10.9 175.4 all-gather.1

commit v6 on v5

--- a/solution.py
+++ b/solution.py
@@ -156,7 +156,7 @@
         o_ref[...] = (acc_ref[...] / total_ref[...]).astype(o_ref.dtype)
 
 
-def attention_half(queries, keys, values, first_row):
+def attention_half(queries, keys, values, first_row, ready):
     row_count, q_heads, head_width = queries.shape
     kv_heads = keys.shape[1]
     group_size = q_heads // kv_heads
@@ -168,6 +168,7 @@
     )
     both = jnp.concatenate([keys, values], axis=1).transpose(1, 0, 2)
     both_all = lax.all_gather(both, "ctx", axis=1, tiled=True)
+    both_all, ready = lax.optimization_barrier((both_all, ready))
     key_count = both_all.shape[1]
     key_block = math.gcd(key_count, 4096)
     rows = group_size * row_count
@@ -198,7 +199,7 @@
         ),
         compiler_params=pltpu.CompilerParams(dimension_semantics=("parallel", "arbitrary")),
     )(jnp.reshape(first_row, (1,)).astype(jnp.int32), grouped, both_all, both_all)
-    return (
+    return ready, (
         out.reshape(kv_heads, group_size, row_count, head_width)
         .transpose(2, 0, 1, 3)
         .reshape(row_count, q_heads * head_width)
@@ -219,7 +220,6 @@
     q_part = lax.dynamic_slice_in_dim(queries, seg * q_share, q_share, 1)
     k_part = lax.dynamic_slice_in_dim(keys, seg * kv_share, kv_share, 1)
     v_part = lax.dynamic_slice_in_dim(values, seg * kv_share, kv_share, 1)
-    attended = attention_half(q_part, k_part, v_part, first_row)
 
     current = layer_in
     channel_count = current.shape[1]
@@ -277,6 +277,7 @@
     )
     state_part = result.reshape(row_count, heads_core * state_width).astype(jnp.bfloat16)
 
+    state_part, attended = attention_half(q_part, k_part, v_part, first_row, state_part)
     keep_state = seg == 0
     state_in_half = lax.ppermute(state_part, "segment", [(1, 0)])
     attended_in_half = lax.ppermute(attended, "segment", [(0, 1)])

time: 229 us -> 227 us (level)
    ppermute x11, waiting for transfers between devices: 100 us -> 111 us  [shifted_up(): return lax.ppermute(value, axis, pairs)]
    all_gather x1, waiting for transfers between devices: 32.5 us -> 21.6 us  [attention_half(): both_all = lax.all_gather(both, 'ctx', axis=1, tiled=True)]
  transfers between devices with their start and end apart: 15 -> 15, of which waited for: 13 -> 14; matrix products, arithmetic and copies ran while one was open for 11% -> 10% of each run, Pallas kernels for 9% -> 0%
where the time goes in v6:
time: 227 us; the launch traced here: 222 us
  waiting for transfers between devices  137 us (60%)
  starting transfers between devices  24.6 us (11%)
  Pallas kernels  20.2 us (9%)
  between operations  13.9 us (6%)
  matrix products  11.2 us (5%)
  other arithmetic  8.85 us (4%)
  local copies, waits for them, and re-layouts  6.92 us (3%)
    ppermute x11, waiting for transfers between devices, shifted_up(): return lax.ppermute(value, axis, pairs)  111 us
    all_gather x1, waiting for transfers between devices, attention_half(): both_all = lax.all_gather(both, 'ctx', axis=1, tiled=True)  21.6 us
    pallas_call x1, Pallas kernels, attention_half(): pl.pallas_call(functools.partial(flash_kernel, row_count=row_count, key_b...  20.2 us
    ppermute x11, starting transfers between devices, shifted_up(): return lax.ppermute(value, axis, pairs)  18.7 us
    add x5, other arithmetic, merge_states(): later[0][:, None, None] * earlier[1] + later[1]  6.78 us
  transfers between devices with their start and end apart: 15, of which 14 were waited for; matrix products, arithmetic and copies ran while one was open for 10% of the time, Pallas kernels for 0%

profile of v6, /device:TPU:231, one launch (start us, length us, event | category | flops | bytes accessed | tf_op | source)
XLA Modules:
  0.0 222.4 jit_solution(5492596893735277268)
XLA Ops:
  8.5 1.3 copy.44
  9.8 1.4 fusion.42
  11.2 4.1 %fusion = f32[128,1024]{0,1:T(8,128)S(1)} fusion(bf16[128,2048]{1,0:T(8,128)(2,1)} %param.13, bf16[1,2048,1024]{2,1,0:T(8,128)(2,1)} %param.14), kind=kOutput, calls=%fused_computation | convolution fusion | flops 536870912 | bytes 5242880 | tf_op jit(solution)/shard_map/dot_general | solution.py:233
  15.7 1.4 collective-permute-start
  17.3 3.2 %collective-permute-done = f32[128,273]{0,1:T(8,128)S(1)} collective-permute-done((f32[128,273]{0,1:T(8,128)S(1)}, f32[128,273]{0,1:T(8,128)S(1)}, u32[]{:S(2)}, u32[]{:S(2)}) %collective-permute-start) | collective-permute-done | bytes 139808 | tf_op jit(solution)/shard_map/ppermute | solution.py:25
  21.7 4.8 %collective-permute-start.6 = (f32[16,64,128]{2,1,0:T(8,128)S(1)}, f32[16,64,128]{2,1,0:T(8,128)}, u32[]{:S(2)}, u32[]{:S(2)}) collective-permute-start(f32[16,64,128]{2,1,0:T(8,128)S(1)} %fusion.58), channel_id=1, source_target_pairs={{0,2},{2,4},{4,6},{6,8},{8,10},{10,12},{12,14},{14,16},{16,18},{18... | collective-permute-start | bytes 1572872 | tf_op jit(solution)/shard_map/ppermute | solution.py:21
  26.5 13.7 %collective-permute-done.6 = f32[16,64,128]{2,1,0:T(8,128)} collective-permute-done((f32[16,64,128]{2,1,0:T(8,128)S(1)}, f32[16,64,128]{2,1,0:T(8,128)}, u32[]{:S(2)}, u32[]{:S(2)}) %collective-permute-start.6) | collective-permute-done | bytes 524320 | tf_op jit(solution)/shard_map/ppermute | solution.py:21
  41.4 1.3 collective-permute-start.7
  42.7 1.9 collective-permute-start.1
  44.6 9.9 %collective-permute-done.1 = f32[16]{0:T(128)S(1)} collective-permute-done((f32[16]{0:T(128)S(1)}, f32[16]{0:T(128)S(1)}, u32[]{:S(2)}, u32[]{:S(2)}) %collective-permute-start.1) | collective-permute-done | bytes 96 | tf_op jit(solution)/shard_map/ppermute | solution.py:21
  54.5 1.5 collective-permute-done.7
  57.9 1.3 collective-permute-start.8
  59.2 1.3 collective-permute-start.2
  60.5 3.1 %collective-permute-done.2 = f32[16]{0:T(128)S(1)} collective-permute-done((f32[16]{0:T(128)S(1)}, f32[16]{0:T(128)S(1)}, u32[]{:S(2)}, u32[]{:S(2)}) %collective-permute-start.2) | collective-permute-done | bytes 96 | tf_op jit(solution)/shard_map/ppermute | solution.py:21
  63.6 24.7 %collective-permute-done.8 = f32[16,64,128]{2,1,0:T(8,128)S(1)} collective-permute-done((f32[16,64,128]{2,1,0:T(8,128)S(1)}, f32[16,64,128]{2,1,0:T(8,128)S(1)}, u32[]{:S(2)}, u32[]{:S(2)}) %collective-permute-start.8) | collective-permute-done | bytes 524320 | tf_op jit(solution)/shard_map/ppermute | solution.py:21
  88.4 1.3 multiply_add_fusion.2
  89.7 1.3 collective-permute-start.9
  92.5 6.2 %collective-permute-done.3 = f32[16]{0:T(128)S(1)} collective-permute-done((f32[16]{0:T(128)S(1)}, f32[16]{0:T(128)S(1)}, u32[]{:S(2)}, u32[]{:S(2)}) %collective-permute-start.3) | collective-permute-done | bytes 96 | tf_op jit(solution)/shard_map/ppermute | solution.py:21
  98.8 8.1 %collective-permute-done.9 = f32[16,64,128]{2,1,0:T(8,128)} collective-permute-done((f32[16,64,128]{2,1,0:T(8,128)S(1)}, f32[16,64,128]{2,1,0:T(8,128)}, u32[]{:S(2)}, u32[]{:S(2)}) %collective-permute-start.9) | collective-permute-done | bytes 524320 | tf_op jit(solution)/shard_map/ppermute | solution.py:21
  108.1 1.4 collective-permute-start.10
  109.7 1.3 collective-permute-start.4
  111.7 15.2 %collective-permute-done.4 = f32[16]{0:T(128)S(1)} collective-permute-done((f32[16]{0:T(128)S(1)}, f32[16]{0:T(128)S(1)}, u32[]{:S(2)}, u32[]{:S(2)}) %collective-permute-start.4) | collective-permute-done | bytes 96 | tf_op jit(solution)/shard_map/ppermute | solution.py:21
  127.0 16.2 %collective-permute-done.10 = f32[16,64,128]{2,1,0:T(8,128)} collective-permute-done((f32[16,64,128]{2,1,0:T(8,128)S(1)}, f32[16,64,128]{2,1,0:T(8,128)}, u32[]{:S(2)}, u32[]{:S(2)}) %collective-permute-start.10) | collective-permute-done | bytes 524320 | tf_op jit(solution)/shard_map/ppermute | solution.py:21
  143.1 2.0 multiply_add_fusion
  146.7 2.2 %fusion.2 = f32[16,64,128]{2,1,0:T(8,128)S(1)} fusion(f32[128,16,64]{0,2,1:T(8,128)S(1)} %bitcast.102, f32[16,128]{1,0:T(8,128)S(1)} %get-tuple-element.21, f32[128,128]{1,0:T(8,128)S(1)} %convolution_multiply_fusion, f32[16,128]{1,0:T(8,128)S(1)} %copy.50, pred[128,128]{1,0:T(8,128)(4,1)S(1)} %iota_compare_fusion), kind=kOutput, calls=%fused_computation.3 | convolution fusion | flops 202637312 | bytes 1146880 | tf_op jit(solution)/shard_map/gkts,sgkp->tgkp/dot_general | solution.py:46
  149.0 1.5 collective-permute-start.5
  150.5 3.8 %collective-permute-done.5 = f32[16]{0:T(128)S(1)} collective-permute-done((f32[16]{0:T(128)S(1)}, f32[16]{0:T(128)S(1)}, u32[]{:S(2)}, u32[]{:S(2)}) %collective-permute-start.5) | collective-permute-done | bytes 96 | tf_op jit(solution)/shard_map/ppermute | solution.py:21
  154.3 8.5 %collective-permute-done.11 = f32[16,64,128]{2,1,0:T(8,128)} collective-permute-done((f32[16,64,128]{2,1,0:T(8,128)}, f32[16,64,128]{2,1,0:T(8,128)}, u32[]{:S(2)}, u32[]{:S(2)}) %collective-permute-start.11) | collective-permute-done | bytes 524320 | tf_op jit(solution)/shard_map/ppermute | solution.py:21
  162.9 2.6 %fusion.12 = (f32[128,16]{0,1:T(8,128)S(1)}, f32[16,64,128]{2,1,0:T(8,128)S(1)}) fusion(f32[16,64,128]{2,1,0:T(8,128)S(1)} %fusion.2, f32[16]{0:T(128)S(1)} %fusion.67, f32[128,16]{0,1:T(8,128)S(1)} %copy.52, f32[128,1024]{0,1:T(8,128)S(1)} %get-tuple-element.16, f32[128,273]{0,1:T(8,128)S(1)} %fusion.56, f32[128]{0:T(128)S(1)} %fusion.70, ...), kind=kOutput, calls=%fused_computation.16 | convolution fusion | flops 204355584 | bytes 4804102 | tf_op jit(solution)/shard_map/tgn,gkpn->tgkp/dot_general | solution.py:69
  165.8 21.6 %all-gather.2.cloned.1.call-done.k_ref.v_ref = bf16[4,8192,128]{2,1,0:T(8,128)(2,1)} async-done(((bf16[4,128,128]{2,1,0:T(8,128)(2,1)}), bf16[4,8192,128]{2,1,0:T(8,128)(2,1)}) %all-gather.2.cloned.1.call-update) | async-done | bytes 8388624 | tf_op jit(solution)/shard_map/all_gather | solution.py:170
  187.4 20.2 %shard_map.100 = bf16[2,512,128]{2,1,0:T(8,128)(2,1)} custom-call(s32[1]{0:T(128)} %bitcast.28.first_ref, bf16[2,512,128]{2,1,0:T(8,128)(2,1)} %bitcast.105, bf16[4,8192,128]{2,1,0:T(8,128)(2,1)} %all-gather.2.cloned.1.call-done.k_ref.v_ref, bf16[4,8192,128]{2,1,0:T(8,128)(2,1)} %all-gather.2.cloned.1.call-done.k_ref.v_ref), custom_call_target="tpu_custom_call" | custom-call | tf_op jit(solution)/shard_map/pallas_call | solution.py:182
  210.1 3.2 %collective-permute-start.13 = (bf16[128,1024]{0,1:T(8,128)(2,1)S(1)}, bf16[128,1024]{0,1:T(8,128)(2,1)S(1)}, u32[]{:S(2)}, u32[]{:S(2)}) collective-permute-start(bf16[128,1024]{0,1:T(8,128)(2,1)S(1)} %fusion.18), channel_id=1, source_target_pairs={{128,0},{129,1},{130,2},{131,3},{132,4},{133,5},{134,6},{135,7},{1... | collective-permute-start | bytes 786440 | tf_op jit(solution)/shard_map/ppermute | solution.py:282
  (73 shorter events, 17.0 us)
Async XLA Ops:
  6.5 103.1 %copy-start = (bf16[128,16,128]{2,1,0:T(8,128)(2,1)S(1)}, bf16[128,16,128]{2,1,0:T(8,128)(2,1)}, u32[]{:S(2)}) copy-start(bf16[128,16,128]{2,1,0:T(8,128)(2,1)} %param.10) | copy-start | bytes 1572868
  6.5 180.9 %all-gather.2.cloned.1.call-start = ((), (), s32[]{:S(2)}) async-start(), calls=%async_computation | async-start | bytes 8519680 | tf_op jit(solution)/shard_map/all_gather | solution.py:170
  11.2 6.0 %copy-start.6 = (f32[1,32]{1,0:T(1,128)S(1)}, f32[1,32]{1,0:T(1,128)}, u32[]{:S(2)}) copy-start(f32[1,32]{1,0:T(1,128)} %param.16) | copy-start | bytes 388
  11.2 6.0 %copy-start.7 = (f32[1,32]{1,0:T(1,128)S(1)}, f32[1,32]{1,0:T(1,128)}, u32[]{:S(2)}) copy-start(f32[1,32]{1,0:T(1,128)} %param.17) | copy-start | bytes 388
  15.7 4.7 %collective-permute-start = (f32[128,273]{0,1:T(8,128)S(1)}, f32[128,273]{0,1:T(8,128)S(1)}, u32[]{:S(2)}, u32[]{:S(2)}) collective-permute-start(f32[128,273]{0,1:T(8,128)S(1)} %pad_maximum_fusion), channel_id=1, source_target_pairs={{0,1},{1,0},{2,3},{3,2},{4,5},{5,4},{6,7},{7,6},{8,9},{9,8},{10,11... | collective-permute-start | bytes 419336 | tf_op jit(solution)/shard_map/ppermute | solution.py:25
  17.1 73.9 %copy-start.8 = (f32[1,32]{1,0:T(1,128)S(1)}, f32[1,32]{1,0:T(1,128)}, u32[]{:S(2)}) copy-start(f32[1,32]{1,0:T(1,128)} %param.18) | copy-start | bytes 388
  21.0 88.5 %copy-start.5 = (f32[1,32,64]{2,1,0:T(8,128)S(1)}, f32[1,32,64]{2,1,0:T(8,128)}, u32[]{:S(2)}) copy-start(f32[1,32,64]{2,1,0:T(8,128)} %param.19) | copy-start | bytes 24580
  21.7 18.5 %collective-permute-start.6 = (f32[16,64,128]{2,1,0:T(8,128)S(1)}, f32[16,64,128]{2,1,0:T(8,128)}, u32[]{:S(2)}, u32[]{:S(2)}) collective-permute-start(f32[16,64,128]{2,1,0:T(8,128)S(1)} %fusion.58), channel_id=1, source_target_pairs={{0,2},{2,4},{4,6},{6,8},{8,10},{10,12},{12,14},{14,16},{16,18},{18... | collective-permute-start | bytes 1572872 | tf_op jit(solution)/shard_map/ppermute | solution.py:21
  41.4 14.6 %collective-permute-start.7 = (f32[16,64,128]{2,1,0:T(8,128)S(1)}, f32[16,64,128]{2,1,0:T(8,128)S(1)}, u32[]{:S(2)}, u32[]{:S(2)}) collective-permute-start(f32[16,64,128]{2,1,0:T(8,128)S(1)} %multiply_add_fusion.4), channel_id=1, source_target_pairs={{0,4},{2,6},{4,8},{6,10},{8,12},{10,14},{12,16},{14,18},{16,20},{1... | collective-permute-start | bytes 1572872 | tf_op jit(solution)/shard_map/ppermute | solution.py:21
  42.7 11.8 %collective-permute-start.1 = (f32[16]{0:T(128)S(1)}, f32[16]{0:T(128)S(1)}, u32[]{:S(2)}, u32[]{:S(2)}) collective-permute-start(f32[16]{0:T(128)S(1)} %fusion.79), channel_id=1, source_target_pairs={{0,2},{2,4},{4,6},{6,8},{8,10},{10,12},{12,14},{14,16},{16,18},{18... | collective-permute-start | bytes 200 | tf_op jit(solution)/shard_map/ppermute | solution.py:21
  56.0 0.8 copy-start.2
  57.9 5.7 %copy-start.1 = (f32[16,64,128]{2,1,0:T(8,128)}, f32[16,64,128]{2,1,0:T(8,128)S(1)}, u32[]{:S(2)}) copy-start(f32[16,64,128]{2,1,0:T(8,128)S(1)} %multiply_add_fusion.3) | copy-start | bytes 1572868
  57.9 30.4 %collective-permute-start.8 = (f32[16,64,128]{2,1,0:T(8,128)S(1)}, f32[16,64,128]{2,1,0:T(8,128)S(1)}, u32[]{:S(2)}, u32[]{:S(2)}) collective-permute-start(f32[16,64,128]{2,1,0:T(8,128)S(1)} %multiply_add_fusion.3), channel_id=1, source_target_pairs={{0,8},{2,10},{4,12},{6,14},{8,16},{10,18},{12,20},{14,22},{16,24},... | collective-permute-start | bytes 1572872 | tf_op jit(solution)/shard_map/ppermute | solution.py:21
  59.2 4.4 %collective-permute-start.2 = (f32[16]{0:T(128)S(1)}, f32[16]{0:T(128)S(1)}, u32[]{:S(2)}, u32[]{:S(2)}) collective-permute-start(f32[16]{0:T(128)S(1)} %get-tuple-element.13), channel_id=1, source_target_pairs={{0,4},{2,6},{4,8},{6,10},{8,12},{10,14},{12,16},{14,18},{16,20},{1... | collective-permute-start | bytes 200 | tf_op jit(solution)/shard_map/ppermute | solution.py:21
  88.4 10.4 %copy-start.3 = (f32[16,64,128]{2,1,0:T(8,128)}, f32[16,64,128]{2,1,0:T(8,128)S(1)}, u32[]{:S(2)}) copy-start(f32[16,64,128]{2,1,0:T(8,128)S(1)} %collective-permute-done.8) | copy-start | bytes 1572868
  89.7 17.2 %collective-permute-start.9 = (f32[16,64,128]{2,1,0:T(8,128)S(1)}, f32[16,64,128]{2,1,0:T(8,128)}, u32[]{:S(2)}, u32[]{:S(2)}) collective-permute-start(f32[16,64,128]{2,1,0:T(8,128)S(1)} %multiply_add_fusion.2), channel_id=1, source_target_pairs={{0,16},{2,18},{4,20},{6,22},{8,24},{10,26},{12,28},{14,30},{16,32}... | collective-permute-start | bytes 1572872 | tf_op jit(solution)/shard_map/ppermute | solution.py:21
  91.1 7.7 %collective-permute-start.3 = (f32[16]{0:T(128)S(1)}, f32[16]{0:T(128)S(1)}, u32[]{:S(2)}, u32[]{:S(2)}) collective-permute-start(f32[16]{0:T(128)S(1)} %fusion.76), channel_id=1, source_target_pairs={{0,8},{2,10},{4,12},{6,14},{8,16},{10,18},{12,20},{14,22},{16,24},... | collective-permute-start | bytes 200 | tf_op jit(solution)/shard_map/ppermute | solution.py:21
  108.1 54.8 %copy-start.4 = (f32[16,64,128]{2,1,0:T(8,128)S(1)}, f32[16,64,128]{2,1,0:T(8,128)}, u32[]{:S(2)}) copy-start(f32[16,64,128]{2,1,0:T(8,128)} %copy-done.3) | copy-start | bytes 1572868
  108.1 35.0 %collective-permute-start.10 = (f32[16,64,128]{2,1,0:T(8,128)S(1)}, f32[16,64,128]{2,1,0:T(8,128)}, u32[]{:S(2)}, u32[]{:S(2)}) collective-permute-start(f32[16,64,128]{2,1,0:T(8,128)S(1)} %multiply_add_fusion.1), channel_id=1, source_target_pairs={{0,32},{2,34},{4,36},{6,38},{8,40},{10,42},{12,44},{14,46},{16,48}... | collective-permute-start | bytes 1572872 | tf_op jit(solution)/shard_map/ppermute | solution.py:21
  109.7 17.3 %collective-permute-start.4 = (f32[16]{0:T(128)S(1)}, f32[16]{0:T(128)S(1)}, u32[]{:S(2)}, u32[]{:S(2)}) collective-permute-start(f32[16]{0:T(128)S(1)} %fusion.74), channel_id=1, source_target_pairs={{0,16},{2,18},{4,20},{6,22},{8,24},{10,26},{12,28},{14,30},{16,32}... | collective-permute-start | bytes 200 | tf_op jit(solution)/shard_map/ppermute | solution.py:21
  145.1 17.8 %collective-permute-start.11 = (f32[16,64,128]{2,1,0:T(8,128)}, f32[16,64,128]{2,1,0:T(8,128)}, u32[]{:S(2)}, u32[]{:S(2)}) collective-permute-start(f32[16,64,128]{2,1,0:T(8,128)} %multiply_add_fusion), channel_id=1, source_target_pairs={{0,64},{2,66},{4,68},{6,70},{8,72},{10,74},{12,76},{14,78},{16,80}... | collective-permute-start | bytes 1572872 | tf_op jit(solution)/shard_map/ppermute | solution.py:21
  149.0 5.3 %collective-permute-start.5 = (f32[16]{0:T(128)S(1)}, f32[16]{0:T(128)S(1)}, u32[]{:S(2)}, u32[]{:S(2)}) collective-permute-start(f32[16]{0:T(128)S(1)} %fusion.72), channel_id=1, source_target_pairs={{0,32},{2,34},{4,36},{6,38},{8,40},{10,42},{12,44},{14,46},{16,48}... | collective-permute-start | bytes 200 | tf_op jit(solution)/shard_map/ppermute | solution.py:21
  208.8 4.5 %collective-permute-start.12 = (bf16[128,1024]{0,1:T(8,128)(2,1)S(1)}, bf16[128,1024]{0,1:T(8,128)(2,1)S(1)}, u32[]{:S(2)}, u32[]{:S(2)}) collective-permute-start(bf16[128,1024]{0,1:T(8,128)(2,1)S(1)} %bitcast.107), channel_id=1, source_target_pairs={{0,128},{1,129},{2,130},{3,131},{4,132},{5,133},{6,134},{7,135},{8... | collective-permute-start | bytes 786440 | tf_op jit(solution)/shard_map/ppermute | solution.py:283
  210.1 4.3 %collective-permute-start.13 = (bf16[128,1024]{0,1:T(8,128)(2,1)S(1)}, bf16[128,1024]{0,1:T(8,128)(2,1)S(1)}, u32[]{:S(2)}, u32[]{:S(2)}) collective-permute-start(bf16[128,1024]{0,1:T(8,128)(2,1)S(1)} %fusion.18), channel_id=1, source_target_pairs={{128,0},{129,1},{130,2},{131,3},{132,4},{133,5},{134,6},{135,7},{1... | collective-permute-start | bytes 786440 | tf_op jit(solution)/shard_map/ppermute | solution.py:282
Sparse Core Ops, SparseCore 0:
  10.9 176.5 all-gather.1

commit v7 on v6

--- a/solution.py
+++ b/solution.py
@@ -156,7 +156,7 @@
         o_ref[...] = (acc_ref[...] / total_ref[...]).astype(o_ref.dtype)
 
 
-def attention_half(queries, keys, values, first_row, ready):
+def attention_half(queries, keys, values, first_row, ready, gathered):
     row_count, q_heads, head_width = queries.shape
     kv_heads = keys.shape[1]
     group_size = q_heads // kv_heads
@@ -221,6 +221,8 @@
     k_part = lax.dynamic_slice_in_dim(keys, seg * kv_share, kv_share, 1)
     v_part = lax.dynamic_slice_in_dim(values, seg * kv_share, kv_share, 1)
 
+    both_kv = jnp.concatenate([k_part, v_part], axis=1).transpose(1, 0, 2)
+    both_kv, layer_in = lax.optimization_barrier((both_kv, layer_in))
     current = layer_in
     channel_count = current.shape[1]
     heads_dev = dt_bias.shape[1]
@@ -277,7 +279,7 @@
     )
     state_part = result.reshape(row_count, heads_core * state_width).astype(jnp.bfloat16)
 
-    state_part, attended = attention_half(q_part, k_part, v_part, first_row, state_part)
+    state_part, attended = attention_half(q_part, k_part, v_part, first_row, state_part, both_kv)
     keep_state = seg == 0
     state_in_half = lax.ppermute(state_part, "segment", [(1, 0)])
     attended_in_half = lax.ppermute(attended, "segment", [(0, 1)])

time: 227 us -> 227 us (level)
  no operation moved by 1% of the time
where the time goes in v7:
time: 227 us; the launch traced here: 222 us
  waiting for transfers between devices  137 us (60%)
  starting transfers between devices  24.6 us (11%)
  Pallas kernels  20.2 us (9%)
  between operations  13.9 us (6%)
  matrix products  11.2 us (5%)
  other arithmetic  8.85 us (4%)
  local copies, waits for them, and re-layouts  6.92 us (3%)
    ppermute x11, waiting for transfers between devices, shifted_up(): return lax.ppermute(value, axis, pairs)  111 us
    all_gather x1, waiting for transfers between devices, attention_half(): both_all = lax.all_gather(both, 'ctx', axis=1, tiled=True)  21.6 us
    pallas_call x1, Pallas kernels, attention_half(): pl.pallas_call(functools.partial(flash_kernel, row_count=row_count, key_b...  20.2 us
    ppermute x11, starting transfers between devices, shifted_up(): return lax.ppermute(value, axis, pairs)  18.7 us
    add x5, other arithmetic, merge_states(): later[0][:, None, None] * earlier[1] + later[1]  6.78 us
  transfers between devices with their start and end apart: 15, of which 14 were waited for; matrix products, arithmetic and copies ran while one was open for 10% of the time, Pallas kernels for 0%

profile of v7, /device:TPU:231, one launch (start us, length us, event | category | flops | bytes accessed | tf_op | source)
XLA Modules:
  0.0 222.4 jit_solution(1162116287808580280)
XLA Ops:
  8.5 1.3 copy.44
  9.8 1.4 fusion.42
  11.2 4.1 %fusion = f32[128,1024]{0,1:T(8,128)S(1)} fusion(bf16[128,2048]{1,0:T(8,128)(2,1)} %param.13, bf16[1,2048,1024]{2,1,0:T(8,128)(2,1)} %param.14), kind=kOutput, calls=%fused_computation | convolution fusion | flops 536870912 | bytes 5242880 | tf_op jit(solution)/shard_map/dot_general | solution.py:235
  15.7 1.4 collective-permute-start
  17.3 3.2 %collective-permute-done = f32[128,273]{0,1:T(8,128)S(1)} collective-permute-done((f32[128,273]{0,1:T(8,128)S(1)}, f32[128,273]{0,1:T(8,128)S(1)}, u32[]{:S(2)}, u32[]{:S(2)}) %collective-permute-start) | collective-permute-done | bytes 139808 | tf_op jit(solution)/shard_map/ppermute | solution.py:25
  21.7 4.8 %collective-permute-start.6 = (f32[16,64,128]{2,1,0:T(8,128)S(1)}, f32[16,64,128]{2,1,0:T(8,128)}, u32[]{:S(2)}, u32[]{:S(2)}) collective-permute-start(f32[16,64,128]{2,1,0:T(8,128)S(1)} %fusion.58), channel_id=1, source_target_pairs={{0,2},{2,4},{4,6},{6,8},{8,10},{10,12},{12,14},{14,16},{16,18},{18... | collective-permute-start | bytes 1572872 | tf_op jit(solution)/shard_map/ppermute | solution.py:21
  26.5 13.7 %collective-permute-done.6 = f32[16,64,128]{2,1,0:T(8,128)} collective-permute-done((f32[16,64,128]{2,1,0:T(8,128)S(1)}, f32[16,64,128]{2,1,0:T(8,128)}, u32[]{:S(2)}, u32[]{:S(2)}) %collective-permute-start.6) | collective-permute-done | bytes 524320 | tf_op jit(solution)/shard_map/ppermute | solution.py:21
  41.4 1.3 collective-permute-start.7
  42.7 1.9 collective-permute-start.1
  44.6 9.9 %collective-permute-done.1 = f32[16]{0:T(128)S(1)} collective-permute-done((f32[16]{0:T(128)S(1)}, f32[16]{0:T(128)S(1)}, u32[]{:S(2)}, u32[]{:S(2)}) %collective-permute-start.1) | collective-permute-done | bytes 96 | tf_op jit(solution)/shard_map/ppermute | solution.py:21
  54.5 1.5 collective-permute-done.7
  57.9 1.3 collective-permute-start.8
  59.2 1.3 collective-permute-start.2
  60.5 3.1 %collective-permute-done.2 = f32[16]{0:T(128)S(1)} collective-permute-done((f32[16]{0:T(128)S(1)}, f32[16]{0:T(128)S(1)}, u32[]{:S(2)}, u32[]{:S(2)}) %collective-permute-start.2) | collective-permute-done | bytes 96 | tf_op jit(solution)/shard_map/ppermute | solution.py:21
  63.6 24.7 %collective-permute-done.8 = f32[16,64,128]{2,1,0:T(8,128)S(1)} collective-permute-done((f32[16,64,128]{2,1,0:T(8,128)S(1)}, f32[16,64,128]{2,1,0:T(8,128)S(1)}, u32[]{:S(2)}, u32[]{:S(2)}) %collective-permute-start.8) | collective-permute-done | bytes 524320 | tf_op jit(solution)/shard_map/ppermute | solution.py:21
  88.4 1.3 multiply_add_fusion.2
  89.7 1.3 collective-permute-start.9
  92.5 6.2 %collective-permute-done.3 = f32[16]{0:T(128)S(1)} collective-permute-done((f32[16]{0:T(128)S(1)}, f32[16]{0:T(128)S(1)}, u32[]{:S(2)}, u32[]{:S(2)}) %collective-permute-start.3) | collective-permute-done | bytes 96 | tf_op jit(solution)/shard_map/ppermute | solution.py:21
  98.8 8.1 %collective-permute-done.9 = f32[16,64,128]{2,1,0:T(8,128)} collective-permute-done((f32[16,64,128]{2,1,0:T(8,128)S(1)}, f32[16,64,128]{2,1,0:T(8,128)}, u32[]{:S(2)}, u32[]{:S(2)}) %collective-permute-start.9) | collective-permute-done | bytes 524320 | tf_op jit(solution)/shard_map/ppermute | solution.py:21
  108.1 1.4 collective-permute-start.10
  109.7 1.3 collective-permute-start.4
  111.7 15.2 %collective-permute-done.4 = f32[16]{0:T(128)S(1)} collective-permute-done((f32[16]{0:T(128)S(1)}, f32[16]{0:T(128)S(1)}, u32[]{:S(2)}, u32[]{:S(2)}) %collective-permute-start.4) | collective-permute-done | bytes 96 | tf_op jit(solution)/shard_map/ppermute | solution.py:21
  127.0 16.2 %collective-permute-done.10 = f32[16,64,128]{2,1,0:T(8,128)} collective-permute-done((f32[16,64,128]{2,1,0:T(8,128)S(1)}, f32[16,64,128]{2,1,0:T(8,128)}, u32[]{:S(2)}, u32[]{:S(2)}) %collective-permute-start.10) | collective-permute-done | bytes 524320 | tf_op jit(solution)/shard_map/ppermute | solution.py:21
  143.1 2.0 multiply_add_fusion
  146.7 2.2 %fusion.2 = f32[16,64,128]{2,1,0:T(8,128)S(1)} fusion(f32[128,16,64]{0,2,1:T(8,128)S(1)} %bitcast.102, f32[16,128]{1,0:T(8,128)S(1)} %get-tuple-element.23, f32[128,128]{1,0:T(8,128)S(1)} %convolution_multiply_fusion, f32[16,128]{1,0:T(8,128)S(1)} %copy.50, pred[128,128]{1,0:T(8,128)(4,1)S(1)} %iota_compare_fusion), kind=kOutput, calls=%fused_computation.3 | convolution fusion | flops 202637312 | bytes 1146880 | tf_op jit(solution)/shard_map/gkts,sgkp->tgkp/dot_general | solution.py:46
  149.0 1.5 collective-permute-start.5
  150.5 3.8 %collective-permute-done.5 = f32[16]{0:T(128)S(1)} collective-permute-done((f32[16]{0:T(128)S(1)}, f32[16]{0:T(128)S(1)}, u32[]{:S(2)}, u32[]{:S(2)}) %collective-permute-start.5) | collective-permute-done | bytes 96 | tf_op jit(solution)/shard_map/ppermute | solution.py:21
  154.3 8.5 %collective-permute-done.11 = f32[16,64,128]{2,1,0:T(8,128)} collective-permute-done((f32[16,64,128]{2,1,0:T(8,128)}, f32[16,64,128]{2,1,0:T(8,128)}, u32[]{:S(2)}, u32[]{:S(2)}) %collective-permute-start.11) | collective-permute-done | bytes 524320 | tf_op jit(solution)/shard_map/ppermute | solution.py:21
  162.9 2.6 %fusion.12 = (f32[128,16]{0,1:T(8,128)S(1)}, f32[16,64,128]{2,1,0:T(8,128)S(1)}) fusion(f32[16,64,128]{2,1,0:T(8,128)S(1)} %fusion.2, f32[16]{0:T(128)S(1)} %fusion.67, f32[128,16]{0,1:T(8,128)S(1)} %copy.52, f32[128,1024]{0,1:T(8,128)S(1)} %get-tuple-element.18, f32[128,273]{0,1:T(8,128)S(1)} %fusion.56, f32[128]{0:T(128)S(1)} %fusion.70, ...), kind=kOutput, calls=%fused_computation.16 | convolution fusion | flops 204355584 | bytes 4804102 | tf_op jit(solution)/shard_map/tgn,gkpn->tgkp/dot_general | solution.py:69
  165.8 21.6 %all-gather.2.cloned.1.call-done.k_ref.v_ref = bf16[4,8192,128]{2,1,0:T(8,128)(2,1)} async-done(((bf16[4,128,128]{2,1,0:T(8,128)(2,1)}), bf16[4,8192,128]{2,1,0:T(8,128)(2,1)}) %all-gather.2.cloned.1.call-update) | async-done | bytes 8388624 | tf_op jit(solution)/shard_map/all_gather | solution.py:170
  187.4 20.2 %shard_map.100 = bf16[2,512,128]{2,1,0:T(8,128)(2,1)} custom-call(s32[1]{0:T(128)} %bitcast.28.first_ref, bf16[2,512,128]{2,1,0:T(8,128)(2,1)} %bitcast.105, bf16[4,8192,128]{2,1,0:T(8,128)(2,1)} %all-gather.2.cloned.1.call-done.k_ref.v_ref, bf16[4,8192,128]{2,1,0:T(8,128)(2,1)} %all-gather.2.cloned.1.call-done.k_ref.v_ref), custom_call_target="tpu_custom_call" | custom-call | tf_op jit(solution)/shard_map/pallas_call | solution.py:182
  210.1 3.2 %collective-permute-start.13 = (bf16[128,1024]{0,1:T(8,128)(2,1)S(1)}, bf16[128,1024]{0,1:T(8,128)(2,1)S(1)}, u32[]{:S(2)}, u32[]{:S(2)}) collective-permute-start(bf16[128,1024]{0,1:T(8,128)(2,1)S(1)} %fusion.18), channel_id=1, source_target_pairs={{128,0},{129,1},{130,2},{131,3},{132,4},{133,5},{134,6},{135,7},{1... | collective-permute-start | bytes 786440 | tf_op jit(solution)/shard_map/ppermute | solution.py:284
  (73 shorter events, 17.0 us)
Async XLA Ops:
  6.5 103.1 %copy-start = (bf16[128,16,128]{2,1,0:T(8,128)(2,1)S(1)}, bf16[128,16,128]{2,1,0:T(8,128)(2,1)}, u32[]{:S(2)}) copy-start(bf16[128,16,128]{2,1,0:T(8,128)(2,1)} %param.10) | copy-start | bytes 1572868
  6.5 180.9 %all-gather.2.cloned.1.call-start = ((), (), s32[]{:S(2)}) async-start(), calls=%async_computation | async-start | bytes 8519680 | tf_op jit(solution)/shard_map/all_gather | solution.py:170
  11.2 6.0 %copy-start.6 = (f32[1,32]{1,0:T(1,128)S(1)}, f32[1,32]{1,0:T(1,128)}, u32[]{:S(2)}) copy-start(f32[1,32]{1,0:T(1,128)} %param.16) | copy-start | bytes 388
  11.2 6.0 %copy-start.7 = (f32[1,32]{1,0:T(1,128)S(1)}, f32[1,32]{1,0:T(1,128)}, u32[]{:S(2)}) copy-start(f32[1,32]{1,0:T(1,128)} %param.17) | copy-start | bytes 388
  15.7 4.7 %collective-permute-start = (f32[128,273]{0,1:T(8,128)S(1)}, f32[128,273]{0,1:T(8,128)S(1)}, u32[]{:S(2)}, u32[]{:S(2)}) collective-permute-start(f32[128,273]{0,1:T(8,128)S(1)} %pad_maximum_fusion), channel_id=1, source_target_pairs={{0,1},{1,0},{2,3},{3,2},{4,5},{5,4},{6,7},{7,6},{8,9},{9,8},{10,11... | collective-permute-start | bytes 419336 | tf_op jit(solution)/shard_map/ppermute | solution.py:25
  17.1 73.9 %copy-start.8 = (f32[1,32]{1,0:T(1,128)S(1)}, f32[1,32]{1,0:T(1,128)}, u32[]{:S(2)}) copy-start(f32[1,32]{1,0:T(1,128)} %param.18) | copy-start | bytes 388
  21.0 88.5 %copy-start.5 = (f32[1,32,64]{2,1,0:T(8,128)S(1)}, f32[1,32,64]{2,1,0:T(8,128)}, u32[]{:S(2)}) copy-start(f32[1,32,64]{2,1,0:T(8,128)} %param.19) | copy-start | bytes 24580
  21.7 18.5 %collective-permute-start.6 = (f32[16,64,128]{2,1,0:T(8,128)S(1)}, f32[16,64,128]{2,1,0:T(8,128)}, u32[]{:S(2)}, u32[]{:S(2)}) collective-permute-start(f32[16,64,128]{2,1,0:T(8,128)S(1)} %fusion.58), channel_id=1, source_target_pairs={{0,2},{2,4},{4,6},{6,8},{8,10},{10,12},{12,14},{14,16},{16,18},{18... | collective-permute-start | bytes 1572872 | tf_op jit(solution)/shard_map/ppermute | solution.py:21
  41.4 14.6 %collective-permute-start.7 = (f32[16,64,128]{2,1,0:T(8,128)S(1)}, f32[16,64,128]{2,1,0:T(8,128)S(1)}, u32[]{:S(2)}, u32[]{:S(2)}) collective-permute-start(f32[16,64,128]{2,1,0:T(8,128)S(1)} %multiply_add_fusion.4), channel_id=1, source_target_pairs={{0,4},{2,6},{4,8},{6,10},{8,12},{10,14},{12,16},{14,18},{16,20},{1... | collective-permute-start | bytes 1572872 | tf_op jit(solution)/shard_map/ppermute | solution.py:21
  42.7 11.8 %collective-permute-start.1 = (f32[16]{0:T(128)S(1)}, f32[16]{0:T(128)S(1)}, u32[]{:S(2)}, u32[]{:S(2)}) collective-permute-start(f32[16]{0:T(128)S(1)} %fusion.79), channel_id=1, source_target_pairs={{0,2},{2,4},{4,6},{6,8},{8,10},{10,12},{12,14},{14,16},{16,18},{18... | collective-permute-start | bytes 200 | tf_op jit(solution)/shard_map/ppermute | solution.py:21
  56.0 0.8 copy-start.2
  57.9 5.7 %copy-start.1 = (f32[16,64,128]{2,1,0:T(8,128)}, f32[16,64,128]{2,1,0:T(8,128)S(1)}, u32[]{:S(2)}) copy-start(f32[16,64,128]{2,1,0:T(8,128)S(1)} %multiply_add_fusion.3) | copy-start | bytes 1572868
  57.9 30.4 %collective-permute-start.8 = (f32[16,64,128]{2,1,0:T(8,128)S(1)}, f32[16,64,128]{2,1,0:T(8,128)S(1)}, u32[]{:S(2)}, u32[]{:S(2)}) collective-permute-start(f32[16,64,128]{2,1,0:T(8,128)S(1)} %multiply_add_fusion.3), channel_id=1, source_target_pairs={{0,8},{2,10},{4,12},{6,14},{8,16},{10,18},{12,20},{14,22},{16,24},... | collective-permute-start | bytes 1572872 | tf_op jit(solution)/shard_map/ppermute | solution.py:21
  59.2 4.4 %collective-permute-start.2 = (f32[16]{0:T(128)S(1)}, f32[16]{0:T(128)S(1)}, u32[]{:S(2)}, u32[]{:S(2)}) collective-permute-start(f32[16]{0:T(128)S(1)} %get-tuple-element.15), channel_id=1, source_target_pairs={{0,4},{2,6},{4,8},{6,10},{8,12},{10,14},{12,16},{14,18},{16,20},{1... | collective-permute-start | bytes 200 | tf_op jit(solution)/shard_map/ppermute | solution.py:21
  88.4 10.4 %copy-start.3 = (f32[16,64,128]{2,1,0:T(8,128)}, f32[16,64,128]{2,1,0:T(8,128)S(1)}, u32[]{:S(2)}) copy-start(f32[16,64,128]{2,1,0:T(8,128)S(1)} %collective-permute-done.8) | copy-start | bytes 1572868
  89.7 17.2 %collective-permute-start.9 = (f32[16,64,128]{2,1,0:T(8,128)S(1)}, f32[16,64,128]{2,1,0:T(8,128)}, u32[]{:S(2)}, u32[]{:S(2)}) collective-permute-start(f32[16,64,128]{2,1,0:T(8,128)S(1)} %multiply_add_fusion.2), channel_id=1, source_target_pairs={{0,16},{2,18},{4,20},{6,22},{8,24},{10,26},{12,28},{14,30},{16,32}... | collective-permute-start | bytes 1572872 | tf_op jit(solution)/shard_map/ppermute | solution.py:21
  91.1 7.7 %collective-permute-start.3 = (f32[16]{0:T(128)S(1)}, f32[16]{0:T(128)S(1)}, u32[]{:S(2)}, u32[]{:S(2)}) collective-permute-start(f32[16]{0:T(128)S(1)} %fusion.76), channel_id=1, source_target_pairs={{0,8},{2,10},{4,12},{6,14},{8,16},{10,18},{12,20},{14,22},{16,24},... | collective-permute-start | bytes 200 | tf_op jit(solution)/shard_map/ppermute | solution.py:21
  108.1 54.8 %copy-start.4 = (f32[16,64,128]{2,1,0:T(8,128)S(1)}, f32[16,64,128]{2,1,0:T(8,128)}, u32[]{:S(2)}) copy-start(f32[16,64,128]{2,1,0:T(8,128)} %copy-done.3) | copy-start | bytes 1572868
  108.1 35.0 %collective-permute-start.10 = (f32[16,64,128]{2,1,0:T(8,128)S(1)}, f32[16,64,128]{2,1,0:T(8,128)}, u32[]{:S(2)}, u32[]{:S(2)}) collective-permute-start(f32[16,64,128]{2,1,0:T(8,128)S(1)} %multiply_add_fusion.1), channel_id=1, source_target_pairs={{0,32},{2,34},{4,36},{6,38},{8,40},{10,42},{12,44},{14,46},{16,48}... | collective-permute-start | bytes 1572872 | tf_op jit(solution)/shard_map/ppermute | solution.py:21
  109.7 17.3 %collective-permute-start.4 = (f32[16]{0:T(128)S(1)}, f32[16]{0:T(128)S(1)}, u32[]{:S(2)}, u32[]{:S(2)}) collective-permute-start(f32[16]{0:T(128)S(1)} %fusion.74), channel_id=1, source_target_pairs={{0,16},{2,18},{4,20},{6,22},{8,24},{10,26},{12,28},{14,30},{16,32}... | collective-permute-start | bytes 200 | tf_op jit(solution)/shard_map/ppermute | solution.py:21
  145.1 17.8 %collective-permute-start.11 = (f32[16,64,128]{2,1,0:T(8,128)}, f32[16,64,128]{2,1,0:T(8,128)}, u32[]{:S(2)}, u32[]{:S(2)}) collective-permute-start(f32[16,64,128]{2,1,0:T(8,128)} %multiply_add_fusion), channel_id=1, source_target_pairs={{0,64},{2,66},{4,68},{6,70},{8,72},{10,74},{12,76},{14,78},{16,80}... | collective-permute-start | bytes 1572872 | tf_op jit(solution)/shard_map/ppermute | solution.py:21
  149.0 5.3 %collective-permute-start.5 = (f32[16]{0:T(128)S(1)}, f32[16]{0:T(128)S(1)}, u32[]{:S(2)}, u32[]{:S(2)}) collective-permute-start(f32[16]{0:T(128)S(1)} %fusion.72), channel_id=1, source_target_pairs={{0,32},{2,34},{4,36},{6,38},{8,40},{10,42},{12,44},{14,46},{16,48}... | collective-permute-start | bytes 200 | tf_op jit(solution)/shard_map/ppermute | solution.py:21
  208.8 4.5 %collective-permute-start.12 = (bf16[128,1024]{0,1:T(8,128)(2,1)S(1)}, bf16[128,1024]{0,1:T(8,128)(2,1)S(1)}, u32[]{:S(2)}, u32[]{:S(2)}) collective-permute-start(bf16[128,1024]{0,1:T(8,128)(2,1)S(1)} %bitcast.107), channel_id=1, source_target_pairs={{0,128},{1,129},{2,130},{3,131},{4,132},{5,133},{6,134},{7,135},{8... | collective-permute-start | bytes 786440 | tf_op jit(solution)/shard_map/ppermute | solution.py:285
  210.1 4.3 %collective-permute-start.13 = (bf16[128,1024]{0,1:T(8,128)(2,1)S(1)}, bf16[128,1024]{0,1:T(8,128)(2,1)S(1)}, u32[]{:S(2)}, u32[]{:S(2)}) collective-permute-start(bf16[128,1024]{0,1:T(8,128)(2,1)S(1)} %fusion.18), channel_id=1, source_target_pairs={{128,0},{129,1},{130,2},{131,3},{132,4},{133,5},{134,6},{135,7},{1... | collective-permute-start | bytes 786440 | tf_op jit(solution)/shard_map/ppermute | solution.py:284
Sparse Core Ops, SparseCore 0:
  10.9 176.5 all-gather.1

commit v8 on v6

--- a/solution.py
+++ b/solution.py
@@ -179,31 +179,41 @@
     def value_index(h, j, first_ref):
         return (kv_heads + h, jnp.minimum(j, (first_ref[0] + row_count - 1) // key_block), 0)
 
-    out = pl.pallas_call(
-        functools.partial(flash_kernel, row_count=row_count, key_block=key_block, scale=score_scale),
-        out_shape=jax.ShapeDtypeStruct((kv_heads, rows, head_width), jnp.bfloat16),
-        grid_spec=pltpu.PrefetchScalarGridSpec(
-            num_scalar_prefetch=1,
-            grid=(kv_heads, key_count // key_block),
-            in_specs=[
-                pl.BlockSpec((None, rows, head_width), lambda h, j, f: (h, 0, 0)),
-                pl.BlockSpec((None, key_block, head_width), key_index),
-                pl.BlockSpec((None, key_block, head_width), value_index),
-            ],
-            out_specs=pl.BlockSpec((None, rows, head_width), lambda h, j, f: (h, 0, 0)),
-            scratch_shapes=[
-                pltpu.VMEM((rows, 1), jnp.float32),
-                pltpu.VMEM((rows, 1), jnp.float32),
-                pltpu.VMEM((rows, head_width), jnp.float32),
-            ],
-        ),
-        compiler_params=pltpu.CompilerParams(dimension_semantics=("parallel", "arbitrary")),
-    )(jnp.reshape(first_row, (1,)).astype(jnp.int32), grouped, both_all, both_all)
-    return ready, (
-        out.reshape(kv_heads, group_size, row_count, head_width)
-        .transpose(2, 0, 1, 3)
-        .reshape(row_count, q_heads * head_width)
-    )
+    parts = []
+    for head in range(kv_heads):
+
+        def key_index(h, j, first_ref, head=head):
+            return (head, jnp.minimum(j, (first_ref[0] + row_count - 1) // key_block), 0)
+
+        def value_index(h, j, first_ref, head=head):
+            return (kv_heads + head, jnp.minimum(j, (first_ref[0] + row_count - 1) // key_block), 0)
+
+        out = pl.pallas_call(
+            functools.partial(flash_kernel, row_count=row_count, key_block=key_block, scale=score_scale),
+            out_shape=jax.ShapeDtypeStruct((1, rows, head_width), jnp.bfloat16),
+            grid_spec=pltpu.PrefetchScalarGridSpec(
+                num_scalar_prefetch=1,
+                grid=(1, key_count // key_block),
+                in_specs=[
+                    pl.BlockSpec((None, rows, head_width), lambda h, j, f, head=head: (head, 0, 0)),
+                    pl.BlockSpec((None, key_block, head_width), key_index),
+                    pl.BlockSpec((None, key_block, head_width), value_index),
+                ],
+                out_specs=pl.BlockSpec((None, rows, head_width), lambda h, j, f: (0, 0, 0)),
+                scratch_shapes=[
+                    pltpu.VMEM((rows, 1), jnp.float32),
+                    pltpu.VMEM((rows, 1), jnp.float32),
+                    pltpu.VMEM((rows, head_width), jnp.float32),
+                ],
+            ),
+            compiler_params=pltpu.CompilerParams(dimension_semantics=("parallel", "arbitrary")),
+        )(jnp.reshape(first_row, (1,)).astype(jnp.int32), grouped, both_all, both_all)
+        parts.append(
+            out.reshape(group_size, row_count, head_width)
+            .transpose(1, 0, 2)
+            .reshape(row_count, group_size * head_width)
+        )
+    return ready, parts
 
 
 def body(queries, keys, values, layer_in, w_bc, w_dt, dt_bias, decay_rate, skip_gain, out_gain):
@@ -280,7 +290,10 @@
     state_part, attended = attention_half(q_part, k_part, v_part, first_row, state_part)
     keep_state = seg == 0
     state_in_half = lax.ppermute(state_part, "segment", [(1, 0)])
-    attended_in_half = lax.ppermute(attended, "segment", [(0, 1)])
+    attended_in_half = jnp.concatenate(
+        [lax.ppermute(part, "segment", [(0, 1)]) for part in attended], axis=1
+    )
+    attended = jnp.concatenate(attended, axis=1)
     first = jnp.where(keep_state, state_part, attended_in_half)
     second = jnp.where(keep_state, state_in_half, attended)
     return jnp.concatenate([first, second], axis=1)[None]

time: 227 us -> 230 us (1.013)
  Pallas kernels: 20.2 us -> 22.5 us
    pallas_call x1 -> x2, Pallas kernels: 20.2 us -> 22.5 us  [attention_half(): pl.pallas_call(functools.partial(flash_kernel, row_count=row_count, key_b...]
  transfers between devices with their start and end apart: 15 -> 16, of which waited for: 14 -> 14; matrix products, arithmetic and copies ran while one was open for 10% -> 10% of each run, Pallas kernels for 0% -> 0%
where the time goes in v8:
time: 230 us; the launch traced here: 226 us
  waiting for transfers between devices  137 us (60%)
  starting transfers between devices  25.8 us (11%)
  Pallas kernels  22.5 us (10%)
  between operations  13.9 us (6%)
  matrix products  11.2 us (5%)
  other arithmetic  8.9 us (4%)
  local copies, waits for them, and re-layouts  6.97 us (3%)
    ppermute x11, waiting for transfers between devices, shifted_up(): return lax.ppermute(value, axis, pairs)  111 us
    pallas_call x2, Pallas kernels, attention_half(): pl.pallas_call(functools.partial(flash_kernel, row_count=row_count, key_b...  22.5 us
    all_gather x1, waiting for transfers between devices, attention_half(): both_all = lax.all_gather(both, 'ctx', axis=1, tiled=True)  21.7 us
    ppermute x11, starting transfers between devices, shifted_up(): return lax.ppermute(value, axis, pairs)  18.7 us
    add x5, other arithmetic, merge_states(): later[0][:, None, None] * earlier[1] + later[1]  6.77 us
  transfers between devices with their start and end apart: 16, of which 14 were waited for; matrix products, arithmetic and copies ran while one was open for 10% of the time, Pallas kernels for 0%

profile of v8, /device:TPU:231, one launch (start us, length us, event | category | flops | bytes accessed | tf_op | source)
XLA Modules:
  0.0 226.1 jit_solution(12629330415839499319)
XLA Ops:
  8.5 1.3 copy.46
  9.8 1.4 fusion.42
  11.2 4.1 %fusion = f32[128,1024]{0,1:T(8,128)S(1)} fusion(bf16[128,2048]{1,0:T(8,128)(2,1)} %param.13, bf16[1,2048,1024]{2,1,0:T(8,128)(2,1)} %param.14), kind=kOutput, calls=%fused_computation | convolution fusion | flops 536870912 | bytes 5242880 | tf_op jit(solution)/shard_map/dot_general | solution.py:243
  15.7 1.4 collective-permute-start
  17.2 3.2 %collective-permute-done = f32[128,273]{0,1:T(8,128)S(1)} collective-permute-done((f32[128,273]{0,1:T(8,128)S(1)}, f32[128,273]{0,1:T(8,128)S(1)}, u32[]{:S(2)}, u32[]{:S(2)}) %collective-permute-start) | collective-permute-done | bytes 139808 | tf_op jit(solution)/shard_map/ppermute | solution.py:25
  21.7 4.8 %collective-permute-start.6 = (f32[16,64,128]{2,1,0:T(8,128)S(1)}, f32[16,64,128]{2,1,0:T(8,128)}, u32[]{:S(2)}, u32[]{:S(2)}) collective-permute-start(f32[16,64,128]{2,1,0:T(8,128)S(1)} %fusion.58), channel_id=1, source_target_pairs={{0,2},{2,4},{4,6},{6,8},{8,10},{10,12},{12,14},{14,16},{16,18},{18... | collective-permute-start | bytes 1572872 | tf_op jit(solution)/shard_map/ppermute | solution.py:21
  26.5 13.7 %collective-permute-done.6 = f32[16,64,128]{2,1,0:T(8,128)} collective-permute-done((f32[16,64,128]{2,1,0:T(8,128)S(1)}, f32[16,64,128]{2,1,0:T(8,128)}, u32[]{:S(2)}, u32[]{:S(2)}) %collective-permute-start.6) | collective-permute-done | bytes 524320 | tf_op jit(solution)/shard_map/ppermute | solution.py:21
  41.4 1.3 collective-permute-start.7
  42.7 1.9 collective-permute-start.1
  44.6 9.9 %collective-permute-done.1 = f32[16]{0:T(128)S(1)} collective-permute-done((f32[16]{0:T(128)S(1)}, f32[16]{0:T(128)S(1)}, u32[]{:S(2)}, u32[]{:S(2)}) %collective-permute-start.1) | collective-permute-done | bytes 96 | tf_op jit(solution)/shard_map/ppermute | solution.py:21
  54.5 1.5 collective-permute-done.7
  57.9 1.3 collective-permute-start.8
  59.2 1.3 collective-permute-start.2
  60.5 3.1 %collective-permute-done.2 = f32[16]{0:T(128)S(1)} collective-permute-done((f32[16]{0:T(128)S(1)}, f32[16]{0:T(128)S(1)}, u32[]{:S(2)}, u32[]{:S(2)}) %collective-permute-start.2) | collective-permute-done | bytes 96 | tf_op jit(solution)/shard_map/ppermute | solution.py:21
  63.6 24.6 %collective-permute-done.8 = f32[16,64,128]{2,1,0:T(8,128)S(1)} collective-permute-done((f32[16,64,128]{2,1,0:T(8,128)S(1)}, f32[16,64,128]{2,1,0:T(8,128)S(1)}, u32[]{:S(2)}, u32[]{:S(2)}) %collective-permute-start.8) | collective-permute-done | bytes 524320 | tf_op jit(solution)/shard_map/ppermute | solution.py:21
  88.3 1.3 multiply_add_fusion.2
  89.6 1.3 collective-permute-start.9
  92.4 6.3 %collective-permute-done.3 = f32[16]{0:T(128)S(1)} collective-permute-done((f32[16]{0:T(128)S(1)}, f32[16]{0:T(128)S(1)}, u32[]{:S(2)}, u32[]{:S(2)}) %collective-permute-start.3) | collective-permute-done | bytes 96 | tf_op jit(solution)/shard_map/ppermute | solution.py:21
  98.8 7.8 %collective-permute-done.9 = f32[16,64,128]{2,1,0:T(8,128)} collective-permute-done((f32[16,64,128]{2,1,0:T(8,128)S(1)}, f32[16,64,128]{2,1,0:T(8,128)}, u32[]{:S(2)}, u32[]{:S(2)}) %collective-permute-start.9) | collective-permute-done | bytes 524320 | tf_op jit(solution)/shard_map/ppermute | solution.py:21
  107.8 1.4 collective-permute-start.10
  111.4 14.9 %collective-permute-done.4 = f32[16]{0:T(128)S(1)} collective-permute-done((f32[16]{0:T(128)S(1)}, f32[16]{0:T(128)S(1)}, u32[]{:S(2)}, u32[]{:S(2)}) %collective-permute-start.4) | collective-permute-done | bytes 96 | tf_op jit(solution)/shard_map/ppermute | solution.py:21
  126.3 16.8 %collective-permute-done.10 = f32[16,64,128]{2,1,0:T(8,128)} collective-permute-done((f32[16,64,128]{2,1,0:T(8,128)S(1)}, f32[16,64,128]{2,1,0:T(8,128)}, u32[]{:S(2)}, u32[]{:S(2)}) %collective-permute-start.10) | collective-permute-done | bytes 524320 | tf_op jit(solution)/shard_map/ppermute | solution.py:21
  143.0 1.9 multiply_add_fusion
  146.6 2.2 fusion.2
  148.9 1.5 collective-permute-start.5
  150.4 3.8 %collective-permute-done.5 = f32[16]{0:T(128)S(1)} collective-permute-done((f32[16]{0:T(128)S(1)}, f32[16]{0:T(128)S(1)}, u32[]{:S(2)}, u32[]{:S(2)}) %collective-permute-start.5) | collective-permute-done | bytes 96 | tf_op jit(solution)/shard_map/ppermute | solution.py:21
  154.2 8.5 %collective-permute-done.11 = f32[16,64,128]{2,1,0:T(8,128)} collective-permute-done((f32[16,64,128]{2,1,0:T(8,128)}, f32[16,64,128]{2,1,0:T(8,128)}, u32[]{:S(2)}, u32[]{:S(2)}) %collective-permute-start.11) | collective-permute-done | bytes 524320 | tf_op jit(solution)/shard_map/ppermute | solution.py:21
  162.8 2.6 %fusion.12 = (f32[128,16]{0,1:T(8,128)S(1)}, f32[16,64,128]{2,1,0:T(8,128)S(1)}) fusion(f32[16,64,128]{2,1,0:T(8,128)S(1)} %fusion.2, f32[16]{0:T(128)S(1)} %fusion.67, f32[128,16]{0,1:T(8,128)S(1)} %copy.54, f32[128,1024]{0,1:T(8,128)S(1)} %get-tuple-element.16, f32[128,273]{0,1:T(8,128)S(1)} %fusion.56, f32[128]{0:T(128)S(1)} %fusion.70, ...), kind=kOutput, calls=%fused_computation.16 | convolution fusion | flops 204355584 | bytes 4804102 | tf_op jit(solution)/shard_map/tgn,gkpn->tgkp/dot_general | solution.py:69
  165.7 21.7 %all-gather.2.cloned.1.call-done.k_ref.v_ref = bf16[4,8192,128]{2,1,0:T(8,128)(2,1)} async-done(((bf16[4,128,128]{2,1,0:T(8,128)(2,1)}), bf16[4,8192,128]{2,1,0:T(8,128)(2,1)}) %all-gather.2.cloned.1.call-update) | async-done | bytes 8388624 | tf_op jit(solution)/shard_map/all_gather | solution.py:170
  187.4 11.2 %shard_map.100 = bf16[1,512,128]{2,1,0:T(8,128)(2,1)} custom-call(s32[1]{0:T(128)} %bitcast.28.first_ref, bf16[2,512,128]{2,1,0:T(8,128)(2,1)} %bitcast.106, bf16[4,8192,128]{2,1,0:T(8,128)(2,1)} %all-gather.2.cloned.1.call-done.k_ref.v_ref, bf16[4,8192,128]{2,1,0:T(8,128)(2,1)} %all-gather.2.cloned.1.call-done.k_ref.v_ref), custom_call_target="tpu_custom_call" | custom-call | tf_op jit(solution)/shard_map/pallas_call | solution.py:191
  198.6 11.4 %shard_map.101 = bf16[1,512,128]{2,1,0:T(8,128)(2,1)} custom-call(s32[1]{0:T(128)} %bitcast.28.first_ref, bf16[2,512,128]{2,1,0:T(8,128)(2,1)} %bitcast.107, bf16[4,8192,128]{2,1,0:T(8,128)(2,1)} %all-gather.2.cloned.1.call-done.k_ref.v_ref, bf16[4,8192,128]{2,1,0:T(8,128)(2,1)} %all-gather.2.cloned.1.call-done.k_ref.v_ref), custom_call_target="tpu_custom_call" | custom-call | tf_op jit(solution)/shard_map/pallas_call | solution.py:191
  213.7 3.2 %collective-permute-start.14 = (bf16[128,1024]{0,1:T(8,128)(2,1)S(1)}, bf16[128,1024]{0,1:T(8,128)(2,1)S(1)}, u32[]{:S(2)}, u32[]{:S(2)}) collective-permute-start(bf16[128,1024]{0,1:T(8,128)(2,1)S(1)} %fusion.18), channel_id=1, source_target_pairs={{128,0},{129,1},{130,2},{131,3},{132,4},{133,5},{134,6},{135,7},{1... | collective-permute-start | bytes 786440 | tf_op jit(solution)/shard_map/ppermute | solution.py:292
  (79 shorter events, 19.6 us)
Async XLA Ops:
  6.5 102.8 %copy-start = (bf16[128,16,128]{2,1,0:T(8,128)(2,1)S(1)}, bf16[128,16,128]{2,1,0:T(8,128)(2,1)}, u32[]{:S(2)}) copy-start(bf16[128,16,128]{2,1,0:T(8,128)(2,1)} %param.10) | copy-start | bytes 1572868
  6.5 180.9 %all-gather.2.cloned.1.call-start = ((), (), s32[]{:S(2)}) async-start(), calls=%async_computation | async-start | bytes 8519680 | tf_op jit(solution)/shard_map/all_gather | solution.py:170
  11.2 6.0 %copy-start.7 = (f32[1,32]{1,0:T(1,128)S(1)}, f32[1,32]{1,0:T(1,128)}, u32[]{:S(2)}) copy-start(f32[1,32]{1,0:T(1,128)} %param.16) | copy-start | bytes 388
  11.2 6.0 %copy-start.8 = (f32[1,32]{1,0:T(1,128)S(1)}, f32[1,32]{1,0:T(1,128)}, u32[]{:S(2)}) copy-start(f32[1,32]{1,0:T(1,128)} %param.17) | copy-start | bytes 388
  15.7 4.7 %collective-permute-start = (f32[128,273]{0,1:T(8,128)S(1)}, f32[128,273]{0,1:T(8,128)S(1)}, u32[]{:S(2)}, u32[]{:S(2)}) collective-permute-start(f32[128,273]{0,1:T(8,128)S(1)} %pad_maximum_fusion), channel_id=1, source_target_pairs={{0,1},{1,0},{2,3},{3,2},{4,5},{5,4},{6,7},{7,6},{8,9},{9,8},{10,11... | collective-permute-start | bytes 419336 | tf_op jit(solution)/shard_map/ppermute | solution.py:25
  17.1 73.8 %copy-start.9 = (f32[1,32]{1,0:T(1,128)S(1)}, f32[1,32]{1,0:T(1,128)}, u32[]{:S(2)}) copy-start(f32[1,32]{1,0:T(1,128)} %param.18) | copy-start | bytes 388
  21.0 88.2 %copy-start.6 = (f32[1,32,64]{2,1,0:T(8,128)S(1)}, f32[1,32,64]{2,1,0:T(8,128)}, u32[]{:S(2)}) copy-start(f32[1,32,64]{2,1,0:T(8,128)} %param.19) | copy-start | bytes 24580
  21.7 18.5 %collective-permute-start.6 = (f32[16,64,128]{2,1,0:T(8,128)S(1)}, f32[16,64,128]{2,1,0:T(8,128)}, u32[]{:S(2)}, u32[]{:S(2)}) collective-permute-start(f32[16,64,128]{2,1,0:T(8,128)S(1)} %fusion.58), channel_id=1, source_target_pairs={{0,2},{2,4},{4,6},{6,8},{8,10},{10,12},{12,14},{14,16},{16,18},{18... | collective-permute-start | bytes 1572872 | tf_op jit(solution)/shard_map/ppermute | solution.py:21
  41.4 14.6 %collective-permute-start.7 = (f32[16,64,128]{2,1,0:T(8,128)S(1)}, f32[16,64,128]{2,1,0:T(8,128)S(1)}, u32[]{:S(2)}, u32[]{:S(2)}) collective-permute-start(f32[16,64,128]{2,1,0:T(8,128)S(1)} %multiply_add_fusion.4), channel_id=1, source_target_pairs={{0,4},{2,6},{4,8},{6,10},{8,12},{10,14},{12,16},{14,18},{16,20},{1... | collective-permute-start | bytes 1572872 | tf_op jit(solution)/shard_map/ppermute | solution.py:21
  42.7 11.8 %collective-permute-start.1 = (f32[16]{0:T(128)S(1)}, f32[16]{0:T(128)S(1)}, u32[]{:S(2)}, u32[]{:S(2)}) collective-permute-start(f32[16]{0:T(128)S(1)} %fusion.79), channel_id=1, source_target_pairs={{0,2},{2,4},{4,6},{6,8},{8,10},{10,12},{12,14},{14,16},{16,18},{18... | collective-permute-start | bytes 200 | tf_op jit(solution)/shard_map/ppermute | solution.py:21
  56.0 0.8 copy-start.2
  57.9 5.7 %copy-start.1 = (f32[16,64,128]{2,1,0:T(8,128)}, f32[16,64,128]{2,1,0:T(8,128)S(1)}, u32[]{:S(2)}) copy-start(f32[16,64,128]{2,1,0:T(8,128)S(1)} %multiply_add_fusion.3) | copy-start | bytes 1572868
  57.9 30.3 %collective-permute-start.8 = (f32[16,64,128]{2,1,0:T(8,128)S(1)}, f32[16,64,128]{2,1,0:T(8,128)S(1)}, u32[]{:S(2)}, u32[]{:S(2)}) collective-permute-start(f32[16,64,128]{2,1,0:T(8,128)S(1)} %multiply_add_fusion.3), channel_id=1, source_target_pairs={{0,8},{2,10},{4,12},{6,14},{8,16},{10,18},{12,20},{14,22},{16,24},... | collective-permute-start | bytes 1572872 | tf_op jit(solution)/shard_map/ppermute | solution.py:21
  59.2 4.4 %collective-permute-start.2 = (f32[16]{0:T(128)S(1)}, f32[16]{0:T(128)S(1)}, u32[]{:S(2)}, u32[]{:S(2)}) collective-permute-start(f32[16]{0:T(128)S(1)} %get-tuple-element.13), channel_id=1, source_target_pairs={{0,4},{2,6},{4,8},{6,10},{8,12},{10,14},{12,16},{14,18},{16,20},{1... | collective-permute-start | bytes 200 | tf_op jit(solution)/shard_map/ppermute | solution.py:21
  88.3 10.5 %copy-start.3 = (f32[16,64,128]{2,1,0:T(8,128)}, f32[16,64,128]{2,1,0:T(8,128)S(1)}, u32[]{:S(2)}) copy-start(f32[16,64,128]{2,1,0:T(8,128)S(1)} %collective-permute-done.8) | copy-start | bytes 1572868
  89.6 17.0 %collective-permute-start.9 = (f32[16,64,128]{2,1,0:T(8,128)S(1)}, f32[16,64,128]{2,1,0:T(8,128)}, u32[]{:S(2)}, u32[]{:S(2)}) collective-permute-start(f32[16,64,128]{2,1,0:T(8,128)S(1)} %multiply_add_fusion.2), channel_id=1, source_target_pairs={{0,16},{2,18},{4,20},{6,22},{8,24},{10,26},{12,28},{14,30},{16,32}... | collective-permute-start | bytes 1572872 | tf_op jit(solution)/shard_map/ppermute | solution.py:21
  91.0 7.8 %collective-permute-start.3 = (f32[16]{0:T(128)S(1)}, f32[16]{0:T(128)S(1)}, u32[]{:S(2)}, u32[]{:S(2)}) collective-permute-start(f32[16]{0:T(128)S(1)} %fusion.76), channel_id=1, source_target_pairs={{0,8},{2,10},{4,12},{6,14},{8,16},{10,18},{12,20},{14,22},{16,24},... | collective-permute-start | bytes 200 | tf_op jit(solution)/shard_map/ppermute | solution.py:21
  107.7 55.0 %copy-start.4 = (f32[16,64,128]{2,1,0:T(8,128)S(1)}, f32[16,64,128]{2,1,0:T(8,128)}, u32[]{:S(2)}) copy-start(f32[16,64,128]{2,1,0:T(8,128)} %copy-done.3) | copy-start | bytes 1572868
  107.8 35.3 %collective-permute-start.10 = (f32[16,64,128]{2,1,0:T(8,128)S(1)}, f32[16,64,128]{2,1,0:T(8,128)}, u32[]{:S(2)}, u32[]{:S(2)}) collective-permute-start(f32[16,64,128]{2,1,0:T(8,128)S(1)} %multiply_add_fusion.1), channel_id=1, source_target_pairs={{0,32},{2,34},{4,36},{6,38},{8,40},{10,42},{12,44},{14,46},{16,48}... | collective-permute-start | bytes 1572872 | tf_op jit(solution)/shard_map/ppermute | solution.py:21
  109.3 16.9 %collective-permute-start.4 = (f32[16]{0:T(128)S(1)}, f32[16]{0:T(128)S(1)}, u32[]{:S(2)}, u32[]{:S(2)}) collective-permute-start(f32[16]{0:T(128)S(1)} %fusion.74), channel_id=1, source_target_pairs={{0,16},{2,18},{4,20},{6,22},{8,24},{10,26},{12,28},{14,30},{16,32}... | collective-permute-start | bytes 200 | tf_op jit(solution)/shard_map/ppermute | solution.py:21
  145.0 17.8 %collective-permute-start.11 = (f32[16,64,128]{2,1,0:T(8,128)}, f32[16,64,128]{2,1,0:T(8,128)}, u32[]{:S(2)}, u32[]{:S(2)}) collective-permute-start(f32[16,64,128]{2,1,0:T(8,128)} %multiply_add_fusion), channel_id=1, source_target_pairs={{0,64},{2,66},{4,68},{6,70},{8,72},{10,74},{12,76},{14,78},{16,80}... | collective-permute-start | bytes 1572872 | tf_op jit(solution)/shard_map/ppermute | solution.py:21
  148.9 5.3 %collective-permute-start.5 = (f32[16]{0:T(128)S(1)}, f32[16]{0:T(128)S(1)}, u32[]{:S(2)}, u32[]{:S(2)}) collective-permute-start(f32[16]{0:T(128)S(1)} %fusion.72), channel_id=1, source_target_pairs={{0,32},{2,34},{4,36},{6,38},{8,40},{10,42},{12,44},{14,46},{16,48}... | collective-permute-start | bytes 200 | tf_op jit(solution)/shard_map/ppermute | solution.py:21
  198.6 11.4 %copy-start.5 = (bf16[1,512,128]{2,1,0:T(8,128)(2,1)S(1)}, bf16[1,512,128]{2,1,0:T(8,128)(2,1)}, u32[]{:S(2)}) copy-start(bf16[1,512,128]{2,1,0:T(8,128)(2,1)} %shard_map.100) | copy-start | bytes 393220
  210.1 6.8 %collective-permute-start.12 = (bf16[128,512]{0,1:T(8,128)(2,1)S(1)}, bf16[128,512]{0,1:T(8,128)(2,1)S(1)}, u32[]{:S(2)}, u32[]{:S(2)}) collective-permute-start(bf16[128,512]{0,1:T(8,128)(2,1)S(1)} %bitcast.112), channel_id=1, source_target_pairs={{0,128},{1,129},{2,130},{3,131},{4,132},{5,133},{6,134},{7,135},{8... | collective-permute-start | bytes 393224 | tf_op jit(solution)/shard_map/ppermute | solution.py:294
  212.4 4.5 %collective-permute-start.13 = (bf16[128,512]{0,1:T(8,128)(2,1)S(1)}, bf16[128,512]{0,1:T(8,128)(2,1)S(1)}, u32[]{:S(2)}, u32[]{:S(2)}) collective-permute-start(bf16[128,512]{0,1:T(8,128)(2,1)S(1)} %bitcast.114), channel_id=1, source_target_pairs={{0,128},{1,129},{2,130},{3,131},{4,132},{5,133},{6,134},{7,135},{8... | collective-permute-start | bytes 393224 | tf_op jit(solution)/shard_map/ppermute | solution.py:294
  213.7 4.3 %collective-permute-start.14 = (bf16[128,1024]{0,1:T(8,128)(2,1)S(1)}, bf16[128,1024]{0,1:T(8,128)(2,1)S(1)}, u32[]{:S(2)}, u32[]{:S(2)}) collective-permute-start(bf16[128,1024]{0,1:T(8,128)(2,1)S(1)} %fusion.18), channel_id=1, source_target_pairs={{128,0},{129,1},{130,2},{131,3},{132,4},{133,5},{134,6},{135,7},{1... | collective-permute-start | bytes 786440 | tf_op jit(solution)/shard_map/ppermute | solution.py:292
Sparse Core Ops, SparseCore 0:
  10.9 176.5 all-gather.1
